TPU v7x, 128 devices: a whole 4x4x4 slice. The times are simulated.
128 devices in a mesh: section: 8 (over x, core), wafer: 4 (over y), sub: 4 (over z).
Axes of the slice: x: 4, y: 4, z: 4, core: 2. Of those that a mesh axis runs over, the one named last changes fastest.
Arguments:
- tod: float32 [1, 256, 8192], P(None, 'wafer', ('section', 'sub')), may hold values from -6 to 6
- templates: float32 [1, 256, 8192], P(None, 'wafer', ('section', 'sub'))
- det_weight: float32 [256], P('wafer'), may hold values from 0.3 to 3
- pixel: int32 [1, 256, 8192], P(None, 'wafer', ('section', 'sub')), may hold values from 0 to 511
- hitlist: int32 [1, 64, 512], P(None, 'wafer', ('section', 'sub')), may hold values from 0 to 127, as said below
- counts: int32 [1, 64, 32], P(None, 'wafer', ('section', 'sub')), may hold values from 2 to 16
Outputs:
- sky_map: float32 [8192], P(('wafer', 'sub'))
Inputs may be any that keep to these rules, and one draw needn't show every extreme that they name: `hitlist`: for each micro-batch, source device and tile, the live slots name distinct blocks of that source, and no block is named by live slots of two tiles; in each micro-batch exactly one tile has a full hit list (all 16 slots live) from every source device.
All inputs are finite; a program needn't handle non-finite values.
Results may differ from a plain program's by a relative error of at most 0.0003.
Values sent between devices are 32-bit elements; how exact they have to be, the bound alone decides.
No kernel may reach another device: no remote copies, remote signals or barrier semaphores. Data moves between devices by JAX's collectives and lax.ppermute only.
A program may use at most 64 MiB of HBM per device.

v0:
```python
import jax
import jax.numpy as jnp
from jax import lax
from jax.sharding import PartitionSpec as P

BL = 128
TILE = 512


def bin_block(values, pixels, weights, tile_size):
    upper_count = tile_size // 128
    row_count = values.shape[0]
    upper_part = pixels // 128
    lower_part = pixels % 128
    upper_hot = (
        lax.broadcasted_iota(jnp.int32, (upper_count, row_count), 0) == upper_part[None, :]
    ).astype(jnp.float32)
    lower_hot = (
        lax.broadcasted_iota(jnp.int32, (row_count, 128), 1) == lower_part[:, None]
    ).astype(jnp.float32)
    stacked = jnp.concatenate([upper_hot * values[None, :], upper_hot * weights[None, :]], axis=0)
    binned = jnp.dot(
        stacked, lower_hot, precision=lax.Precision.HIGHEST, preferred_element_type=jnp.float32
    )
    return (binned[:upper_count].reshape(-1), binned[upper_count:].reshape(-1))


def shards(tod, templates, det_weight, pixel, hitlist, counts):
    samp_local = tod.shape[2]
    owners = hitlist.shape[1]
    slots = hitlist.shape[2]
    per_det = samp_local // BL
    tile_size = TILE
    slot_ids = lax.broadcasted_iota(jnp.int32, (owners, slots), 1)
    block_weight = jnp.repeat(det_weight, per_det)
    num_tile = jnp.zeros((tile_size,), jnp.float32)
    wgt_tile = jnp.zeros((tile_size,), jnp.float32)

    def add_source(carry, inputs_now):
        num_part, wgt_part = bin_block(inputs_now[0], inputs_now[1], inputs_now[2], tile_size)
        return ((carry[0] + num_part, carry[1] + wgt_part), None)

    template_rows = templates[0]
    streams = tod[0]
    gram_sum = lax.dot_general(
        template_rows,
        template_rows,
        (((1,), (1,)), ((), ())),
        precision=lax.Precision.HIGHEST,
        preferred_element_type=jnp.float32,
    )
    projection = lax.dot_general(
        template_rows,
        streams,
        (((1,), (1,)), ((), ())),
        precision=lax.Precision.HIGHEST,
        preferred_element_type=jnp.float32,
    )
    gram_sum, projection = lax.psum((gram_sum, projection), ("section", "sub"))
    factor = jnp.linalg.cholesky(gram_sum)
    coef_fit = jax.scipy.linalg.cho_solve((factor, True), projection)
    removed = lax.dot_general(
        coef_fit,
        template_rows,
        (((0,), (0,)), ((), ())),
        precision=lax.Precision.HIGHEST,
        preferred_element_type=jnp.float32,
    )
    filtered = streams - removed
    weighted = (filtered * det_weight[:, None]).reshape(-1, BL)
    pixel_blocks = pixel[0].reshape(-1, BL)
    hit_rows = hitlist[0]
    live_slots = slot_ids < counts[0]
    send_values = jnp.where(live_slots[:, :, None], weighted[hit_rows], 0.0)
    send_pixels = jnp.where(live_slots[:, :, None], pixel_blocks[hit_rows], 0)
    send_weights = jnp.where(live_slots, block_weight[hit_rows], 0.0)
    got_values = lax.all_to_all(
        send_values, ("wafer", "sub"), split_axis=0, concat_axis=0, tiled=True
    )
    got_pixels = lax.all_to_all(
        send_pixels, ("wafer", "sub"), split_axis=0, concat_axis=0, tiled=True
    )
    got_weights = lax.all_to_all(
        send_weights, ("wafer", "sub"), split_axis=0, concat_axis=0, tiled=True
    )
    full_weights = jnp.broadcast_to(got_weights[..., None], got_values.shape)
    row_len = slots * BL
    (num_tile, wgt_tile), unused = lax.scan(
        add_source,
        (num_tile, wgt_tile),
        (
            got_values.reshape(-1, row_len),
            got_pixels.reshape(-1, row_len),
            full_weights.reshape(-1, row_len),
        ),
    )
    num_tile, wgt_tile = lax.psum((num_tile, wgt_tile), "section")
    return num_tile / jnp.maximum(wgt_tile, 1.0)


def solution(mesh):
    placed = (
        P(None, "wafer", ("section", "sub")),
        P(None, "wafer", ("section", "sub")),
        P("wafer"),
        P(None, "wafer", ("section", "sub")),
        P(None, "wafer", ("section", "sub")),
        P(None, "wafer", ("section", "sub")),
    )
    return jax.shard_map(
        shards, mesh=mesh, in_specs=placed, out_specs=P(("wafer", "sub")), check_vma=False
    )
```

profile of v0, /device:TPU:0, one launch (start us, length us, event | category | flops | bytes accessed | tf_op | source)
XLA Modules:
  0.0 205.6 jit_solution(17069625567429026814)
XLA Ops:
  0.0 0.7 compare_select_fusion.4
  0.8 0.6 copy-done.3
  1.7 1.9 gather_fusion.2
  3.7 0.6 copy-done.4
  4.3 0.7 compare_select_fusion.3
  5.0 8.2 %all-to-all-start.2 = ((f32[16,1,16]{2,1,0:T(1,128)}), f32[16,1,16]{2,1,0:T(1,128)S(1)}, u32[]{:S(2)}, u32[]{:S(2)}) async-start(f32[16,1,16]{2,1,0:T(1,128)} %compare_select_fusion.3), calls=%async_computation.2 | async-start | bytes 16384 | tf_op jit(solution)/shard_map/all_to_all | solution.py:83
  13.7 128.0 %all-reduce = (f32[64,64]{1,0:T(8,128)S(1)}, f32[64,64]{0,1:T(8,128)S(1)}) all-reduce(f32[64,64]{1,0:T(8,128)S(1)} %fusion.11, f32[64,64]{0,1:T(8,128)S(1)} %fusion.13), channel_id=1, replica_groups=mesh['section'=8,'wafer'=4,'sub'=4] {'section','sub'}, use_global_device_ids=true, to_apply=%region_3.4 | all-reduce | flops 8192 | bytes 65536 | tf_op jit(solution)/shard_map/psum | solution.py:59
  141.8 5.8 %cholesky.16 = f32[64,64]{1,0:T(8,128)S(1)} custom-call(f32[64,64]{1,0:T(8,128)S(1)} %fusion.21), custom_call_target="Cholesky" | custom-call | tf_op jit(solution)/shard_map/jit(cholesky)/cholesky | solution.py:60
  147.7 0.6 compare_reduce_fusion
  148.3 0.7 fusion.16
  149.0 4.9 %custom-call.10 = f32[1,64,64]{1,2,0:T(8,128)S(1)} custom-call(f32[1,64,64]{2,1,0:T(8,128)S(1)} %fusion.16), custom_call_target="InvertDiagBlocksLowerTriangular" | custom-call | tf_op jit(solution)/shard_map/jit(_cho_solve)/triangular_solve | solution.py:61
  154.6 0.7 gather_fusion.1
  155.3 0.8 broadcast_select_fusion
  156.2 0.7 gather_fusion
  156.9 4.3 %all-to-all-start.1 = ((f32[16,16,128]{2,1,0:T(8,128)}), f32[16,16,128]{2,1,0:T(8,128)S(1)}, u32[]{:S(2)}, u32[]{:S(2)}) async-start(f32[16,16,128]{2,1,0:T(8,128)} %broadcast_select_fusion), calls=%async_computation.1 | async-start | bytes 262144 | tf_op jit(solution)/shard_map/all_to_all | solution.py:77
  161.3 0.8 broadcast_select_fusion.1
  162.0 7.1 %all-to-all-done.1 = f32[16,16,128]{2,1,0:T(8,128)S(1)} async-done(((f32[16,16,128]{2,1,0:T(8,128)}), f32[16,16,128]{2,1,0:T(8,128)S(1)}, u32[]{:S(2)}, u32[]{:S(2)}) %all-to-all-start.1) | async-done | bytes 131104 | tf_op jit(solution)/shard_map/all_to_all | solution.py:77
  169.1 3.6 %all-to-all-start = ((s32[16,16,128]{2,1,0:T(8,128)}), s32[16,16,128]{2,1,0:T(8,128)S(1)}, u32[]{:S(2)}, u32[]{:S(2)}) async-start(s32[16,16,128]{2,1,0:T(8,128)} %broadcast_select_fusion.1), calls=%async_computation | async-start | bytes 262144 | tf_op jit(solution)/shard_map/all_to_all | solution.py:80
  172.9 7.6 %all-to-all-done = s32[16,16,128]{2,1,0:T(8,128)S(1)} async-done(((s32[16,16,128]{2,1,0:T(8,128)}), s32[16,16,128]{2,1,0:T(8,128)S(1)}, u32[]{:S(2)}, u32[]{:S(2)}) %all-to-all-start) | async-done | bytes 131104 | tf_op jit(solution)/shard_map/all_to_all | solution.py:80
  180.6 12.0 %while.15 = (s32[]{:T(128)}, f32[512]{0:T(512)S(1)}, f32[512]{0:T(512)S(1)}, s32[16,2048]{1,0:T(8,128)S(1)}, f32[16,2048]{1,0:T(8,128)S(1)}, /*index=5*/f32[16,2048]{1,0:T(8,128)S(1)}, s32[]{:T(128)}, s32[]{:T(128)}) while((s32[]{:T(128)}, f32[512]{0:T(512)S(1)}, f32[512]{0:T(512)S(1)}, s32[16,2048]{1,0:T(8,128)S(1)}, ...), condition=%wide.region_5.6_spmd.clone, body=%wide.region_4.5_spmd.clone.sunk | while | flops 25524224 | bytes 254055 | solution.py:88
  185.2 0.6 fusion.30
  186.0 0.6 fusion.30
  186.7 0.6 fusion.30
  187.5 0.6 fusion.30
  188.2 0.6 fusion.30
  189.0 0.6 fusion.30
  189.8 0.6 fusion.30
  190.5 0.6 fusion.30
  191.3 0.6 fusion.30
  192.0 0.6 fusion.30
  192.6 12.4 %all-reduce.1 = (f32[512]{0:T(512)S(1)}, f32[512]{0:T(512)S(1)}) all-reduce(f32[512]{0:T(512)S(1)} %get-tuple-element.86, f32[512]{0:T(512)S(1)} %get-tuple-element.87), channel_id=1, replica_groups=mesh['section'=8,'wafer'=4,'sub'=4] {'section'}, use_global_device_ids=true, to_apply=%region_6.7 | all-reduce | flops 1024 | bytes 8192 | tf_op jit(solution)/shard_map/psum | solution.py:97
  205.0 0.6 maximum_divide_fusion
  (117 shorter events, 7.4 us)
Async XLA Ops:
  0.0 13.2 %copy-start = (f32[1,64,256]{2,1,0:T(8,128)S(1)}, f32[1,64,256]{2,1,0:T(8,128)}, u32[]{:S(2)}) copy-start(f32[1,64,256]{2,1,0:T(8,128)} %param.9) | copy-start | bytes 196612
  0.8 0.7 copy-start.3
  3.7 0.7 copy-start.4
  4.3 9.1 %copy-start.1 = (f32[1,64,256]{2,1,0:T(8,128)S(1)}, f32[1,64,256]{2,1,0:T(8,128)}, u32[]{:S(2)}) copy-start(f32[1,64,256]{2,1,0:T(8,128)} %param.8) | copy-start | bytes 196612
  5.0 151.9 %all-to-all-start.2 = ((f32[16,1,16]{2,1,0:T(1,128)}), f32[16,1,16]{2,1,0:T(1,128)S(1)}, u32[]{:S(2)}, u32[]{:S(2)}) async-start(f32[16,1,16]{2,1,0:T(1,128)} %compare_select_fusion.3), calls=%async_computation.2 | async-start | bytes 16384 | tf_op jit(solution)/shard_map/all_to_all | solution.py:83
  155.3 0.8 copy-start.2
  156.9 12.2 %all-to-all-start.1 = ((f32[16,16,128]{2,1,0:T(8,128)}), f32[16,16,128]{2,1,0:T(8,128)S(1)}, u32[]{:S(2)}, u32[]{:S(2)}) async-start(f32[16,16,128]{2,1,0:T(8,128)} %broadcast_select_fusion), calls=%async_computation.1 | async-start | bytes 262144 | tf_op jit(solution)/shard_map/all_to_all | solution.py:77
  169.1 11.4 %all-to-all-start = ((s32[16,16,128]{2,1,0:T(8,128)}), s32[16,16,128]{2,1,0:T(8,128)S(1)}, u32[]{:S(2)}, u32[]{:S(2)}) async-start(s32[16,16,128]{2,1,0:T(8,128)} %broadcast_select_fusion.1), calls=%async_computation | async-start | bytes 262144 | tf_op jit(solution)/shard_map/all_to_all | solution.py:80
where the time goes:
time: 207 us; the launch traced here: 206 us
  blocking collectives  140 us (68%)
  other arithmetic  17.3 us (8%)
  starting transfers between devices  16.1 us (8%)
  waiting for transfers between devices  14.7 us (7%)
  matrix products  10.3 us (5%)
  local copies, waits for them, and re-layouts  5.72 us (3%)
    psum x1, blocking collectives, shards(): gram_sum, projection = lax.psum((gram_sum, projection), ('section', 'sub'))  128 us
    psum x1, blocking collectives, shards(): num_tile, wgt_tile = lax.psum((num_tile, wgt_tile), 'section')  12.4 us
    dot_general x16, matrix products, bin_block(): jnp.dot(stacked, lower_hot, precision=lax.Precision.HIGHEST, preferred_el...  9.19 us
    all_to_all x1, starting transfers between devices, shards(): lax.all_to_all(send_weights, ('wafer', 'sub'), split_axis=0, concat_axis=...  8.16 us
    all_to_all x1, waiting for transfers between devices, shards(): lax.all_to_all(send_pixels, ('wafer', 'sub'), split_axis=0, concat_axis=0...  7.62 us
    all_to_all x1, waiting for transfers between devices, shards(): lax.all_to_all(send_values, ('wafer', 'sub'), split_axis=0, concat_axis=0...  7.09 us
    another operation x3, other arithmetic, shards(): factor = jnp.linalg.cholesky(gram_sum)  6.52 us
    another operation x2, other arithmetic, shards(): coef_fit = jax.scipy.linalg.cho_solve((factor, True), projection)  5.55 us
  transfers between devices with their start and end apart: 3, of which 2 were waited for; matrix products, arithmetic and copies ran while one was open for 8% of the time, Pallas kernels for 0%

commit v1 on v0

--- a/solution.py
+++ b/solution.py
@@ -23,6 +23,16 @@
         stacked, lower_hot, precision=lax.Precision.HIGHEST, preferred_element_type=jnp.float32
     )
     return (binned[:upper_count].reshape(-1), binned[upper_count:].reshape(-1))
+
+
+def all_sum(x, axes):
+    for axis in axes:
+        size = lax.axis_size(axis)
+        bit = 1
+        while bit < size:
+            x = x + lax.ppermute(x, axis, [(i, i ^ bit) for i in range(size)])
+            bit *= 2
+    return x
 
 
 def shards(tod, templates, det_weight, pixel, hitlist, counts):
@@ -56,7 +66,8 @@
         precision=lax.Precision.HIGHEST,
         preferred_element_type=jnp.float32,
     )
-    gram_sum, projection = lax.psum((gram_sum, projection), ("section", "sub"))
+    joined = all_sum(jnp.concatenate([gram_sum, projection], axis=1), ("section", "sub"))
+    gram_sum, projection = joined[:, : gram_sum.shape[1]], joined[:, gram_sum.shape[1] :]
     factor = jnp.linalg.cholesky(gram_sum)
     coef_fit = jax.scipy.linalg.cho_solve((factor, True), projection)
     removed = lax.dot_general(
@@ -94,7 +105,8 @@
             full_weights.reshape(-1, row_len),
         ),
     )
-    num_tile, wgt_tile = lax.psum((num_tile, wgt_tile), "section")
+    both = all_sum(jnp.stack([num_tile, wgt_tile]), ("section",))
+    num_tile, wgt_tile = both[0], both[1]
     return num_tile / jnp.maximum(wgt_tile, 1.0)
 
 

time: 207 us -> 92.9 us (0.45)
  blocking collectives: 140 us -> 0 us
  starting transfers between devices: 16.1 us -> 31.1 us
  waiting for transfers between devices: 14.7 us -> 27.5 us
    psum x2 -> x0, blocking collectives: 140 us -> none  [the longest x1 128 us: shards(): gram_sum, projection = lax.psum((gram_sum, projection), ('section', 'sub'))]
    ppermute x0 -> x8, waiting for transfers between devices: none -> 12.8 us  [all_sum(): x = x + lax.ppermute(x, axis, [(i, i ^ bit) for i in range(size)])]
    ppermute x0 -> x8, starting transfers between devices: none -> 12 us  [all_sum(): x = x + lax.ppermute(x, axis, [(i, i ^ bit) for i in range(size)])]
    all_to_all x1, starting transfers between devices: 3.6 us -> 7.51 us  [shards(): lax.all_to_all(send_pixels, ('wafer', 'sub'), split_axis=0, concat_axis=0...]
  transfers between devices with their start and end apart: 3 -> 11, of which waited for: 2 -> 9; matrix products, arithmetic and copies ran while one was open for 8% -> 21% of each run, Pallas kernels for 0% -> 0%
where the time goes in v1:
time: 92.9 us; the launch traced here: 92.5 us
  starting transfers between devices  31.1 us (33%)
  waiting for transfers between devices  27.5 us (30%)
  other arithmetic  16.7 us (18%)
  matrix products  10.3 us (11%)
  local copies, waits for them, and re-layouts  5.78 us (6%)
    ppermute x8, waiting for transfers between devices, all_sum(): x = x + lax.ppermute(x, axis, [(i, i ^ bit) for i in range(size)])  12.8 us
    ppermute x8, starting transfers between devices, all_sum(): x = x + lax.ppermute(x, axis, [(i, i ^ bit) for i in range(size)])  12 us
    dot_general x16, matrix products, bin_block(): jnp.dot(stacked, lower_hot, precision=lax.Precision.HIGHEST, preferred_el...  9.19 us
    all_to_all x1, starting transfers between devices, shards(): lax.all_to_all(send_weights, ('wafer', 'sub'), split_axis=0, concat_axis=...  8.05 us
    all_to_all x1, waiting for transfers between devices, shards(): lax.all_to_all(send_values, ('wafer', 'sub'), split_axis=0, concat_axis=0...  7.62 us
    all_to_all x1, starting transfers between devices, shards(): lax.all_to_all(send_pixels, ('wafer', 'sub'), split_axis=0, concat_axis=0...  7.51 us
    all_to_all x1, waiting for transfers between devices, shards(): lax.all_to_all(send_pixels, ('wafer', 'sub'), split_axis=0, concat_axis=0...  7.09 us
    another operation x3, other arithmetic, shards(): factor = jnp.linalg.cholesky(gram_sum)  6.52 us
  transfers between devices with their start and end apart: 11, of which 9 were waited for; matrix products, arithmetic and copies ran while one was open for 21% of the time, Pallas kernels for 0%

profile of v1, /device:TPU:0, one launch (start us, length us, event | category | flops | bytes accessed | tf_op | source)
XLA Modules:
  0.0 92.5 jit_solution(3322374426382595508)
XLA Ops:
  0.0 0.8 copy-done
  1.4 0.6 copy-done.3
  2.1 0.6 collective-permute-done
  2.7 1.7 %collective-permute-start.1 = (f32[64,128]{0,1:T(8,128)S(1)}, f32[64,128]{0,1:T(8,128)S(1)}, u32[]{:S(2)}, u32[]{:S(2)}) collective-permute-start(f32[64,128]{0,1:T(8,128)S(1)} %fusion.25), channel_id=1, source_target_pairs={{0,32},{16,48},{32,0},{48,16},{64,96},{80,112},{96,64},{112,80},{1... | collective-permute-start | bytes 98312 | tf_op jit(solution)/shard_map/ppermute | solution.py:33
  4.6 1.9 %gather_fusion.2 = f32[256]{0:T(256)S(1)} fusion(f32[128]{0:T(128)S(1)} %reshape.156, s32[1024]{0:T(1024)S(1)} %pad_clamp_fusion), kind=kCustom, calls=%fused_computation.2 | custom fusion | bytes 3072 | tf_op jit(solution)/shard_map/gather | solution.py:87
  7.0 3.2 %collective-permute-start.2 = (f32[64,128]{0,1:T(8,128)S(1)}, f32[64,128]{0,1:T(8,128)S(1)}, u32[]{:S(2)}, u32[]{:S(2)}) collective-permute-start(f32[64,128]{0,1:T(8,128)S(1)} %add.89), channel_id=1, source_target_pairs={{0,64},{16,80},{32,96},{48,112},{64,0},{80,16},{96,32},{112,48},{1... | collective-permute-start | bytes 98312 | tf_op jit(solution)/shard_map/ppermute | solution.py:33
  10.2 0.7 compare_select_fusion.3
  10.9 8.0 %all-to-all-start.2 = ((f32[16,1,16]{2,1,0:T(1,128)}), f32[16,1,16]{2,1,0:T(1,128)S(1)}, u32[]{:S(2)}, u32[]{:S(2)}) async-start(f32[16,1,16]{2,1,0:T(1,128)} %compare_select_fusion.3), calls=%async_computation.2 | async-start | bytes 16384 | tf_op jit(solution)/shard_map/all_to_all | solution.py:94
  19.0 2.0 %collective-permute-start.3 = (f32[64,128]{0,1:T(8,128)S(1)}, f32[64,128]{0,1:T(8,128)S(1)}, u32[]{:S(2)}, u32[]{:S(2)}) collective-permute-start(f32[64,128]{0,1:T(8,128)S(1)} %add.90), channel_id=1, source_target_pairs={{0,1},{1,0},{2,3},{3,2},{4,5},{5,4},{6,7},{7,6},{8,9},{9,8},{10,11... | collective-permute-start | bytes 98312 | tf_op jit(solution)/shard_map/ppermute | solution.py:33
  21.1 0.7 gather_fusion
  21.8 1.5 %collective-permute-done.3 = f32[64,128]{0,1:T(8,128)S(1)} collective-permute-done((f32[64,128]{0,1:T(8,128)S(1)}, f32[64,128]{0,1:T(8,128)S(1)}, u32[]{:S(2)}, u32[]{:S(2)}) %collective-permute-start.3) | collective-permute-done | bytes 32800 | tf_op jit(solution)/shard_map/ppermute | solution.py:33
  23.4 3.5 %collective-permute-start.4 = (f32[64,128]{0,1:T(8,128)S(1)}, f32[64,128]{0,1:T(8,128)S(1)}, u32[]{:S(2)}, u32[]{:S(2)}) collective-permute-start(f32[64,128]{0,1:T(8,128)S(1)} %add.91), channel_id=1, source_target_pairs={{0,2},{1,3},{2,0},{3,1},{4,6},{5,7},{6,4},{7,5},{8,10},{9,11},{10,... | collective-permute-start | bytes 98312 | tf_op jit(solution)/shard_map/ppermute | solution.py:33
  26.9 0.8 broadcast_select_fusion.1
  27.7 1.6 %collective-permute-done.4 = f32[64,128]{0,1:T(8,128)S(1)} collective-permute-done((f32[64,128]{0,1:T(8,128)S(1)}, f32[64,128]{0,1:T(8,128)S(1)}, u32[]{:S(2)}, u32[]{:S(2)}) %collective-permute-start.4) | collective-permute-done | bytes 32800 | tf_op jit(solution)/shard_map/ppermute | solution.py:33
  29.3 5.8 %cholesky.16 = f32[64,64]{1,0:T(8,128)S(1)} custom-call(f32[64,64]{1,0:T(8,128)S(1)} %fusion.22), custom_call_target="Cholesky" | custom-call | tf_op jit(solution)/shard_map/jit(cholesky)/cholesky | solution.py:71
  35.2 0.6 compare_reduce_fusion
  35.9 0.7 fusion.16
  36.5 4.9 %custom-call.10 = f32[1,64,64]{1,2,0:T(8,128)S(1)} custom-call(f32[1,64,64]{2,1,0:T(8,128)S(1)} %fusion.16), custom_call_target="InvertDiagBlocksLowerTriangular" | custom-call | tf_op jit(solution)/shard_map/jit(_cho_solve)/triangular_solve | solution.py:72
  42.1 0.7 gather_fusion.1
  42.9 7.5 %all-to-all-start = ((s32[16,16,128]{2,1,0:T(8,128)}), s32[16,16,128]{2,1,0:T(8,128)S(1)}, u32[]{:S(2)}, u32[]{:S(2)}) async-start(s32[16,16,128]{2,1,0:T(8,128)} %broadcast_select_fusion.1), calls=%async_computation | async-start | bytes 262144 | tf_op jit(solution)/shard_map/all_to_all | solution.py:91
  50.4 0.8 broadcast_select_fusion
  51.1 7.1 %all-to-all-done = s32[16,16,128]{2,1,0:T(8,128)S(1)} async-done(((s32[16,16,128]{2,1,0:T(8,128)}), s32[16,16,128]{2,1,0:T(8,128)S(1)}, u32[]{:S(2)}, u32[]{:S(2)}) %all-to-all-start) | async-done | bytes 131104 | tf_op jit(solution)/shard_map/all_to_all | solution.py:91
  58.2 3.6 %all-to-all-start.1 = ((f32[16,16,128]{2,1,0:T(8,128)}), f32[16,16,128]{2,1,0:T(8,128)S(1)}, u32[]{:S(2)}, u32[]{:S(2)}) async-start(f32[16,16,128]{2,1,0:T(8,128)} %broadcast_select_fusion), calls=%async_computation.1 | async-start | bytes 262144 | tf_op jit(solution)/shard_map/all_to_all | solution.py:88
  62.1 7.6 %all-to-all-done.1 = f32[16,16,128]{2,1,0:T(8,128)S(1)} async-done(((f32[16,16,128]{2,1,0:T(8,128)}), f32[16,16,128]{2,1,0:T(8,128)S(1)}, u32[]{:S(2)}, u32[]{:S(2)}) %all-to-all-start.1) | async-done | bytes 131104 | tf_op jit(solution)/shard_map/all_to_all | solution.py:88
  69.7 12.0 %while.15 = (s32[]{:T(128)}, f32[512]{0:T(512)S(1)}, f32[512]{0:T(512)S(1)}, s32[16,2048]{1,0:T(8,128)S(1)}, f32[16,2048]{1,0:T(8,128)S(1)}, /*index=5*/f32[16,2048]{1,0:T(8,128)S(1)}, s32[]{:T(128)}, s32[]{:T(128)}) while((s32[]{:T(128)}, f32[512]{0:T(512)S(1)}, f32[512]{0:T(512)S(1)}, s32[16,2048]{1,0:T(8,128)S(1)}, ...), condition=%wide.region_3.4_spmd.clone, body=%wide.region_2.3_spmd.clone.sunk | while | flops 25524224 | bytes 254055 | solution.py:99
  69.9 0.6 fusion.34
  81.9 1.2 %collective-permute-done.5 = f32[2,512]{1,0:T(2,128)S(1)} collective-permute-done((f32[2,512]{1,0:T(2,128)S(1)}, f32[2,512]{1,0:T(2,128)S(1)}, u32[]{:S(2)}, u32[]{:S(2)}) %collective-permute-start.5) | collective-permute-done | bytes 4128 | tf_op jit(solution)/shard_map/ppermute | solution.py:33
  83.0 0.7 collective-permute-start.6
  83.7 3.0 %collective-permute-done.6 = f32[2,512]{1,0:T(2,128)S(1)} collective-permute-done((f32[2,512]{1,0:T(2,128)S(1)}, f32[2,512]{1,0:T(2,128)S(1)}, u32[]{:S(2)}, u32[]{:S(2)}) %collective-permute-start.6) | collective-permute-done | bytes 4128 | tf_op jit(solution)/shard_map/ppermute | solution.py:33
  86.7 0.7 collective-permute-start.7
  87.4 4.5 %collective-permute-done.7 = f32[2,512]{1,0:T(2,128)S(1)} collective-permute-done((f32[2,512]{1,0:T(2,128)S(1)}, f32[2,512]{1,0:T(2,128)S(1)}, u32[]{:S(2)}, u32[]{:S(2)}) %collective-permute-start.7) | collective-permute-done | bytes 4128 | tf_op jit(solution)/shard_map/ppermute | solution.py:33
  91.9 0.6 fusion.23
  (144 shorter events, 13.2 us)
Async XLA Ops:
  0.0 0.8 copy-start
  0.0 1.0 %copy-start.1 = (f32[1,64,256]{2,1,0:T(8,128)S(1)}, f32[1,64,256]{2,1,0:T(8,128)}, u32[]{:S(2)}) copy-start(f32[1,64,256]{2,1,0:T(8,128)} %param.8) | copy-start | bytes 196612
  1.3 0.7 copy-start.3
  1.3 1.3 %collective-permute-start = (f32[64,128]{0,1:T(8,128)S(1)}, f32[64,128]{0,1:T(8,128)S(1)}, u32[]{:S(2)}, u32[]{:S(2)}) collective-permute-start(f32[64,128]{0,1:T(8,128)S(1)} %pad_maximum_fusion), channel_id=1, source_target_pairs={{0,16},{16,0},{32,48},{48,32},{64,80},{80,64},{96,112},{112,96},{1... | collective-permute-start | bytes 98312 | tf_op jit(solution)/shard_map/ppermute | solution.py:33
  2.6 1.7 %copy-start.4 = (f32[64]{0:T(128)S(1)}, f32[64]{0:T(128)}, u32[]{:S(2)}) copy-start(f32[64]{0:T(128)} %param.10) | copy-start | bytes 772
  2.7 4.3 %collective-permute-start.1 = (f32[64,128]{0,1:T(8,128)S(1)}, f32[64,128]{0,1:T(8,128)S(1)}, u32[]{:S(2)}, u32[]{:S(2)}) collective-permute-start(f32[64,128]{0,1:T(8,128)S(1)} %fusion.25), channel_id=1, source_target_pairs={{0,32},{16,48},{32,0},{48,16},{64,96},{80,112},{96,64},{112,80},{1... | collective-permute-start | bytes 98312 | tf_op jit(solution)/shard_map/ppermute | solution.py:33
  7.0 3.2 %copy-start.5 = (s32[1,16,1]{1,2,0:T(1,128)S(1)}, s32[1,16,1]{1,2,0:T(1,128)}, u32[]{:S(2)}) copy-start(s32[1,16,1]{1,2,0:T(1,128)} %param.13) | copy-start | bytes 196
  7.0 12.0 %collective-permute-start.2 = (f32[64,128]{0,1:T(8,128)S(1)}, f32[64,128]{0,1:T(8,128)S(1)}, u32[]{:S(2)}, u32[]{:S(2)}) collective-permute-start(f32[64,128]{0,1:T(8,128)S(1)} %add.89), channel_id=1, source_target_pairs={{0,64},{16,80},{32,96},{48,112},{64,0},{80,16},{96,32},{112,48},{1... | collective-permute-start | bytes 98312 | tf_op jit(solution)/shard_map/ppermute | solution.py:33
  10.9 31.9 %all-to-all-start.2 = ((f32[16,1,16]{2,1,0:T(1,128)}), f32[16,1,16]{2,1,0:T(1,128)S(1)}, u32[]{:S(2)}, u32[]{:S(2)}) async-start(f32[16,1,16]{2,1,0:T(1,128)} %compare_select_fusion.3), calls=%async_computation.2 | async-start | bytes 16384 | tf_op jit(solution)/shard_map/all_to_all | solution.py:94
  19.0 2.1 %copy-start.2 = (s32[1,64,256]{2,1,0:T(8,128)S(1)}, s32[1,64,256]{2,1,0:T(8,128)}, u32[]{:S(2)}) copy-start(s32[1,64,256]{2,1,0:T(8,128)} %param.11) | copy-start | bytes 196612
  19.0 4.3 %collective-permute-start.3 = (f32[64,128]{0,1:T(8,128)S(1)}, f32[64,128]{0,1:T(8,128)S(1)}, u32[]{:S(2)}, u32[]{:S(2)}) collective-permute-start(f32[64,128]{0,1:T(8,128)S(1)} %add.90), channel_id=1, source_target_pairs={{0,1},{1,0},{2,3},{3,2},{4,5},{5,4},{6,7},{7,6},{8,9},{9,8},{10,11... | collective-permute-start | bytes 98312 | tf_op jit(solution)/shard_map/ppermute | solution.py:33
  23.4 5.8 %collective-permute-start.4 = (f32[64,128]{0,1:T(8,128)S(1)}, f32[64,128]{0,1:T(8,128)S(1)}, u32[]{:S(2)}, u32[]{:S(2)}) collective-permute-start(f32[64,128]{0,1:T(8,128)S(1)} %add.91), channel_id=1, source_target_pairs={{0,2},{1,3},{2,0},{3,1},{4,6},{5,7},{6,4},{7,5},{8,10},{9,11},{10,... | collective-permute-start | bytes 98312 | tf_op jit(solution)/shard_map/ppermute | solution.py:33
  42.9 15.4 %all-to-all-start = ((s32[16,16,128]{2,1,0:T(8,128)}), s32[16,16,128]{2,1,0:T(8,128)S(1)}, u32[]{:S(2)}, u32[]{:S(2)}) async-start(s32[16,16,128]{2,1,0:T(8,128)} %broadcast_select_fusion.1), calls=%async_computation | async-start | bytes 262144 | tf_op jit(solution)/shard_map/all_to_all | solution.py:91
  58.2 11.4 %all-to-all-start.1 = ((f32[16,16,128]{2,1,0:T(8,128)}), f32[16,16,128]{2,1,0:T(8,128)S(1)}, u32[]{:S(2)}, u32[]{:S(2)}) async-start(f32[16,16,128]{2,1,0:T(8,128)} %broadcast_select_fusion), calls=%async_computation.1 | async-start | bytes 262144 | tf_op jit(solution)/shard_map/all_to_all | solution.py:88
  81.8 1.2 %collective-permute-start.5 = (f32[2,512]{1,0:T(2,128)S(1)}, f32[2,512]{1,0:T(2,128)S(1)}, u32[]{:S(2)}, u32[]{:S(2)}) collective-permute-start(f32[2,512]{1,0:T(2,128)S(1)} %pad_maximum_fusion.1), channel_id=1, source_target_pairs={{0,16},{16,0},{32,48},{48,32},{64,80},{80,64},{96,112},{112,96},{1... | collective-permute-start | bytes 12296 | tf_op jit(solution)/shard_map/ppermute | solution.py:33
  83.0 3.7 %collective-permute-start.6 = (f32[2,512]{1,0:T(2,128)S(1)}, f32[2,512]{1,0:T(2,128)S(1)}, u32[]{:S(2)}, u32[]{:S(2)}) collective-permute-start(f32[2,512]{1,0:T(2,128)S(1)} %fusion.24), channel_id=1, source_target_pairs={{0,32},{16,48},{32,0},{48,16},{64,96},{80,112},{96,64},{112,80},{1... | collective-permute-start | bytes 12296 | tf_op jit(solution)/shard_map/ppermute | solution.py:33
  86.7 5.2 %collective-permute-start.7 = (f32[2,512]{1,0:T(2,128)S(1)}, f32[2,512]{1,0:T(2,128)S(1)}, u32[]{:S(2)}, u32[]{:S(2)}) collective-permute-start(f32[2,512]{1,0:T(2,128)S(1)} %fusion.28), channel_id=1, source_target_pairs={{0,64},{16,80},{32,96},{48,112},{64,0},{80,16},{96,32},{112,48},{1... | collective-permute-start | bytes 12296 | tf_op jit(solution)/shard_map/ppermute | solution.py:33

commit v2 on v1

v2 whole, which is shorter than its diff:
```python
import jax
import jax.numpy as jnp
from jax import lax
from jax.sharding import PartitionSpec as P

BL = 128
TILE = 512
HIGHEST = lax.Precision.HIGHEST


def all_sum(x, axes):
    for axis in axes:
        size = lax.axis_size(axis)
        bit = 1
        while bit < size:
            x = x + lax.ppermute(x, axis, [(i, i ^ bit) for i in range(size)])
            bit *= 2
    return x


def bin_tiles(values, pixels, weights, tile_of_sample, owners):
    uppers = owners * (TILE // 128)
    upper = jnp.where(tile_of_sample >= 0, tile_of_sample * (TILE // 128) + pixels // 128, -1).reshape(-1)
    lower = (pixels % 128).reshape(-1)
    count = upper.shape[0]
    upper_hot = (lax.broadcasted_iota(jnp.int32, (uppers, count), 0) == upper[None, :]).astype(jnp.float32)
    lower_hot = (lax.broadcasted_iota(jnp.int32, (128, count), 0) == lower[None, :]).astype(jnp.float32)
    stacked = jnp.concatenate(
        [upper_hot * values.reshape(1, -1), upper_hot * weights.reshape(1, -1)], axis=0
    )
    binned = lax.dot_general(
        stacked, lower_hot, (((1,), (1,)), ((), ())), precision=HIGHEST,
        preferred_element_type=jnp.float32,
    )
    num = binned[:uppers].reshape(owners, TILE)
    wgt = binned[uppers:].reshape(owners, TILE)
    return jnp.concatenate([num, wgt], axis=1)


def shards(tod, templates, det_weight, pixel, hitlist, counts):
    dets, samp_local = tod.shape[1], tod.shape[2]
    owners = hitlist.shape[1]
    slots = hitlist.shape[2]
    per_det = samp_local // BL
    blocks = dets * per_det

    template_rows = templates[0]
    streams = tod[0]
    gram_sum = lax.dot_general(
        template_rows, template_rows, (((1,), (1,)), ((), ())),
        precision=HIGHEST, preferred_element_type=jnp.float32,
    )
    projection = lax.dot_general(
        template_rows, streams, (((1,), (1,)), ((), ())),
        precision=HIGHEST, preferred_element_type=jnp.float32,
    )
    joined = all_sum(jnp.concatenate([gram_sum, projection], axis=1), ("section", "sub"))
    gram_sum, projection = joined[:, : gram_sum.shape[1]], joined[:, gram_sum.shape[1] :]
    factor = jnp.linalg.cholesky(gram_sum)
    coef_fit = jax.scipy.linalg.cho_solve((factor, True), projection)
    removed = lax.dot_general(
        coef_fit, template_rows, (((0,), (0,)), ((), ())),
        precision=HIGHEST, preferred_element_type=jnp.float32,
    )
    filtered = streams - removed
    weighted = filtered * det_weight[:, None]
    sample_weight = jnp.broadcast_to(det_weight[:, None], streams.shape)

    slot_ids = lax.broadcasted_iota(jnp.int32, (owners, slots), 1)
    live = slot_ids < counts[0]
    named = (hitlist[0][:, :, None] == lax.broadcasted_iota(jnp.int32, (1, 1, blocks), 2)) & live[:, :, None]
    in_tile = jnp.any(named, axis=1)
    tile_ids = lax.broadcasted_iota(jnp.int32, (owners, blocks), 0)
    tile_of_block = jnp.where(jnp.any(in_tile, axis=0), jnp.sum(jnp.where(in_tile, tile_ids, 0), axis=0), -1)
    tile_of_sample = jnp.repeat(tile_of_block.reshape(dets, per_det), BL, axis=1)

    partial = bin_tiles(weighted, pixel[0], sample_weight, tile_of_sample, owners)
    got = lax.all_to_all(partial, ("wafer", "sub"), split_axis=0, concat_axis=0, tiled=True)
    tile_sum = all_sum(jnp.sum(got, axis=0), ("section",))
    num_tile, wgt_tile = tile_sum[:TILE], tile_sum[TILE:]
    return num_tile / jnp.maximum(wgt_tile, 1.0)


def solution(mesh):
    placed = (
        P(None, "wafer", ("section", "sub")),
        P(None, "wafer", ("section", "sub")),
        P("wafer"),
        P(None, "wafer", ("section", "sub")),
        P(None, "wafer", ("section", "sub")),
        P(None, "wafer", ("section", "sub")),
    )
    return jax.shard_map(
        shards, mesh=mesh, in_specs=placed, out_specs=P(("wafer", "sub")), check_vma=False
    )
```

time: 92.9 us -> 71 us (0.76)
  blocking collectives: 0 us -> 15.3 us
  starting transfers between devices: 31.1 us -> 15.8 us
  waiting for transfers between devices: 27.5 us -> 13 us
  local copies, waits for them, and re-layouts: 5.78 us -> 3.24 us
  matrix products: 10.3 us -> 7.84 us
  other arithmetic: 16.7 us -> 15.3 us
    all_to_all x3 -> x0, starting transfers between devices: 19.2 us -> none  [the longest x1 8.05 us: shards(): lax.all_to_all(send_weights, ('wafer', 'sub'), split_axis=0, concat_axis=...]
    all_to_all x0 -> x1, blocking collectives: none -> 15.3 us  [shards(): lax.all_to_all(partial, ('wafer', 'sub'), split_axis=0, concat_axis=0, ti...]
    all_to_all x3 -> x0, waiting for transfers between devices: 14.7 us -> none  [the longest x1 7.62 us: shards(): lax.all_to_all(send_values, ('wafer', 'sub'), split_axis=0, concat_axis=0...]
    dot_general x16 -> x1, matrix products: 9.19 us -> 5.09 us  [bin_tiles(): lax.dot_general(stacked, lower_hot, (((1,), (1,)), ((), ())), precision=H...]
    ppermute x8, starting transfers between devices: 12 us -> 15.8 us  [all_sum(): x = x + lax.ppermute(x, axis, [(i, i ^ bit) for i in range(size)])]
    gather x4 -> x0, local copies, waits for them, and re-layouts: 3.42 us -> none  [the longest x2 1.96 us: shards(): send_weights = jnp.where(live_slots, block_weight[hit_rows], 0.0)]
    select_n x36 -> x1, other arithmetic: 3.2 us -> 0.07 us  [bin_tiles(): lower = (pixels % 128).reshape(-1)]
    unnamed x15 -> x6, local copies, waits for them, and re-layouts: 1.57 us -> 2.51 us
  transfers between devices with their start and end apart: 11 -> 8, of which waited for: 9 -> 7; matrix products, arithmetic and copies ran while one was open for 21% -> 6% of each run, Pallas kernels for 0% -> 0%
where the time goes in v2:
time: 71 us; the launch traced here: 70.7 us
  starting transfers between devices  15.8 us (22%)
  other arithmetic  15.3 us (22%)
  blocking collectives  15.3 us (22%)
  waiting for transfers between devices  13 us (18%)
  matrix products  7.84 us (11%)
  local copies, waits for them, and re-layouts  3.24 us (5%)
    ppermute x8, starting transfers between devices, all_sum(): x = x + lax.ppermute(x, axis, [(i, i ^ bit) for i in range(size)])  15.8 us
    all_to_all x1, blocking collectives, shards(): lax.all_to_all(partial, ('wafer', 'sub'), split_axis=0, concat_axis=0, ti...  15.3 us
    ppermute x8, waiting for transfers between devices, all_sum(): x = x + lax.ppermute(x, axis, [(i, i ^ bit) for i in range(size)])  13 us
    another operation x3, other arithmetic, shards(): factor = jnp.linalg.cholesky(gram_sum)  6.52 us
    another operation x2, other arithmetic, shards(): coef_fit = jax.scipy.linalg.cho_solve((factor, True), projection)  5.55 us
    dot_general x1, matrix products, bin_tiles(): lax.dot_general(stacked, lower_hot, (((1,), (1,)), ((), ())), precision=H...  5.09 us
    unnamed x6, local copies, waits for them, and re-layouts  2.51 us
  transfers between devices with their start and end apart: 8, of which 7 were waited for; matrix products, arithmetic and copies ran while one was open for 6% of the time, Pallas kernels for 0%

profile of v2, /device:TPU:0, one launch (start us, length us, event | category | flops | bytes accessed | tf_op | source)
XLA Modules:
  0.0 70.7 jit_solution(11466546777750393818)
XLA Ops:
  0.0 0.8 %copy-done = f32[1,64,256]{2,1,0:T(8,128)S(1)} copy-done((f32[1,64,256]{2,1,0:T(8,128)S(1)}, f32[1,64,256]{2,1,0:T(8,128)}, u32[]{:S(2)}) %copy-start) | copy-done | bytes 65560
  0.8 0.2 fusion.17
  1.0 1.0 %fusion.15 = f32[64,64]{0,1:T(8,128)S(1)} fusion(f32[1,64,256]{2,1,0:T(8,128)S(1)} %copy-done, f32[1,64,256]{2,1,0:T(8,128)} %param.6), kind=kOutput, calls=%fused_computation.26 | convolution fusion | flops 12582912 | bytes 147456 | tf_op jit(solution)/shard_map/dot_general | solution.py:53
  2.2 0.7 %iota_compare_fusion.6 = pred[16,16]{1,0:T(8,128)(4,1)S(1)} fusion(s32[16]{0:T(128)} %bitcast.41), kind=kLoop, calls=%fused_computation.48 | loop fusion | flops 256 | bytes 320 | tf_op jit(solution)/shard_map/lt | solution.py:70
  2.9 0.8 %fusion.10 = (pred[16,128]{1,0:T(8,128)(4,1)S(1)}, pred[128]{0:T(512)(128)(4,1)S(1)}) fusion(s32[16,16]{1,0:T(8,128)} %bitcast.40, pred[16,16]{1,0:T(8,128)(4,1)S(1)} %iota_compare_fusion.6), kind=kLoop, calls=%fused_computation.14 | loop fusion | flops 128896 | bytes 3456 | tf_op jit(solution)/shard_map/reduce_or | solution.py:72
  3.8 1.7 %collective-permute-start.1 = (f32[64,128]{0,1:T(8,128)S(1)}, f32[64,128]{0,1:T(8,128)S(1)}, u32[]{:S(2)}, u32[]{:S(2)}) collective-permute-start(f32[64,128]{0,1:T(8,128)S(1)} %fusion.30), channel_id=1, source_target_pairs={{0,32},{16,48},{32,0},{48,16},{64,96},{80,112},{96,64},{112,80},{1... | collective-permute-start | bytes 98312 | tf_op jit(solution)/shard_map/ppermute | solution.py:16
  5.5 2.9 %collective-permute-done.1 = f32[64,128]{0,1:T(8,128)S(1)} collective-permute-done((f32[64,128]{0,1:T(8,128)S(1)}, f32[64,128]{0,1:T(8,128)S(1)}, u32[]{:S(2)}, u32[]{:S(2)}) %collective-permute-start.1) | collective-permute-done | bytes 32800 | tf_op jit(solution)/shard_map/ppermute | solution.py:16
  8.4 3.2 %collective-permute-start.2 = (f32[64,128]{0,1:T(8,128)S(1)}, f32[64,128]{0,1:T(8,128)S(1)}, u32[]{:S(2)}, u32[]{:S(2)}) collective-permute-start(f32[64,128]{0,1:T(8,128)S(1)} %add.63), channel_id=1, source_target_pairs={{0,64},{16,80},{32,96},{48,112},{64,0},{80,16},{96,32},{112,48},{1... | collective-permute-start | bytes 98312 | tf_op jit(solution)/shard_map/ppermute | solution.py:16
  11.6 0.2 ge.23
  12.1 0.9 %copy.21 = s32[8,2,8,128]{3,1,2,0:T(2,128)S(1)} copy(s32[8,2,8,128]{3,2,1,0:T(8,128)} %bitcast.39) | data formatting | bytes 131072
  13.0 1.3 %collective-permute-done.2 = f32[64,128]{0,1:T(8,128)S(1)} collective-permute-done((f32[64,128]{0,1:T(8,128)S(1)}, f32[64,128]{0,1:T(8,128)S(1)}, u32[]{:S(2)}, u32[]{:S(2)}) %collective-permute-start.2) | collective-permute-done | bytes 32800 | tf_op jit(solution)/shard_map/ppermute | solution.py:16
  14.3 2.1 %collective-permute-start.3 = (f32[64,128]{0,1:T(8,128)S(1)}, f32[64,128]{0,1:T(8,128)S(1)}, u32[]{:S(2)}, u32[]{:S(2)}) collective-permute-start(f32[64,128]{0,1:T(8,128)S(1)} %add.64), channel_id=1, source_target_pairs={{0,1},{1,0},{2,3},{3,2},{4,5},{5,4},{6,7},{7,6},{8,9},{9,8},{10,11... | collective-permute-start | bytes 98312 | tf_op jit(solution)/shard_map/ppermute | solution.py:16
  16.6 2.0 %collective-permute-done.3 = f32[64,128]{0,1:T(8,128)S(1)} collective-permute-done((f32[64,128]{0,1:T(8,128)S(1)}, f32[64,128]{0,1:T(8,128)S(1)}, u32[]{:S(2)}, u32[]{:S(2)}) %collective-permute-start.3) | collective-permute-done | bytes 32800 | tf_op jit(solution)/shard_map/ppermute | solution.py:16
  18.7 4.1 %collective-permute-start.4 = (f32[64,128]{0,1:T(8,128)S(1)}, f32[64,128]{0,1:T(8,128)S(1)}, u32[]{:S(2)}, u32[]{:S(2)}) collective-permute-start(f32[64,128]{0,1:T(8,128)S(1)} %add.65), channel_id=1, source_target_pairs={{0,2},{1,3},{2,0},{3,1},{4,6},{5,7},{6,4},{7,5},{8,10},{9,11},{10,... | collective-permute-start | bytes 98312 | tf_op jit(solution)/shard_map/ppermute | solution.py:16
  22.7 0.7 %broadcast_bitcast_fusion = f32[8,2,8,128]{3,2,1,0:T(8,128)S(1)} fusion(f32[64]{0:T(128)} %param.8), kind=kLoop, calls=%fused_computation.43 | loop fusion | bytes 65792
  23.5 1.5 %collective-permute-done.4 = f32[64,128]{0,1:T(8,128)S(1)} collective-permute-done((f32[64,128]{0,1:T(8,128)S(1)}, f32[64,128]{0,1:T(8,128)S(1)}, u32[]{:S(2)}, u32[]{:S(2)}) %collective-permute-start.4) | collective-permute-done | bytes 32800 | tf_op jit(solution)/shard_map/ppermute | solution.py:16
  25.1 5.8 %cholesky.16 = f32[64,64]{1,0:T(8,128)S(1)} custom-call(f32[64,64]{1,0:T(8,128)S(1)} %fusion.28), custom_call_target="Cholesky" | custom-call | tf_op jit(solution)/shard_map/jit(cholesky)/cholesky | solution.py:59
  31.0 0.6 compare_reduce_fusion
  31.6 0.7 fusion.22
  32.3 4.9 %custom-call.10 = f32[1,64,64]{1,2,0:T(8,128)S(1)} custom-call(f32[1,64,64]{2,1,0:T(8,128)S(1)} %fusion.22), custom_call_target="InvertDiagBlocksLowerTriangular" | custom-call | tf_op jit(solution)/shard_map/jit(_cho_solve)/triangular_solve | solution.py:60
  37.2 0.2 fusion.23
  37.4 0.2 fusion.25
  37.6 1.1 %fusion.8 = f32[8,2,8,128]{3,2,1,0:T(8,128)S(1)} fusion(f32[64,64]{1,0:T(8,128)S(1)} %fusion.25, f32[1,64,256]{2,1,0:T(8,128)S(1)} %copy-done, f32[1,64,256]{2,1,0:T(8,128)} %param.6, f32[64]{0:T(128)} %param.8), kind=kOutput, calls=%fused_computation.11 | convolution fusion | flops 12615680 | bytes 213248 | tf_op jit(solution)/shard_map/dot_general | solution.py:61
  38.7 0.8 %fusion.6 = (f32[64,16384]{1,0:T(8,128)S(1)}, f32[64,16384]{1,0:T(8,128)S(1)}) fusion(f32[16384]{0:T(1024)S(1)} %bitcast.36, s32[16384]{0:T(1024)S(1)} %get-tuple-element.10, f32[16384]{0:T(1024)S(1)} %bitcast.35), kind=kLoop, calls=%fused_computation.8 | loop fusion | flops 3145728 | bytes 8585216 | tf_op jit(solution)/shard_map/mul | solution.py:29
  39.6 5.1 %fusion = f32[128,128]{1,0:T(8,128)S(1)} fusion(f32[64,16384]{1,0:T(8,128)S(1)} %get-tuple-element.12, f32[64,16384]{1,0:T(8,128)S(1)} %get-tuple-element.11, s32[16384]{0:T(1024)S(1)} %get-tuple-element.9), kind=kOutput, calls=%fused_computation | convolution fusion | flops 3225419776 | bytes 8519680 | tf_op jit(solution)/shard_map/dot_general | solution.py:31
  44.8 15.3 %all_to_all.9 = f32[16,1,1024]{2,1,0:T(1,128)S(1)} all-to-all(f32[16,1,1024]{2,1,0:T(1,128)S(1)} %all_to_all.6), channel_id=1, replica_groups=mesh['section'=8,'wafer'=4,'sub'=4] {'wafer','sub'}, dimensions={0} | all-to-all | bytes 131072 | tf_op jit(solution)/shard_map/all_to_all | solution.py:78
  60.2 1.2 %collective-permute-done.5 = f32[1024]{0:T(1024)S(1)} collective-permute-done((f32[1024]{0:T(1024)S(1)}, f32[1024]{0:T(1024)S(1)}, u32[]{:S(2)}, u32[]{:S(2)}) %collective-permute-start.5) | collective-permute-done | bytes 4128 | tf_op jit(solution)/shard_map/ppermute | solution.py:16
  61.3 1.5 %collective-permute-start.6 = (f32[1024]{0:T(1024)S(1)}, f32[1024]{0:T(1024)S(1)}, u32[]{:S(2)}, u32[]{:S(2)}) collective-permute-start(f32[1024]{0:T(1024)S(1)} %add.69), channel_id=1, source_target_pairs={{0,32},{16,48},{32,0},{48,16},{64,96},{80,112},{96,64},{112,80},{1... | collective-permute-start | bytes 12296 | tf_op jit(solution)/shard_map/ppermute | solution.py:16
  62.8 2.1 %collective-permute-done.6 = f32[1024]{0:T(1024)S(1)} collective-permute-done((f32[1024]{0:T(1024)S(1)}, f32[1024]{0:T(1024)S(1)}, u32[]{:S(2)}, u32[]{:S(2)}) %collective-permute-start.6) | collective-permute-done | bytes 4128 | tf_op jit(solution)/shard_map/ppermute | solution.py:16
  64.9 3.0 %collective-permute-start.7 = (f32[1024]{0:T(1024)S(1)}, f32[1024]{0:T(1024)S(1)}, u32[]{:S(2)}, u32[]{:S(2)}) collective-permute-start(f32[1024]{0:T(1024)S(1)} %add.70), channel_id=1, source_target_pairs={{0,64},{16,80},{32,96},{48,112},{64,0},{80,16},{96,32},{112,48},{1... | collective-permute-start | bytes 12296 | tf_op jit(solution)/shard_map/ppermute | solution.py:16
  68.0 2.1 %collective-permute-done.7 = f32[1024]{0:T(1024)S(1)} collective-permute-done((f32[1024]{0:T(1024)S(1)}, f32[1024]{0:T(1024)S(1)}, u32[]{:S(2)}, u32[]{:S(2)}) %collective-permute-start.7) | collective-permute-done | bytes 4128 | tf_op jit(solution)/shard_map/ppermute | solution.py:16
  70.1 0.6 maximum_divide_fusion
  (33 shorter events, 1.1 us)
Async XLA Ops:
  0.0 0.8 %copy-start = (f32[1,64,256]{2,1,0:T(8,128)S(1)}, f32[1,64,256]{2,1,0:T(8,128)}, u32[]{:S(2)}) copy-start(f32[1,64,256]{2,1,0:T(8,128)} %param.7) | copy-start | bytes 196612
  2.1 1.7 %collective-permute-start = (f32[64,128]{0,1:T(8,128)S(1)}, f32[64,128]{0,1:T(8,128)S(1)}, u32[]{:S(2)}, u32[]{:S(2)}) collective-permute-start(f32[64,128]{0,1:T(8,128)S(1)} %pad_maximum_fusion), channel_id=1, source_target_pairs={{0,16},{16,0},{32,48},{48,32},{64,80},{80,64},{96,112},{112,96},{1... | collective-permute-start | bytes 98312 | tf_op jit(solution)/shard_map/ppermute | solution.py:16
  3.8 4.6 %collective-permute-start.1 = (f32[64,128]{0,1:T(8,128)S(1)}, f32[64,128]{0,1:T(8,128)S(1)}, u32[]{:S(2)}, u32[]{:S(2)}) collective-permute-start(f32[64,128]{0,1:T(8,128)S(1)} %fusion.30), channel_id=1, source_target_pairs={{0,32},{16,48},{32,0},{48,16},{64,96},{80,112},{96,64},{112,80},{1... | collective-permute-start | bytes 98312 | tf_op jit(solution)/shard_map/ppermute | solution.py:16
  8.4 5.8 %collective-permute-start.2 = (f32[64,128]{0,1:T(8,128)S(1)}, f32[64,128]{0,1:T(8,128)S(1)}, u32[]{:S(2)}, u32[]{:S(2)}) collective-permute-start(f32[64,128]{0,1:T(8,128)S(1)} %add.63), channel_id=1, source_target_pairs={{0,64},{16,80},{32,96},{48,112},{64,0},{80,16},{96,32},{112,48},{1... | collective-permute-start | bytes 98312 | tf_op jit(solution)/shard_map/ppermute | solution.py:16
  14.3 4.4 %collective-permute-start.3 = (f32[64,128]{0,1:T(8,128)S(1)}, f32[64,128]{0,1:T(8,128)S(1)}, u32[]{:S(2)}, u32[]{:S(2)}) collective-permute-start(f32[64,128]{0,1:T(8,128)S(1)} %add.64), channel_id=1, source_target_pairs={{0,1},{1,0},{2,3},{3,2},{4,5},{5,4},{6,7},{7,6},{8,9},{9,8},{10,11... | collective-permute-start | bytes 98312 | tf_op jit(solution)/shard_map/ppermute | solution.py:16
  18.7 6.3 %collective-permute-start.4 = (f32[64,128]{0,1:T(8,128)S(1)}, f32[64,128]{0,1:T(8,128)S(1)}, u32[]{:S(2)}, u32[]{:S(2)}) collective-permute-start(f32[64,128]{0,1:T(8,128)S(1)} %add.65), channel_id=1, source_target_pairs={{0,2},{1,3},{2,0},{3,1},{4,6},{5,7},{6,4},{7,5},{8,10},{9,11},{10,... | collective-permute-start | bytes 98312 | tf_op jit(solution)/shard_map/ppermute | solution.py:16
  60.1 1.2 %collective-permute-start.5 = (f32[1024]{0:T(1024)S(1)}, f32[1024]{0:T(1024)S(1)}, u32[]{:S(2)}, u32[]{:S(2)}) collective-permute-start(f32[1024]{0:T(1024)S(1)} %reduce_sum.19), channel_id=1, source_target_pairs={{0,16},{16,0},{32,48},{48,32},{64,80},{80,64},{96,112},{112,96},{1... | collective-permute-start | bytes 12296 | tf_op jit(solution)/shard_map/ppermute | solution.py:16
  61.3 3.6 %collective-permute-start.6 = (f32[1024]{0:T(1024)S(1)}, f32[1024]{0:T(1024)S(1)}, u32[]{:S(2)}, u32[]{:S(2)}) collective-permute-start(f32[1024]{0:T(1024)S(1)} %add.69), channel_id=1, source_target_pairs={{0,32},{16,48},{32,0},{48,16},{64,96},{80,112},{96,64},{112,80},{1... | collective-permute-start | bytes 12296 | tf_op jit(solution)/shard_map/ppermute | solution.py:16
  64.9 5.1 %collective-permute-start.7 = (f32[1024]{0:T(1024)S(1)}, f32[1024]{0:T(1024)S(1)}, u32[]{:S(2)}, u32[]{:S(2)}) collective-permute-start(f32[1024]{0:T(1024)S(1)} %add.70), channel_id=1, source_target_pairs={{0,64},{16,80},{32,96},{48,112},{64,0},{80,16},{96,32},{112,48},{1... | collective-permute-start | bytes 12296 | tf_op jit(solution)/shard_map/ppermute | solution.py:16

commit v3 on v2

--- a/solution.py
+++ b/solution.py
@@ -18,22 +18,29 @@
     return x
 
 
+def split_bf16(x, parts):
+    pieces = []
+    for _ in range(parts):
+        head = lax.reduce_precision(x, exponent_bits=8, mantissa_bits=7)
+        pieces.append(head.astype(jnp.bfloat16))
+        x = x - head
+    return pieces
+
+
 def bin_tiles(values, pixels, weights, tile_of_sample, owners):
     uppers = owners * (TILE // 128)
     upper = jnp.where(tile_of_sample >= 0, tile_of_sample * (TILE // 128) + pixels // 128, -1).reshape(-1)
     lower = (pixels % 128).reshape(-1)
     count = upper.shape[0]
-    upper_hot = (lax.broadcasted_iota(jnp.int32, (uppers, count), 0) == upper[None, :]).astype(jnp.float32)
-    lower_hot = (lax.broadcasted_iota(jnp.int32, (128, count), 0) == lower[None, :]).astype(jnp.float32)
-    stacked = jnp.concatenate(
-        [upper_hot * values.reshape(1, -1), upper_hot * weights.reshape(1, -1)], axis=0
-    )
+    upper_hot = lax.broadcasted_iota(jnp.int32, (uppers, count), 0) == upper[None, :]
+    lower_hot = (lax.broadcasted_iota(jnp.int32, (128, count), 0) == lower[None, :]).astype(jnp.bfloat16)
+    pieces = split_bf16(values.reshape(1, -1), 3) + split_bf16(weights.reshape(1, -1), 3)
+    stacked = jnp.concatenate([jnp.where(upper_hot, p, jnp.bfloat16(0)) for p in pieces], axis=0)
     binned = lax.dot_general(
-        stacked, lower_hot, (((1,), (1,)), ((), ())), precision=HIGHEST,
-        preferred_element_type=jnp.float32,
-    )
-    num = binned[:uppers].reshape(owners, TILE)
-    wgt = binned[uppers:].reshape(owners, TILE)
+        stacked, lower_hot, (((1,), (1,)), ((), ())), preferred_element_type=jnp.float32,
+    ).reshape(6, uppers, 128)
+    num = ((binned[0] + binned[1]) + binned[2]).reshape(owners, TILE)
+    wgt = ((binned[3] + binned[4]) + binned[5]).reshape(owners, TILE)
     return jnp.concatenate([num, wgt], axis=1)
 
 

time: 71 us -> 71.1 us (level)
  matrix products: 7.84 us -> 6.34 us
  other arithmetic: 15.3 us -> 16.8 us
    unnamed x0 -> x5, other arithmetic: none -> 1.92 us
    dot_general x1, matrix products: 5.09 us -> 3.58 us  [bin_tiles(): lax.dot_general(stacked, lower_hot, (((1,), (1,)), ((), ())), preferred_e...]
    mul x1 -> x0, other arithmetic: 0.82 us -> none  [bin_tiles(): upper_hot * values.reshape(1, -1)]
where the time goes in v3:
time: 71.1 us; the launch traced here: 70.7 us
  other arithmetic  16.8 us (24%)
  starting transfers between devices  15.8 us (22%)
  blocking collectives  15.3 us (22%)
  waiting for transfers between devices  13 us (18%)
  matrix products  6.34 us (9%)
  local copies, waits for them, and re-layouts  3.23 us (5%)
    ppermute x8, starting transfers between devices, all_sum(): x = x + lax.ppermute(x, axis, [(i, i ^ bit) for i in range(size)])  15.8 us
    all_to_all x1, blocking collectives, shards(): lax.all_to_all(partial, ('wafer', 'sub'), split_axis=0, concat_axis=0, ti...  15.3 us
    ppermute x8, waiting for transfers between devices, all_sum(): x = x + lax.ppermute(x, axis, [(i, i ^ bit) for i in range(size)])  13 us
    another operation x3, other arithmetic, shards(): factor = jnp.linalg.cholesky(gram_sum)  6.52 us
    another operation x2, other arithmetic, shards(): coef_fit = jax.scipy.linalg.cho_solve((factor, True), projection)  5.55 us
    dot_general x1, matrix products, bin_tiles(): lax.dot_general(stacked, lower_hot, (((1,), (1,)), ((), ())), preferred_e...  3.58 us
    unnamed x6, local copies, waits for them, and re-layouts  2.51 us
    unnamed x5, other arithmetic  1.92 us
  transfers between devices with their start and end apart: 8, of which 7 were waited for; matrix products, arithmetic and copies ran while one was open for 6% of the time, Pallas kernels for 0%

profile of v3, /device:TPU:0, one launch (start us, length us, event | category | flops | bytes accessed | tf_op | source)
XLA Modules:
  0.0 70.7 jit_solution(17783328377898432676)
XLA Ops:
  0.0 0.8 %copy-done = f32[1,64,256]{2,1,0:T(8,128)S(1)} copy-done((f32[1,64,256]{2,1,0:T(8,128)S(1)}, f32[1,64,256]{2,1,0:T(8,128)}, u32[]{:S(2)}) %copy-start) | copy-done | bytes 65560
  1.0 1.0 %fusion.26 = f32[64,64]{0,1:T(8,128)S(1)} fusion(f32[1,64,256]{2,1,0:T(8,128)S(1)} %copy-done, f32[1,64,256]{2,1,0:T(8,128)} %param.6), kind=kOutput, calls=%fused_computation.45 | convolution fusion | flops 12582912 | bytes 147456 | tf_op jit(solution)/shard_map/dot_general | solution.py:60
  2.2 0.7 %iota_compare_fusion.6 = pred[16,16]{1,0:T(8,128)(4,1)S(1)} fusion(s32[16]{0:T(128)} %bitcast.42), kind=kLoop, calls=%fused_computation.71 | loop fusion | flops 256 | bytes 320 | tf_op jit(solution)/shard_map/lt | solution.py:77
  2.9 0.8 %fusion.17 = (pred[16,128]{1,0:T(8,128)(4,1)S(1)}, pred[128]{0:T(512)(128)(4,1)S(1)}) fusion(s32[16,16]{1,0:T(8,128)} %bitcast.41, pred[16,16]{1,0:T(8,128)(4,1)S(1)} %iota_compare_fusion.6), kind=kLoop, calls=%fused_computation.21 | loop fusion | flops 128896 | bytes 3456 | tf_op jit(solution)/shard_map/reduce_or | solution.py:79
  3.9 1.7 %collective-permute-start.1 = (f32[64,128]{0,1:T(8,128)S(1)}, f32[64,128]{0,1:T(8,128)S(1)}, u32[]{:S(2)}, u32[]{:S(2)}) collective-permute-start(f32[64,128]{0,1:T(8,128)S(1)} %fusion.40), channel_id=1, source_target_pairs={{0,32},{16,48},{32,0},{48,16},{64,96},{80,112},{96,64},{112,80},{1... | collective-permute-start | bytes 98312 | tf_op jit(solution)/shard_map/ppermute | solution.py:16
  6.0 0.9 %copy.21 = s32[8,2,8,128]{3,1,2,0:T(2,128)S(1)} copy(s32[8,2,8,128]{3,2,1,0:T(8,128)} %bitcast.40) | data formatting | bytes 131072
  6.9 1.5 %collective-permute-done.1 = f32[64,128]{0,1:T(8,128)S(1)} collective-permute-done((f32[64,128]{0,1:T(8,128)S(1)}, f32[64,128]{0,1:T(8,128)S(1)}, u32[]{:S(2)}, u32[]{:S(2)}) %collective-permute-start.1) | collective-permute-done | bytes 32800 | tf_op jit(solution)/shard_map/ppermute | solution.py:16
  8.4 3.2 %collective-permute-start.2 = (f32[64,128]{0,1:T(8,128)S(1)}, f32[64,128]{0,1:T(8,128)S(1)}, u32[]{:S(2)}, u32[]{:S(2)}) collective-permute-start(f32[64,128]{0,1:T(8,128)S(1)} %add.87), channel_id=1, source_target_pairs={{0,64},{16,80},{32,96},{48,112},{64,0},{80,16},{96,32},{112,48},{1... | collective-permute-start | bytes 98312 | tf_op jit(solution)/shard_map/ppermute | solution.py:16
  11.9 2.4 %collective-permute-done.2 = f32[64,128]{0,1:T(8,128)S(1)} collective-permute-done((f32[64,128]{0,1:T(8,128)S(1)}, f32[64,128]{0,1:T(8,128)S(1)}, u32[]{:S(2)}, u32[]{:S(2)}) %collective-permute-start.2) | collective-permute-done | bytes 32800 | tf_op jit(solution)/shard_map/ppermute | solution.py:16
  14.3 2.1 %collective-permute-start.3 = (f32[64,128]{0,1:T(8,128)S(1)}, f32[64,128]{0,1:T(8,128)S(1)}, u32[]{:S(2)}, u32[]{:S(2)}) collective-permute-start(f32[64,128]{0,1:T(8,128)S(1)} %add.88), channel_id=1, source_target_pairs={{0,1},{1,0},{2,3},{3,2},{4,5},{5,4},{6,7},{7,6},{8,9},{9,8},{10,11... | collective-permute-start | bytes 98312 | tf_op jit(solution)/shard_map/ppermute | solution.py:16
  16.4 0.7 %broadcast_bitcast_fusion = f32[8,2,8,128]{3,2,1,0:T(8,128)S(1)} fusion(f32[64]{0:T(128)} %param.8), kind=kLoop, calls=%fused_computation.66 | loop fusion | bytes 65792
  17.2 1.5 %collective-permute-done.3 = f32[64,128]{0,1:T(8,128)S(1)} collective-permute-done((f32[64,128]{0,1:T(8,128)S(1)}, f32[64,128]{0,1:T(8,128)S(1)}, u32[]{:S(2)}, u32[]{:S(2)}) %collective-permute-start.3) | collective-permute-done | bytes 32800 | tf_op jit(solution)/shard_map/ppermute | solution.py:16
  18.7 4.1 %collective-permute-start.4 = (f32[64,128]{0,1:T(8,128)S(1)}, f32[64,128]{0,1:T(8,128)S(1)}, u32[]{:S(2)}, u32[]{:S(2)}) collective-permute-start(f32[64,128]{0,1:T(8,128)S(1)} %add.89), channel_id=1, source_target_pairs={{0,2},{1,3},{2,0},{3,1},{4,6},{5,7},{6,4},{7,5},{8,10},{9,11},{10,... | collective-permute-start | bytes 98312 | tf_op jit(solution)/shard_map/ppermute | solution.py:16
  22.7 2.2 %collective-permute-done.4 = f32[64,128]{0,1:T(8,128)S(1)} collective-permute-done((f32[64,128]{0,1:T(8,128)S(1)}, f32[64,128]{0,1:T(8,128)S(1)}, u32[]{:S(2)}, u32[]{:S(2)}) %collective-permute-start.4) | collective-permute-done | bytes 32800 | tf_op jit(solution)/shard_map/ppermute | solution.py:16
  25.1 5.8 %cholesky.16 = f32[64,64]{1,0:T(8,128)S(1)} custom-call(f32[64,64]{1,0:T(8,128)S(1)} %fusion.39), custom_call_target="Cholesky" | custom-call | tf_op jit(solution)/shard_map/jit(cholesky)/cholesky | solution.py:66
  31.0 0.6 compare_reduce_fusion
  31.6 0.7 fusion.33
  32.3 4.9 %custom-call.10 = f32[1,64,64]{1,2,0:T(8,128)S(1)} custom-call(f32[1,64,64]{2,1,0:T(8,128)S(1)} %fusion.33), custom_call_target="InvertDiagBlocksLowerTriangular" | custom-call | tf_op jit(solution)/shard_map/jit(_cho_solve)/triangular_solve | solution.py:67
  37.6 1.1 %fusion.15 = f32[8,2,8,128]{3,2,1,0:T(8,128)S(1)} fusion(f32[64,64]{1,0:T(8,128)S(1)} %fusion.36, f32[1,64,256]{2,1,0:T(8,128)S(1)} %copy-done, f32[1,64,256]{2,1,0:T(8,128)} %param.6, f32[64]{0:T(128)} %param.8), kind=kOutput, calls=%fused_computation.18 | convolution fusion | flops 12615680 | bytes 213248 | tf_op jit(solution)/shard_map/dot_general | solution.py:68
  39.2 0.4 fusion.9
  39.6 0.4 fusion.10
  39.9 0.4 fusion.11
  40.3 0.4 fusion.12
  40.7 0.4 fusion.13
  41.1 3.6 %fusion = f32[384,128]{1,0:T(8,128)S(1)} fusion(bf16[384,16384]{1,0:T(8,128)(2,1)S(1)} %fusion.13, s32[16384]{0:T(1024)S(1)} %get-tuple-element.9), kind=kOutput, calls=%fused_computation.1 | convolution fusion | flops 1612709888 | bytes 12845056 | tf_op jit(solution)/shard_map/dot_general | solution.py:39
  44.8 15.3 %all_to_all.9 = f32[16,1,1024]{2,1,0:T(1,128)S(1)} all-to-all(f32[16,1,1024]{2,1,0:T(1,128)S(1)} %all_to_all.6), channel_id=1, replica_groups=mesh['section'=8,'wafer'=4,'sub'=4] {'wafer','sub'}, dimensions={0} | all-to-all | bytes 131072 | tf_op jit(solution)/shard_map/all_to_all | solution.py:85
  60.2 1.2 %collective-permute-done.5 = f32[1024]{0:T(1024)S(1)} collective-permute-done((f32[1024]{0:T(1024)S(1)}, f32[1024]{0:T(1024)S(1)}, u32[]{:S(2)}, u32[]{:S(2)}) %collective-permute-start.5) | collective-permute-done | bytes 4128 | tf_op jit(solution)/shard_map/ppermute | solution.py:16
  61.4 1.5 %collective-permute-start.6 = (f32[1024]{0:T(1024)S(1)}, f32[1024]{0:T(1024)S(1)}, u32[]{:S(2)}, u32[]{:S(2)}) collective-permute-start(f32[1024]{0:T(1024)S(1)} %add.99), channel_id=1, source_target_pairs={{0,32},{16,48},{32,0},{48,16},{64,96},{80,112},{96,64},{112,80},{1... | collective-permute-start | bytes 12296 | tf_op jit(solution)/shard_map/ppermute | solution.py:16
  62.9 2.1 %collective-permute-done.6 = f32[1024]{0:T(1024)S(1)} collective-permute-done((f32[1024]{0:T(1024)S(1)}, f32[1024]{0:T(1024)S(1)}, u32[]{:S(2)}, u32[]{:S(2)}) %collective-permute-start.6) | collective-permute-done | bytes 4128 | tf_op jit(solution)/shard_map/ppermute | solution.py:16
  65.0 3.0 %collective-permute-start.7 = (f32[1024]{0:T(1024)S(1)}, f32[1024]{0:T(1024)S(1)}, u32[]{:S(2)}, u32[]{:S(2)}) collective-permute-start(f32[1024]{0:T(1024)S(1)} %add.100), channel_id=1, source_target_pairs={{0,64},{16,80},{32,96},{48,112},{64,0},{80,16},{96,32},{112,48},{1... | collective-permute-start | bytes 12296 | tf_op jit(solution)/shard_map/ppermute | solution.py:16
  68.0 2.1 %collective-permute-done.7 = f32[1024]{0:T(1024)S(1)} collective-permute-done((f32[1024]{0:T(1024)S(1)}, f32[1024]{0:T(1024)S(1)}, u32[]{:S(2)}, u32[]{:S(2)}) %collective-permute-start.7) | collective-permute-done | bytes 4128 | tf_op jit(solution)/shard_map/ppermute | solution.py:16
  70.1 0.6 maximum_divide_fusion
  (40 shorter events, 2.3 us)
Async XLA Ops:
  0.0 0.8 %copy-start = (f32[1,64,256]{2,1,0:T(8,128)S(1)}, f32[1,64,256]{2,1,0:T(8,128)}, u32[]{:S(2)}) copy-start(f32[1,64,256]{2,1,0:T(8,128)} %param.7) | copy-start | bytes 196612
  2.1 1.7 %collective-permute-start = (f32[64,128]{0,1:T(8,128)S(1)}, f32[64,128]{0,1:T(8,128)S(1)}, u32[]{:S(2)}, u32[]{:S(2)}) collective-permute-start(f32[64,128]{0,1:T(8,128)S(1)} %pad_maximum_fusion), channel_id=1, source_target_pairs={{0,16},{16,0},{32,48},{48,32},{64,80},{80,64},{96,112},{112,96},{1... | collective-permute-start | bytes 98312 | tf_op jit(solution)/shard_map/ppermute | solution.py:16
  3.9 4.6 %collective-permute-start.1 = (f32[64,128]{0,1:T(8,128)S(1)}, f32[64,128]{0,1:T(8,128)S(1)}, u32[]{:S(2)}, u32[]{:S(2)}) collective-permute-start(f32[64,128]{0,1:T(8,128)S(1)} %fusion.40), channel_id=1, source_target_pairs={{0,32},{16,48},{32,0},{48,16},{64,96},{80,112},{96,64},{112,80},{1... | collective-permute-start | bytes 98312 | tf_op jit(solution)/shard_map/ppermute | solution.py:16
  8.4 5.8 %collective-permute-start.2 = (f32[64,128]{0,1:T(8,128)S(1)}, f32[64,128]{0,1:T(8,128)S(1)}, u32[]{:S(2)}, u32[]{:S(2)}) collective-permute-start(f32[64,128]{0,1:T(8,128)S(1)} %add.87), channel_id=1, source_target_pairs={{0,64},{16,80},{32,96},{48,112},{64,0},{80,16},{96,32},{112,48},{1... | collective-permute-start | bytes 98312 | tf_op jit(solution)/shard_map/ppermute | solution.py:16
  14.3 4.4 %collective-permute-start.3 = (f32[64,128]{0,1:T(8,128)S(1)}, f32[64,128]{0,1:T(8,128)S(1)}, u32[]{:S(2)}, u32[]{:S(2)}) collective-permute-start(f32[64,128]{0,1:T(8,128)S(1)} %add.88), channel_id=1, source_target_pairs={{0,1},{1,0},{2,3},{3,2},{4,5},{5,4},{6,7},{7,6},{8,9},{9,8},{10,11... | collective-permute-start | bytes 98312 | tf_op jit(solution)/shard_map/ppermute | solution.py:16
  18.7 6.3 %collective-permute-start.4 = (f32[64,128]{0,1:T(8,128)S(1)}, f32[64,128]{0,1:T(8,128)S(1)}, u32[]{:S(2)}, u32[]{:S(2)}) collective-permute-start(f32[64,128]{0,1:T(8,128)S(1)} %add.89), channel_id=1, source_target_pairs={{0,2},{1,3},{2,0},{3,1},{4,6},{5,7},{6,4},{7,5},{8,10},{9,11},{10,... | collective-permute-start | bytes 98312 | tf_op jit(solution)/shard_map/ppermute | solution.py:16
  60.2 1.2 %collective-permute-start.5 = (f32[1024]{0:T(1024)S(1)}, f32[1024]{0:T(1024)S(1)}, u32[]{:S(2)}, u32[]{:S(2)}) collective-permute-start(f32[1024]{0:T(1024)S(1)} %reduce_sum.19), channel_id=1, source_target_pairs={{0,16},{16,0},{32,48},{48,32},{64,80},{80,64},{96,112},{112,96},{1... | collective-permute-start | bytes 12296 | tf_op jit(solution)/shard_map/ppermute | solution.py:16
  61.4 3.6 %collective-permute-start.6 = (f32[1024]{0:T(1024)S(1)}, f32[1024]{0:T(1024)S(1)}, u32[]{:S(2)}, u32[]{:S(2)}) collective-permute-start(f32[1024]{0:T(1024)S(1)} %add.99), channel_id=1, source_target_pairs={{0,32},{16,48},{32,0},{48,16},{64,96},{80,112},{96,64},{112,80},{1... | collective-permute-start | bytes 12296 | tf_op jit(solution)/shard_map/ppermute | solution.py:16
  65.0 5.1 %collective-permute-start.7 = (f32[1024]{0:T(1024)S(1)}, f32[1024]{0:T(1024)S(1)}, u32[]{:S(2)}, u32[]{:S(2)}) collective-permute-start(f32[1024]{0:T(1024)S(1)} %add.100), channel_id=1, source_target_pairs={{0,64},{16,80},{32,96},{48,112},{64,0},{80,16},{96,32},{112,48},{1... | collective-permute-start | bytes 12296 | tf_op jit(solution)/shard_map/ppermute | solution.py:16

commit v4 on v3

--- a/solution.py
+++ b/solution.py
@@ -8,13 +8,29 @@
 HIGHEST = lax.Precision.HIGHEST
 
 
+def partner_rounds(axis):
+    size = lax.axis_size(axis)
+    if axis == "section":
+        chips = size // 2
+        yield [(i, i ^ 1) for i in range(size)]
+        inner = 2
+    else:
+        chips = size
+        inner = 1
+    if chips == 4:
+        yield [(i, i ^ inner) for i in range(size)]
+        yield [(i, (3 - i // inner) * inner + i % inner) for i in range(size)]
+    else:
+        bit = inner
+        while bit < size:
+            yield [(i, i ^ bit) for i in range(size)]
+            bit *= 2
+
+
 def all_sum(x, axes):
     for axis in axes:
-        size = lax.axis_size(axis)
-        bit = 1
-        while bit < size:
-            x = x + lax.ppermute(x, axis, [(i, i ^ bit) for i in range(size)])
-            bit *= 2
+        for pairs in partner_rounds(axis):
+            x = x + lax.ppermute(x, axis, pairs)
     return x
 
 

time: 71.1 us -> 70.1 us (0.986)
  starting transfers between devices: 15.8 us -> 14.2 us
  waiting for transfers between devices: 13 us -> 14.1 us
    ppermute x8, starting transfers between devices: 15.8 us -> 14.2 us  [all_sum(): x = x + lax.ppermute(x, axis, pairs)]
    ppermute x8, waiting for transfers between devices: 13 us -> 14.1 us  [all_sum(): x = x + lax.ppermute(x, axis, pairs)]
where the time goes in v4:
time: 70.1 us; the launch traced here: 69.7 us
  other arithmetic  16.8 us (24%)
  blocking collectives  14.7 us (21%)
  starting transfers between devices  14.2 us (20%)
  waiting for transfers between devices  14.1 us (20%)
  matrix products  6.34 us (9%)
  local copies, waits for them, and re-layouts  3.23 us (5%)
    all_to_all x1, blocking collectives, shards(): lax.all_to_all(partial, ('wafer', 'sub'), split_axis=0, concat_axis=0, ti...  14.7 us
    ppermute x8, starting transfers between devices, all_sum(): x = x + lax.ppermute(x, axis, pairs)  14.2 us
    ppermute x8, waiting for transfers between devices, all_sum(): x = x + lax.ppermute(x, axis, pairs)  14.1 us
    another operation x3, other arithmetic, shards(): factor = jnp.linalg.cholesky(gram_sum)  6.52 us
    another operation x2, other arithmetic, shards(): coef_fit = jax.scipy.linalg.cho_solve((factor, True), projection)  5.55 us
    dot_general x1, matrix products, bin_tiles(): lax.dot_general(stacked, lower_hot, (((1,), (1,)), ((), ())), preferred_e...  3.58 us
    unnamed x6, local copies, waits for them, and re-layouts  2.51 us
    unnamed x5, other arithmetic  1.92 us
  transfers between devices with their start and end apart: 8, of which 7 were waited for; matrix products, arithmetic and copies ran while one was open for 6% of the time, Pallas kernels for 0%

profile of v4, /device:TPU:0, one launch (start us, length us, event | category | flops | bytes accessed | tf_op | source)
XLA Modules:
  0.0 69.7 jit_solution(11786430999066432784)
XLA Ops:
  0.0 0.8 %copy-done = f32[1,64,256]{2,1,0:T(8,128)S(1)} copy-done((f32[1,64,256]{2,1,0:T(8,128)S(1)}, f32[1,64,256]{2,1,0:T(8,128)}, u32[]{:S(2)}) %copy-start) | copy-done | bytes 65560
  1.0 1.0 %fusion.26 = f32[64,64]{0,1:T(8,128)S(1)} fusion(f32[1,64,256]{2,1,0:T(8,128)S(1)} %copy-done, f32[1,64,256]{2,1,0:T(8,128)} %param.6), kind=kOutput, calls=%fused_computation.45 | convolution fusion | flops 12582912 | bytes 147456 | tf_op jit(solution)/shard_map/dot_general | solution.py:76
  2.2 0.7 %iota_compare_fusion.6 = pred[16,16]{1,0:T(8,128)(4,1)S(1)} fusion(s32[16]{0:T(128)} %bitcast.42), kind=kLoop, calls=%fused_computation.71 | loop fusion | flops 256 | bytes 320 | tf_op jit(solution)/shard_map/lt | solution.py:93
  2.9 0.8 %fusion.17 = (pred[16,128]{1,0:T(8,128)(4,1)S(1)}, pred[128]{0:T(512)(128)(4,1)S(1)}) fusion(s32[16,16]{1,0:T(8,128)} %bitcast.41, pred[16,16]{1,0:T(8,128)(4,1)S(1)} %iota_compare_fusion.6), kind=kLoop, calls=%fused_computation.21 | loop fusion | flops 128896 | bytes 3456 | tf_op jit(solution)/shard_map/reduce_or | solution.py:95
  3.9 1.7 %collective-permute-start.1 = (f32[64,128]{0,1:T(8,128)S(1)}, f32[64,128]{0,1:T(8,128)S(1)}, u32[]{:S(2)}, u32[]{:S(2)}) collective-permute-start(f32[64,128]{0,1:T(8,128)S(1)} %fusion.40), channel_id=1, source_target_pairs={{0,32},{16,48},{32,0},{48,16},{64,96},{80,112},{96,64},{112,80},{1... | collective-permute-start | bytes 98312 | tf_op jit(solution)/shard_map/ppermute | solution.py:33
  6.0 0.9 %copy.21 = s32[8,2,8,128]{3,1,2,0:T(2,128)S(1)} copy(s32[8,2,8,128]{3,2,1,0:T(8,128)} %bitcast.40) | data formatting | bytes 131072
  6.9 1.5 %collective-permute-done.1 = f32[64,128]{0,1:T(8,128)S(1)} collective-permute-done((f32[64,128]{0,1:T(8,128)S(1)}, f32[64,128]{0,1:T(8,128)S(1)}, u32[]{:S(2)}, u32[]{:S(2)}) %collective-permute-start.1) | collective-permute-done | bytes 32800 | tf_op jit(solution)/shard_map/ppermute | solution.py:33
  8.4 3.0 %collective-permute-start.2 = (f32[64,128]{0,1:T(8,128)S(1)}, f32[64,128]{0,1:T(8,128)S(1)}, u32[]{:S(2)}, u32[]{:S(2)}) collective-permute-start(f32[64,128]{0,1:T(8,128)S(1)} %add.87), channel_id=1, source_target_pairs={{0,96},{16,112},{32,64},{48,80},{64,32},{80,48},{96,0},{112,16},{1... | collective-permute-start | bytes 98312 | tf_op jit(solution)/shard_map/ppermute | solution.py:33
  11.6 2.4 %collective-permute-done.2 = f32[64,128]{0,1:T(8,128)S(1)} collective-permute-done((f32[64,128]{0,1:T(8,128)S(1)}, f32[64,128]{0,1:T(8,128)S(1)}, u32[]{:S(2)}, u32[]{:S(2)}) %collective-permute-start.2) | collective-permute-done | bytes 32800 | tf_op jit(solution)/shard_map/ppermute | solution.py:33
  14.0 2.1 %collective-permute-start.3 = (f32[64,128]{0,1:T(8,128)S(1)}, f32[64,128]{0,1:T(8,128)S(1)}, u32[]{:S(2)}, u32[]{:S(2)}) collective-permute-start(f32[64,128]{0,1:T(8,128)S(1)} %add.88), channel_id=1, source_target_pairs={{0,1},{1,0},{2,3},{3,2},{4,5},{5,4},{6,7},{7,6},{8,9},{9,8},{10,11... | collective-permute-start | bytes 98312 | tf_op jit(solution)/shard_map/ppermute | solution.py:33
  16.1 0.7 %broadcast_bitcast_fusion = f32[8,2,8,128]{3,2,1,0:T(8,128)S(1)} fusion(f32[64]{0:T(128)} %param.8), kind=kLoop, calls=%fused_computation.66 | loop fusion | bytes 65792
  16.9 1.5 %collective-permute-done.3 = f32[64,128]{0,1:T(8,128)S(1)} collective-permute-done((f32[64,128]{0,1:T(8,128)S(1)}, f32[64,128]{0,1:T(8,128)S(1)}, u32[]{:S(2)}, u32[]{:S(2)}) %collective-permute-start.3) | collective-permute-done | bytes 32800 | tf_op jit(solution)/shard_map/ppermute | solution.py:33
  18.4 4.2 %collective-permute-start.4 = (f32[64,128]{0,1:T(8,128)S(1)}, f32[64,128]{0,1:T(8,128)S(1)}, u32[]{:S(2)}, u32[]{:S(2)}) collective-permute-start(f32[64,128]{0,1:T(8,128)S(1)} %add.89), channel_id=1, source_target_pairs={{0,3},{1,2},{2,1},{3,0},{4,7},{5,6},{6,5},{7,4},{8,11},{9,10},{10,... | collective-permute-start | bytes 98312 | tf_op jit(solution)/shard_map/ppermute | solution.py:33
  22.6 2.2 %collective-permute-done.4 = f32[64,128]{0,1:T(8,128)S(1)} collective-permute-done((f32[64,128]{0,1:T(8,128)S(1)}, f32[64,128]{0,1:T(8,128)S(1)}, u32[]{:S(2)}, u32[]{:S(2)}) %collective-permute-start.4) | collective-permute-done | bytes 32800 | tf_op jit(solution)/shard_map/ppermute | solution.py:33
  25.0 5.8 %cholesky.16 = f32[64,64]{1,0:T(8,128)S(1)} custom-call(f32[64,64]{1,0:T(8,128)S(1)} %fusion.39), custom_call_target="Cholesky" | custom-call | tf_op jit(solution)/shard_map/jit(cholesky)/cholesky | solution.py:82
  30.8 0.6 compare_reduce_fusion
  31.5 0.7 fusion.33
  32.1 4.9 %custom-call.10 = f32[1,64,64]{1,2,0:T(8,128)S(1)} custom-call(f32[1,64,64]{2,1,0:T(8,128)S(1)} %fusion.33), custom_call_target="InvertDiagBlocksLowerTriangular" | custom-call | tf_op jit(solution)/shard_map/jit(_cho_solve)/triangular_solve | solution.py:83
  37.5 1.1 %fusion.15 = f32[8,2,8,128]{3,2,1,0:T(8,128)S(1)} fusion(f32[64,64]{1,0:T(8,128)S(1)} %fusion.36, f32[1,64,256]{2,1,0:T(8,128)S(1)} %copy-done, f32[1,64,256]{2,1,0:T(8,128)} %param.6, f32[64]{0:T(128)} %param.8), kind=kOutput, calls=%fused_computation.18 | convolution fusion | flops 12615680 | bytes 213248 | tf_op jit(solution)/shard_map/dot_general | solution.py:84
  38.6 0.4 fusion.8
  39.0 0.4 fusion.9
  39.4 0.4 fusion.10
  39.8 0.4 fusion.11
  40.2 0.4 fusion.12
  40.6 0.4 fusion.13
  41.0 3.6 %fusion = f32[384,128]{1,0:T(8,128)S(1)} fusion(bf16[384,16384]{1,0:T(8,128)(2,1)S(1)} %fusion.13, s32[16384]{0:T(1024)S(1)} %get-tuple-element.9), kind=kOutput, calls=%fused_computation.1 | convolution fusion | flops 1612709888 | bytes 12845056 | tf_op jit(solution)/shard_map/dot_general | solution.py:55
  44.7 14.7 %all_to_all.9 = f32[16,1,1024]{2,1,0:T(1,128)S(1)} all-to-all(f32[16,1,1024]{2,1,0:T(1,128)S(1)} %all_to_all.6), channel_id=1, replica_groups=mesh['section'=8,'wafer'=4,'sub'=4] {'wafer','sub'}, dimensions={0} | all-to-all | bytes 131072 | tf_op jit(solution)/shard_map/all_to_all | solution.py:101
  59.6 1.2 %collective-permute-done.5 = f32[1024]{0:T(1024)S(1)} collective-permute-done((f32[1024]{0:T(1024)S(1)}, f32[1024]{0:T(1024)S(1)}, u32[]{:S(2)}, u32[]{:S(2)}) %collective-permute-start.5) | collective-permute-done | bytes 4128 | tf_op jit(solution)/shard_map/ppermute | solution.py:33
  61.0 3.3 %collective-permute-done.6 = f32[1024]{0:T(1024)S(1)} collective-permute-done((f32[1024]{0:T(1024)S(1)}, f32[1024]{0:T(1024)S(1)}, u32[]{:S(2)}, u32[]{:S(2)}) %collective-permute-start.6) | collective-permute-done | bytes 4128 | tf_op jit(solution)/shard_map/ppermute | solution.py:33
  64.3 2.8 %collective-permute-start.7 = (f32[1024]{0:T(1024)S(1)}, f32[1024]{0:T(1024)S(1)}, u32[]{:S(2)}, u32[]{:S(2)}) collective-permute-start(f32[1024]{0:T(1024)S(1)} %add.100), channel_id=1, source_target_pairs={{0,96},{16,112},{32,64},{48,80},{64,32},{80,48},{96,0},{112,16},{1... | collective-permute-start | bytes 12296 | tf_op jit(solution)/shard_map/ppermute | solution.py:33
  67.1 2.1 %collective-permute-done.7 = f32[1024]{0:T(1024)S(1)} collective-permute-done((f32[1024]{0:T(1024)S(1)}, f32[1024]{0:T(1024)S(1)}, u32[]{:S(2)}, u32[]{:S(2)}) %collective-permute-start.7) | collective-permute-done | bytes 4128 | tf_op jit(solution)/shard_map/ppermute | solution.py:33
  69.2 0.6 maximum_divide_fusion
  (40 shorter events, 2.2 us)
Async XLA Ops:
  0.0 0.8 %copy-start = (f32[1,64,256]{2,1,0:T(8,128)S(1)}, f32[1,64,256]{2,1,0:T(8,128)}, u32[]{:S(2)}) copy-start(f32[1,64,256]{2,1,0:T(8,128)} %param.7) | copy-start | bytes 196612
  2.1 1.7 %collective-permute-start = (f32[64,128]{0,1:T(8,128)S(1)}, f32[64,128]{0,1:T(8,128)S(1)}, u32[]{:S(2)}, u32[]{:S(2)}) collective-permute-start(f32[64,128]{0,1:T(8,128)S(1)} %pad_maximum_fusion), channel_id=1, source_target_pairs={{0,16},{16,0},{32,48},{48,32},{64,80},{80,64},{96,112},{112,96},{1... | collective-permute-start | bytes 98312 | tf_op jit(solution)/shard_map/ppermute | solution.py:33
  3.9 4.6 %collective-permute-start.1 = (f32[64,128]{0,1:T(8,128)S(1)}, f32[64,128]{0,1:T(8,128)S(1)}, u32[]{:S(2)}, u32[]{:S(2)}) collective-permute-start(f32[64,128]{0,1:T(8,128)S(1)} %fusion.40), channel_id=1, source_target_pairs={{0,32},{16,48},{32,0},{48,16},{64,96},{80,112},{96,64},{112,80},{1... | collective-permute-start | bytes 98312 | tf_op jit(solution)/shard_map/ppermute | solution.py:33
  8.4 5.6 %collective-permute-start.2 = (f32[64,128]{0,1:T(8,128)S(1)}, f32[64,128]{0,1:T(8,128)S(1)}, u32[]{:S(2)}, u32[]{:S(2)}) collective-permute-start(f32[64,128]{0,1:T(8,128)S(1)} %add.87), channel_id=1, source_target_pairs={{0,96},{16,112},{32,64},{48,80},{64,32},{80,48},{96,0},{112,16},{1... | collective-permute-start | bytes 98312 | tf_op jit(solution)/shard_map/ppermute | solution.py:33
  14.0 4.4 %collective-permute-start.3 = (f32[64,128]{0,1:T(8,128)S(1)}, f32[64,128]{0,1:T(8,128)S(1)}, u32[]{:S(2)}, u32[]{:S(2)}) collective-permute-start(f32[64,128]{0,1:T(8,128)S(1)} %add.88), channel_id=1, source_target_pairs={{0,1},{1,0},{2,3},{3,2},{4,5},{5,4},{6,7},{7,6},{8,9},{9,8},{10,11... | collective-permute-start | bytes 98312 | tf_op jit(solution)/shard_map/ppermute | solution.py:33
  18.4 6.5 %collective-permute-start.4 = (f32[64,128]{0,1:T(8,128)S(1)}, f32[64,128]{0,1:T(8,128)S(1)}, u32[]{:S(2)}, u32[]{:S(2)}) collective-permute-start(f32[64,128]{0,1:T(8,128)S(1)} %add.89), channel_id=1, source_target_pairs={{0,3},{1,2},{2,1},{3,0},{4,7},{5,6},{6,5},{7,4},{8,11},{9,10},{10,... | collective-permute-start | bytes 98312 | tf_op jit(solution)/shard_map/ppermute | solution.py:33
  59.5 1.2 %collective-permute-start.5 = (f32[1024]{0:T(1024)S(1)}, f32[1024]{0:T(1024)S(1)}, u32[]{:S(2)}, u32[]{:S(2)}) collective-permute-start(f32[1024]{0:T(1024)S(1)} %reduce_sum.19), channel_id=1, source_target_pairs={{0,16},{16,0},{32,48},{48,32},{64,80},{80,64},{96,112},{112,96},{1... | collective-permute-start | bytes 12296 | tf_op jit(solution)/shard_map/ppermute | solution.py:33
  60.7 3.6 %collective-permute-start.6 = (f32[1024]{0:T(1024)S(1)}, f32[1024]{0:T(1024)S(1)}, u32[]{:S(2)}, u32[]{:S(2)}) collective-permute-start(f32[1024]{0:T(1024)S(1)} %add.99), channel_id=1, source_target_pairs={{0,32},{16,48},{32,0},{48,16},{64,96},{80,112},{96,64},{112,80},{1... | collective-permute-start | bytes 12296 | tf_op jit(solution)/shard_map/ppermute | solution.py:33
  64.3 4.8 %collective-permute-start.7 = (f32[1024]{0:T(1024)S(1)}, f32[1024]{0:T(1024)S(1)}, u32[]{:S(2)}, u32[]{:S(2)}) collective-permute-start(f32[1024]{0:T(1024)S(1)} %add.100), channel_id=1, source_target_pairs={{0,96},{16,112},{32,64},{48,80},{64,32},{80,48},{96,0},{112,16},{1... | collective-permute-start | bytes 12296 | tf_op jit(solution)/shard_map/ppermute | solution.py:33

commit v5 on v4

--- a/solution.py
+++ b/solution.py
@@ -1,6 +1,8 @@
 import jax
 import jax.numpy as jnp
 from jax import lax
+from jax.experimental import pallas as pl
+from jax.experimental.pallas import tpu as pltpu
 from jax.sharding import PartitionSpec as P
 
 BL = 128
@@ -60,6 +62,31 @@
     return jnp.concatenate([num, wgt], axis=1)
 
 
+def solve_kernel(joined_ref, coef_ref):
+    n = joined_ref.shape[0]
+    m = joined_ref[...]
+    rows = lax.broadcasted_iota(jnp.int32, m.shape, 0)
+    for k in range(n):
+        row = m[k : k + 1, :]
+        inv_root = 1.0 / jnp.sqrt(row[:, k : k + 1])
+        scaled = row * inv_root
+        column = m[:, k : k + 1] * inv_root
+        m = jnp.where(rows == k, scaled, m - column * scaled)
+    lanes = lax.broadcasted_iota(jnp.int32, (n, n), 1)
+    diag = jnp.sum(jnp.where(lanes == rows[:, :n], m[:, :n], 0.0), axis=1, keepdims=True)
+    coef_ref[...] = m[:, n:] / diag
+
+
+def solve_fit(joined):
+    n = joined.shape[0]
+    return pl.pallas_call(
+        solve_kernel,
+        out_shape=jax.ShapeDtypeStruct((n, joined.shape[1] - n), jnp.float32),
+        in_specs=[pl.BlockSpec(memory_space=pltpu.VMEM)],
+        out_specs=pl.BlockSpec(memory_space=pltpu.VMEM),
+    )(joined)
+
+
 def shards(tod, templates, det_weight, pixel, hitlist, counts):
     dets, samp_local = tod.shape[1], tod.shape[2]
     owners = hitlist.shape[1]
@@ -78,9 +105,7 @@
         precision=HIGHEST, preferred_element_type=jnp.float32,
     )
     joined = all_sum(jnp.concatenate([gram_sum, projection], axis=1), ("section", "sub"))
-    gram_sum, projection = joined[:, : gram_sum.shape[1]], joined[:, gram_sum.shape[1] :]
-    factor = jnp.linalg.cholesky(gram_sum)
-    coef_fit = jax.scipy.linalg.cho_solve((factor, True), projection)
+    coef_fit = solve_fit(joined)
     removed = lax.dot_general(
         coef_fit, template_rows, (((0,), (0,)), ((), ())),
         precision=HIGHEST, preferred_element_type=jnp.float32,

time: 70.1 us -> 64.1 us (0.914)
  other arithmetic: 16.8 us -> 5.5 us
  Pallas kernels: 0 us -> 7.82 us
  waiting for transfers between devices: 14.1 us -> 12.5 us
    another operation x5 -> x0, other arithmetic: 12.1 us -> none  [the longest x3 6.52 us: shards(): factor = jnp.linalg.cholesky(gram_sum)]
    pallas_call x0 -> x1, Pallas kernels: none -> 7.82 us  [solve_fit(): pl.pallas_call(solve_kernel, out_shape=jax.ShapeDtypeStruct((n, joined.sh...]
    ppermute x8, waiting for transfers between devices: 14.1 us -> 12.5 us  [all_sum(): x = x + lax.ppermute(x, axis, pairs)]
where the time goes in v5:
time: 64.1 us; the launch traced here: 63.7 us
  blocking collectives  14.7 us (23%)
  starting transfers between devices  13.8 us (22%)
  waiting for transfers between devices  12.5 us (20%)
  Pallas kernels  7.82 us (12%)
  matrix products  5.92 us (9%)
  other arithmetic  5.5 us (9%)
  local copies, waits for them, and re-layouts  3.15 us (5%)
    all_to_all x1, blocking collectives, shards(): lax.all_to_all(partial, ('wafer', 'sub'), split_axis=0, concat_axis=0, ti...  14.7 us
    ppermute x8, starting transfers between devices, all_sum(): x = x + lax.ppermute(x, axis, pairs)  13.8 us
    ppermute x8, waiting for transfers between devices, all_sum(): x = x + lax.ppermute(x, axis, pairs)  12.5 us
    pallas_call x1, Pallas kernels, solve_fit(): pl.pallas_call(solve_kernel, out_shape=jax.ShapeDtypeStruct((n, joined.sh...  7.82 us
    dot_general x1, matrix products, bin_tiles(): lax.dot_general(stacked, lower_hot, (((1,), (1,)), ((), ())), preferred_e...  3.59 us
    unnamed x6, local copies, waits for them, and re-layouts  2.51 us
    unnamed x5, other arithmetic  1.93 us
  transfers between devices with their start and end apart: 8, of which 7 were waited for; matrix products, arithmetic and copies ran while one was open for 6% of the time, Pallas kernels for 0%

profile of v5, /device:TPU:0, one launch (start us, length us, event | category | flops | bytes accessed | tf_op | source)
XLA Modules:
  0.0 63.7 jit_solution(4040071968063749024)
XLA Ops:
  0.0 0.8 %copy-done = f32[1,64,256]{2,1,0:T(8,128)S(1)} copy-done((f32[1,64,256]{2,1,0:T(8,128)S(1)}, f32[1,64,256]{2,1,0:T(8,128)}, u32[]{:S(2)}) %copy-start) | copy-done | bytes 65560
  0.8 0.2 fusion.28
  1.0 1.0 %fusion.26 = f32[64,64]{1,0:T(8,128)S(1)} fusion(f32[1,64,256]{2,1,0:T(8,128)S(1)} %copy-done, f32[1,64,256]{2,1,0:T(8,128)} %param.6), kind=kOutput, calls=%fused_computation.44 | convolution fusion | flops 12582912 | bytes 147456 | tf_op jit(solution)/shard_map/dot_general | solution.py:103
  2.2 0.7 %iota_compare_fusion.4 = pred[16,16]{1,0:T(8,128)(4,1)S(1)} fusion(s32[16]{0:T(128)} %bitcast.30), kind=kLoop, calls=%fused_computation.59 | loop fusion | flops 256 | bytes 320 | tf_op jit(solution)/shard_map/lt | solution.py:118
  2.9 0.8 %fusion.17 = (pred[16,128]{1,0:T(8,128)(4,1)S(1)}, pred[128]{0:T(512)(128)(4,1)S(1)}) fusion(s32[16,16]{1,0:T(8,128)} %bitcast.29, pred[16,16]{1,0:T(8,128)(4,1)S(1)} %iota_compare_fusion.4), kind=kLoop, calls=%fused_computation.21 | loop fusion | flops 128896 | bytes 3456 | tf_op jit(solution)/shard_map/reduce_or | solution.py:120
  3.9 1.6 %collective-permute-start.1 = (f32[64,128]{1,0:T(8,128)S(1)}, f32[64,128]{1,0:T(8,128)S(1)}, u32[]{:S(2)}, u32[]{:S(2)}) collective-permute-start(f32[64,128]{1,0:T(8,128)S(1)} %fusion.35), channel_id=1, source_target_pairs={{0,32},{16,48},{32,0},{48,16},{64,96},{80,112},{96,64},{112,80},{1... | collective-permute-start | bytes 98312 | tf_op jit(solution)/shard_map/ppermute | solution.py:35
  6.0 0.9 %copy.7 = s32[8,2,8,128]{3,1,2,0:T(2,128)S(1)} copy(s32[8,2,8,128]{3,2,1,0:T(8,128)} %bitcast.28) | data formatting | bytes 131072
  6.9 0.9 %collective-permute-done.1 = f32[64,128]{1,0:T(8,128)S(1)} collective-permute-done((f32[64,128]{1,0:T(8,128)S(1)}, f32[64,128]{1,0:T(8,128)S(1)}, u32[]{:S(2)}, u32[]{:S(2)}) %collective-permute-start.1) | collective-permute-done | bytes 32800 | tf_op jit(solution)/shard_map/ppermute | solution.py:35
  7.9 2.9 %collective-permute-start.2 = (f32[64,128]{1,0:T(8,128)S(1)}, f32[64,128]{1,0:T(8,128)S(1)}, u32[]{:S(2)}, u32[]{:S(2)}) collective-permute-start(f32[64,128]{1,0:T(8,128)S(1)} %add.72), channel_id=1, source_target_pairs={{0,96},{16,112},{32,64},{48,80},{64,32},{80,48},{96,0},{112,16},{1... | collective-permute-start | bytes 98312 | tf_op jit(solution)/shard_map/ppermute | solution.py:35
  10.9 2.0 %collective-permute-done.2 = f32[64,128]{1,0:T(8,128)S(1)} collective-permute-done((f32[64,128]{1,0:T(8,128)S(1)}, f32[64,128]{1,0:T(8,128)S(1)}, u32[]{:S(2)}, u32[]{:S(2)}) %collective-permute-start.2) | collective-permute-done | bytes 32800 | tf_op jit(solution)/shard_map/ppermute | solution.py:35
  13.0 2.0 %collective-permute-start.3 = (f32[64,128]{1,0:T(8,128)S(1)}, f32[64,128]{1,0:T(8,128)S(1)}, u32[]{:S(2)}, u32[]{:S(2)}) collective-permute-start(f32[64,128]{1,0:T(8,128)S(1)} %add.73), channel_id=1, source_target_pairs={{0,1},{1,0},{2,3},{3,2},{4,5},{5,4},{6,7},{7,6},{8,9},{9,8},{10,11... | collective-permute-start | bytes 98312 | tf_op jit(solution)/shard_map/ppermute | solution.py:35
  15.0 0.7 %broadcast_bitcast_fusion = f32[8,2,8,128]{3,2,1,0:T(8,128)S(1)} fusion(f32[64]{0:T(128)} %param.8), kind=kLoop, calls=%fused_computation.57 | loop fusion | bytes 65792
  15.8 1.1 %collective-permute-done.3 = f32[64,128]{1,0:T(8,128)S(1)} collective-permute-done((f32[64,128]{1,0:T(8,128)S(1)}, f32[64,128]{1,0:T(8,128)S(1)}, u32[]{:S(2)}, u32[]{:S(2)}) %collective-permute-start.3) | collective-permute-done | bytes 32800 | tf_op jit(solution)/shard_map/ppermute | solution.py:35
  16.9 4.1 %collective-permute-start.4 = (f32[64,128]{1,0:T(8,128)S(1)}, f32[64,128]{1,0:T(8,128)S(1)}, u32[]{:S(2)}, u32[]{:S(2)}) collective-permute-start(f32[64,128]{1,0:T(8,128)S(1)} %add.74), channel_id=1, source_target_pairs={{0,3},{1,2},{2,1},{3,0},{4,7},{5,6},{6,5},{7,4},{8,11},{9,10},{10,... | collective-permute-start | bytes 98312 | tf_op jit(solution)/shard_map/ppermute | solution.py:35
  21.1 1.9 %collective-permute-done.4 = f32[64,128]{1,0:T(8,128)S(1)} collective-permute-done((f32[64,128]{1,0:T(8,128)S(1)}, f32[64,128]{1,0:T(8,128)S(1)}, u32[]{:S(2)}, u32[]{:S(2)}) %collective-permute-start.4) | collective-permute-done | bytes 32800 | tf_op jit(solution)/shard_map/ppermute | solution.py:35
  23.0 0.6 add.75.joined_ref
  23.6 7.8 %shard_map.64 = f32[64,64]{1,0:T(8,128)} custom-call(f32[64,128]{1,0:T(8,128)} %add.75.joined_ref), custom_call_target="tpu_custom_call" | custom-call | tf_op jit(solution)/shard_map/pallas_call | solution.py:82
  31.4 1.1 %fusion.15 = f32[8,2,8,128]{3,2,1,0:T(8,128)S(1)} fusion(f32[64,64]{1,0:T(8,128)} %shard_map.64, f32[1,64,256]{2,1,0:T(8,128)S(1)} %copy-done, f32[1,64,256]{2,1,0:T(8,128)} %param.6, f32[64]{0:T(128)} %param.8), kind=kOutput, calls=%fused_computation.18 | convolution fusion | flops 12615680 | bytes 213248 | tf_op jit(solution)/shard_map/dot_general | solution.py:109
  32.6 0.4 fusion.8
  32.9 0.4 fusion.9
  33.3 0.4 fusion.10
  33.7 0.4 fusion.11
  34.1 0.4 fusion.12
  34.5 0.4 fusion.13
  34.9 3.6 %fusion = f32[384,128]{1,0:T(8,128)S(1)} fusion(bf16[384,16384]{1,0:T(8,128)(2,1)S(1)} %fusion.13, s32[16384]{0:T(1024)S(1)} %get-tuple-element.9), kind=kOutput, calls=%fused_computation.1 | convolution fusion | flops 1612709888 | bytes 12845056 | tf_op jit(solution)/shard_map/dot_general | solution.py:57
  38.6 14.7 %all_to_all.9 = f32[16,1,1024]{2,1,0:T(1,128)S(1)} all-to-all(f32[16,1,1024]{2,1,0:T(1,128)S(1)} %all_to_all.6), channel_id=1, replica_groups=mesh['section'=8,'wafer'=4,'sub'=4] {'wafer','sub'}, dimensions={0} | all-to-all | bytes 131072 | tf_op jit(solution)/shard_map/all_to_all | solution.py:126
  53.5 1.2 %collective-permute-done.5 = f32[1024]{0:T(1024)S(1)} collective-permute-done((f32[1024]{0:T(1024)S(1)}, f32[1024]{0:T(1024)S(1)}, u32[]{:S(2)}, u32[]{:S(2)}) %collective-permute-start.5) | collective-permute-done | bytes 4128 | tf_op jit(solution)/shard_map/ppermute | solution.py:35
  54.7 0.3 collective-permute-start.6
  54.9 3.3 %collective-permute-done.6 = f32[1024]{0:T(1024)S(1)} collective-permute-done((f32[1024]{0:T(1024)S(1)}, f32[1024]{0:T(1024)S(1)}, u32[]{:S(2)}, u32[]{:S(2)}) %collective-permute-start.6) | collective-permute-done | bytes 4128 | tf_op jit(solution)/shard_map/ppermute | solution.py:35
  58.3 2.8 %collective-permute-start.7 = (f32[1024]{0:T(1024)S(1)}, f32[1024]{0:T(1024)S(1)}, u32[]{:S(2)}, u32[]{:S(2)}) collective-permute-start(f32[1024]{0:T(1024)S(1)} %add.84), channel_id=1, source_target_pairs={{0,96},{16,112},{32,64},{48,80},{64,32},{80,48},{96,0},{112,16},{1... | collective-permute-start | bytes 12296 | tf_op jit(solution)/shard_map/ppermute | solution.py:35
  61.0 2.1 %collective-permute-done.7 = f32[1024]{0:T(1024)S(1)} collective-permute-done((f32[1024]{0:T(1024)S(1)}, f32[1024]{0:T(1024)S(1)}, u32[]{:S(2)}, u32[]{:S(2)}) %collective-permute-start.7) | collective-permute-done | bytes 4128 | tf_op jit(solution)/shard_map/ppermute | solution.py:35
  63.1 0.6 maximum_divide_fusion
  (31 shorter events, 1.2 us)
Async XLA Ops:
  0.0 0.8 %copy-start = (f32[1,64,256]{2,1,0:T(8,128)S(1)}, f32[1,64,256]{2,1,0:T(8,128)}, u32[]{:S(2)}) copy-start(f32[1,64,256]{2,1,0:T(8,128)} %param.7) | copy-start | bytes 196612
  2.2 1.7 %collective-permute-start = (f32[64,128]{1,0:T(8,128)S(1)}, f32[64,128]{1,0:T(8,128)S(1)}, u32[]{:S(2)}, u32[]{:S(2)}) collective-permute-start(f32[64,128]{1,0:T(8,128)S(1)} %pad_maximum_fusion.1), channel_id=1, source_target_pairs={{0,16},{16,0},{32,48},{48,32},{64,80},{80,64},{96,112},{112,96},{1... | collective-permute-start | bytes 98312 | tf_op jit(solution)/shard_map/ppermute | solution.py:35
  3.9 3.9 %collective-permute-start.1 = (f32[64,128]{1,0:T(8,128)S(1)}, f32[64,128]{1,0:T(8,128)S(1)}, u32[]{:S(2)}, u32[]{:S(2)}) collective-permute-start(f32[64,128]{1,0:T(8,128)S(1)} %fusion.35), channel_id=1, source_target_pairs={{0,32},{16,48},{32,0},{48,16},{64,96},{80,112},{96,64},{112,80},{1... | collective-permute-start | bytes 98312 | tf_op jit(solution)/shard_map/ppermute | solution.py:35
  7.9 5.1 %collective-permute-start.2 = (f32[64,128]{1,0:T(8,128)S(1)}, f32[64,128]{1,0:T(8,128)S(1)}, u32[]{:S(2)}, u32[]{:S(2)}) collective-permute-start(f32[64,128]{1,0:T(8,128)S(1)} %add.72), channel_id=1, source_target_pairs={{0,96},{16,112},{32,64},{48,80},{64,32},{80,48},{96,0},{112,16},{1... | collective-permute-start | bytes 98312 | tf_op jit(solution)/shard_map/ppermute | solution.py:35
  13.0 3.9 %collective-permute-start.3 = (f32[64,128]{1,0:T(8,128)S(1)}, f32[64,128]{1,0:T(8,128)S(1)}, u32[]{:S(2)}, u32[]{:S(2)}) collective-permute-start(f32[64,128]{1,0:T(8,128)S(1)} %add.73), channel_id=1, source_target_pairs={{0,1},{1,0},{2,3},{3,2},{4,5},{5,4},{6,7},{7,6},{8,9},{9,8},{10,11... | collective-permute-start | bytes 98312 | tf_op jit(solution)/shard_map/ppermute | solution.py:35
  16.9 6.0 %collective-permute-start.4 = (f32[64,128]{1,0:T(8,128)S(1)}, f32[64,128]{1,0:T(8,128)S(1)}, u32[]{:S(2)}, u32[]{:S(2)}) collective-permute-start(f32[64,128]{1,0:T(8,128)S(1)} %add.74), channel_id=1, source_target_pairs={{0,3},{1,2},{2,1},{3,0},{4,7},{5,6},{6,5},{7,4},{8,11},{9,10},{10,... | collective-permute-start | bytes 98312 | tf_op jit(solution)/shard_map/ppermute | solution.py:35
  53.4 1.2 %collective-permute-start.5 = (f32[1024]{0:T(1024)S(1)}, f32[1024]{0:T(1024)S(1)}, u32[]{:S(2)}, u32[]{:S(2)}) collective-permute-start(f32[1024]{0:T(1024)S(1)} %reduce_sum.19), channel_id=1, source_target_pairs={{0,16},{16,0},{32,48},{48,32},{64,80},{80,64},{96,112},{112,96},{1... | collective-permute-start | bytes 12296 | tf_op jit(solution)/shard_map/ppermute | solution.py:35
  54.7 3.6 %collective-permute-start.6 = (f32[1024]{0:T(1024)S(1)}, f32[1024]{0:T(1024)S(1)}, u32[]{:S(2)}, u32[]{:S(2)}) collective-permute-start(f32[1024]{0:T(1024)S(1)} %add.83), channel_id=1, source_target_pairs={{0,32},{16,48},{32,0},{48,16},{64,96},{80,112},{96,64},{112,80},{1... | collective-permute-start | bytes 12296 | tf_op jit(solution)/shard_map/ppermute | solution.py:35
  58.3 4.8 %collective-permute-start.7 = (f32[1024]{0:T(1024)S(1)}, f32[1024]{0:T(1024)S(1)}, u32[]{:S(2)}, u32[]{:S(2)}) collective-permute-start(f32[1024]{0:T(1024)S(1)} %add.84), channel_id=1, source_target_pairs={{0,96},{16,112},{32,64},{48,80},{64,32},{80,48},{96,0},{112,16},{1... | collective-permute-start | bytes 12296 | tf_op jit(solution)/shard_map/ppermute | solution.py:35

commit v6 on v5

--- a/solution.py
+++ b/solution.py
@@ -29,11 +29,14 @@
             bit *= 2
 
 
-def all_sum(x, axes):
-    for axis in axes:
-        for pairs in partner_rounds(axis):
-            x = x + lax.ppermute(x, axis, pairs)
-    return x
+def all_sum(x, axes, cover=None, cover_round=0):
+    rounds = [(axis, pairs) for axis in axes for pairs in partner_rounds(axis)]
+    covered = None
+    for index, (axis, pairs) in enumerate(rounds):
+        if cover is not None and index == cover_round:
+            x, covered = lax.optimization_barrier((x, cover()))
+        x = x + lax.ppermute(x, axis, pairs)
+    return x, covered
 
 
 def split_bf16(x, parts):
@@ -45,21 +48,13 @@
     return pieces
 
 
-def bin_tiles(values, pixels, weights, tile_of_sample, owners):
-    uppers = owners * (TILE // 128)
-    upper = jnp.where(tile_of_sample >= 0, tile_of_sample * (TILE // 128) + pixels // 128, -1).reshape(-1)
-    lower = (pixels % 128).reshape(-1)
-    count = upper.shape[0]
-    upper_hot = lax.broadcasted_iota(jnp.int32, (uppers, count), 0) == upper[None, :]
-    lower_hot = (lax.broadcasted_iota(jnp.int32, (128, count), 0) == lower[None, :]).astype(jnp.bfloat16)
-    pieces = split_bf16(values.reshape(1, -1), 3) + split_bf16(weights.reshape(1, -1), 3)
+def bin_tiles(quantity, upper_hot, lower_hot, owners):
+    pieces = split_bf16(quantity.reshape(1, -1), 3)
     stacked = jnp.concatenate([jnp.where(upper_hot, p, jnp.bfloat16(0)) for p in pieces], axis=0)
     binned = lax.dot_general(
         stacked, lower_hot, (((1,), (1,)), ((), ())), preferred_element_type=jnp.float32,
-    ).reshape(6, uppers, 128)
-    num = ((binned[0] + binned[1]) + binned[2]).reshape(owners, TILE)
-    wgt = ((binned[3] + binned[4]) + binned[5]).reshape(owners, TILE)
-    return jnp.concatenate([num, wgt], axis=1)
+    ).reshape(3, upper_hot.shape[0], 128)
+    return ((binned[0] + binned[1]) + binned[2]).reshape(owners, TILE)
 
 
 def solve_kernel(joined_ref, coef_ref):
@@ -94,6 +89,20 @@
     per_det = samp_local // BL
     blocks = dets * per_det
 
+    slot_ids = lax.broadcasted_iota(jnp.int32, (owners, slots), 1)
+    live = slot_ids < counts[0]
+    named = (hitlist[0][:, :, None] == lax.broadcasted_iota(jnp.int32, (1, 1, blocks), 2)) & live[:, :, None]
+    in_tile = jnp.any(named, axis=1)
+    tile_ids = lax.broadcasted_iota(jnp.int32, (owners, blocks), 0)
+    tile_of_block = jnp.where(jnp.any(in_tile, axis=0), jnp.sum(jnp.where(in_tile, tile_ids, 0), axis=0), -1)
+    tile_of_sample = jnp.repeat(tile_of_block.reshape(dets, per_det), BL, axis=1)
+
+    uppers = owners * (TILE // 128)
+    upper = jnp.where(tile_of_sample >= 0, tile_of_sample * (TILE // 128) + pixel[0] // 128, -1).reshape(1, -1)
+    lower = (pixel[0] % 128).reshape(1, -1)
+    upper_hot = lax.broadcasted_iota(jnp.int32, (uppers, upper.shape[1]), 0) == upper
+    lower_hot = (lax.broadcasted_iota(jnp.int32, (128, upper.shape[1]), 0) == lower).astype(jnp.bfloat16)
+    sample_weight = jnp.broadcast_to(det_weight[:, None], tod.shape[1:])
     template_rows = templates[0]
     streams = tod[0]
     gram_sum = lax.dot_general(
@@ -104,7 +113,10 @@
         template_rows, streams, (((1,), (1,)), ((), ())),
         precision=HIGHEST, preferred_element_type=jnp.float32,
     )
-    joined = all_sum(jnp.concatenate([gram_sum, projection], axis=1), ("section", "sub"))
+    joined, wgt_part = all_sum(
+        jnp.concatenate([gram_sum, projection], axis=1), ("section", "sub"),
+        cover=lambda: bin_tiles(sample_weight, upper_hot, lower_hot, owners), cover_round=4,
+    )
     coef_fit = solve_fit(joined)
     removed = lax.dot_general(
         coef_fit, template_rows, (((0,), (0,)), ((), ())),
@@ -112,19 +124,11 @@
     )
     filtered = streams - removed
     weighted = filtered * det_weight[:, None]
-    sample_weight = jnp.broadcast_to(det_weight[:, None], streams.shape)
 
-    slot_ids = lax.broadcasted_iota(jnp.int32, (owners, slots), 1)
-    live = slot_ids < counts[0]
-    named = (hitlist[0][:, :, None] == lax.broadcasted_iota(jnp.int32, (1, 1, blocks), 2)) & live[:, :, None]
-    in_tile = jnp.any(named, axis=1)
-    tile_ids = lax.broadcasted_iota(jnp.int32, (owners, blocks), 0)
-    tile_of_block = jnp.where(jnp.any(in_tile, axis=0), jnp.sum(jnp.where(in_tile, tile_ids, 0), axis=0), -1)
-    tile_of_sample = jnp.repeat(tile_of_block.reshape(dets, per_det), BL, axis=1)
-
-    partial = bin_tiles(weighted, pixel[0], sample_weight, tile_of_sample, owners)
+    num_part = bin_tiles(weighted, upper_hot, lower_hot, owners)
+    partial = jnp.concatenate([num_part, wgt_part], axis=1)
     got = lax.all_to_all(partial, ("wafer", "sub"), split_axis=0, concat_axis=0, tiled=True)
-    tile_sum = all_sum(jnp.sum(got, axis=0), ("section",))
+    tile_sum, _ = all_sum(jnp.sum(got, axis=0), ("section",))
     num_tile, wgt_tile = tile_sum[:TILE], tile_sum[TILE:]
     return num_tile / jnp.maximum(wgt_tile, 1.0)
 

time: 64.1 us -> 63.5 us (level)
  waiting for transfers between devices: 12.5 us -> 11.8 us
    select_n x1 -> x3, other arithmetic: 0.07 us -> 2.26 us  [the longest x2 2.19 us: bin_tiles(): jnp.where(upper_hot, p, jnp.bfloat16(0))]
    unnamed x5 -> x0, other arithmetic: 1.93 us -> none
    ppermute x8, waiting for transfers between devices: 12.5 us -> 11.8 us  [all_sum(): x = x + lax.ppermute(x, axis, pairs)]
    dot_general x1 -> x2, matrix products: 3.59 us -> 3.88 us  [bin_tiles(): lax.dot_general(stacked, lower_hot, (((1,), (1,)), ((), ())), preferred_e...]
    unnamed x6 -> x10, local copies, waits for them, and re-layouts: 2.51 us -> 2.53 us
  transfers between devices with their start and end apart: 8 -> 8, of which waited for: 7 -> 7; matrix products, arithmetic and copies ran while one was open for 6% -> 11% of each run, Pallas kernels for 0% -> 0%
where the time goes in v6:
time: 63.5 us; the launch traced here: 63 us
  blocking collectives  14.7 us (23%)
  starting transfers between devices  13.8 us (22%)
  waiting for transfers between devices  11.8 us (19%)
  Pallas kernels  7.81 us (12%)
  matrix products  6.13 us (10%)
  other arithmetic  5.37 us (8%)
  local copies, waits for them, and re-layouts  3.17 us (5%)
    all_to_all x1, blocking collectives, shards(): lax.all_to_all(partial, ('wafer', 'sub'), split_axis=0, concat_axis=0, ti...  14.7 us
    ppermute x8, starting transfers between devices, all_sum(): x = x + lax.ppermute(x, axis, pairs)  13.8 us
    ppermute x8, waiting for transfers between devices, all_sum(): x = x + lax.ppermute(x, axis, pairs)  11.8 us
    pallas_call x1, Pallas kernels, solve_fit(): pl.pallas_call(solve_kernel, out_shape=jax.ShapeDtypeStruct((n, joined.sh...  7.81 us
    dot_general x2, matrix products, bin_tiles(): lax.dot_general(stacked, lower_hot, (((1,), (1,)), ((), ())), preferred_e...  3.88 us
    unnamed x10, local copies, waits for them, and re-layouts  2.53 us
    select_n x2, other arithmetic, bin_tiles(): jnp.where(upper_hot, p, jnp.bfloat16(0))  2.19 us
  transfers between devices with their start and end apart: 8, of which 7 were waited for; matrix products, arithmetic and copies ran while one was open for 11% of the time, Pallas kernels for 0%

profile of v6, /device:TPU:0, one launch (start us, length us, event | category | flops | bytes accessed | tf_op | source)
XLA Modules:
  0.0 63.0 jit_solution(11653537719305788957)
XLA Ops:
  0.0 0.8 %copy-done = f32[1,64,256]{2,1,0:T(8,128)S(1)} copy-done((f32[1,64,256]{2,1,0:T(8,128)S(1)}, f32[1,64,256]{2,1,0:T(8,128)}, u32[]{:S(2)}) %copy-start) | copy-done | bytes 65560
  0.8 0.2 fusion.34
  1.0 1.0 %fusion.32 = f32[64,64]{1,0:T(8,128)S(1)} fusion(f32[1,64,256]{2,1,0:T(8,128)S(1)} %copy-done, f32[1,64,256]{2,1,0:T(8,128)} %param.6), kind=kOutput, calls=%fused_computation.50 | convolution fusion | flops 12582912 | bytes 147456 | tf_op jit(solution)/shard_map/dot_general | solution.py:112
  2.2 0.7 %iota_compare_fusion.5 = pred[16,16]{1,0:T(8,128)(4,1)S(1)} fusion(s32[16]{0:T(128)} %bitcast.29), kind=kLoop, calls=%fused_computation.65 | loop fusion | flops 256 | bytes 320 | tf_op jit(solution)/shard_map/lt | solution.py:93
  2.9 0.8 %fusion.23 = (pred[16,128]{1,0:T(8,128)(4,1)S(1)}, pred[128]{0:T(512)(128)(4,1)S(1)}) fusion(s32[16,16]{1,0:T(8,128)} %bitcast.28, pred[16,16]{1,0:T(8,128)(4,1)S(1)} %iota_compare_fusion.5), kind=kLoop, calls=%fused_computation.27 | loop fusion | flops 128896 | bytes 3456 | tf_op jit(solution)/shard_map/reduce_or | solution.py:95
  3.8 0.1 ge.21
  4.0 0.1 broadcast_in_dim.67
  4.2 0.1 mul.25
  4.3 0.9 %copy.7 = s32[8,2,8,128]{3,1,2,0:T(2,128)S(1)} copy(s32[8,2,8,128]{3,2,1,0:T(8,128)} %bitcast.27) | data formatting | bytes 131072
  5.2 0.7 %broadcast_bitcast_fusion = f32[8,2,8,128]{3,2,1,0:T(8,128)S(1)} fusion(f32[64]{0:T(128)} %param.8), kind=kLoop, calls=%fused_computation.63 | loop fusion | bytes 65792
  6.3 1.6 %collective-permute-start.1 = (f32[64,128]{1,0:T(8,128)S(1)}, f32[64,128]{1,0:T(8,128)S(1)}, u32[]{:S(2)}, u32[]{:S(2)}) collective-permute-start(f32[64,128]{1,0:T(8,128)S(1)} %fusion.42), channel_id=1, source_target_pairs={{0,32},{16,48},{32,0},{48,16},{64,96},{80,112},{96,64},{112,80},{1... | collective-permute-start | bytes 98312 | tf_op jit(solution)/shard_map/ppermute | solution.py:38
  7.9 1.1 %fusion.19 = (bf16[64,16384]{1,0:T(8,128)(2,1)S(1)}, bf16[64,16384]{1,0:T(8,128)(2,1)S(1)}, bf16[64,16384]{1,0:T(8,128)(2,1)S(1)}) fusion(s32[16384]{0:T(1024)S(1)} %get-tuple-element.18, bf16[16384]{0:T(1024)(128)(2,1)S(1)} %get-tuple-element.22, bf16[16384]{0:T(1024)(128)(2,1)S(1)} %get-tuple-element.23, bf16[16384]{0:T(1024)(128)(2,1)S(1)} %get-tuple-element.24), kind=kLoop, calls=%fused_computation.21 | loop fusion | flops 4194304 | bytes 6455296 | tf_op jit(solution)/shard_map/jit(_where)/select_n | solution.py:53
  9.0 1.2 %collective-permute-done.1 = f32[64,128]{1,0:T(8,128)S(1)} collective-permute-done((f32[64,128]{1,0:T(8,128)S(1)}, f32[64,128]{1,0:T(8,128)S(1)}, u32[]{:S(2)}, u32[]{:S(2)}) %collective-permute-start.1) | collective-permute-done | bytes 32800 | tf_op jit(solution)/shard_map/ppermute | solution.py:38
  10.2 2.9 %collective-permute-start.2 = (f32[64,128]{1,0:T(8,128)S(1)}, f32[64,128]{1,0:T(8,128)S(1)}, u32[]{:S(2)}, u32[]{:S(2)}) collective-permute-start(f32[64,128]{1,0:T(8,128)S(1)} %add.72), channel_id=1, source_target_pairs={{0,96},{16,112},{32,64},{48,80},{64,32},{80,48},{96,0},{112,16},{1... | collective-permute-start | bytes 98312 | tf_op jit(solution)/shard_map/ppermute | solution.py:38
  13.1 1.9 %fusion.1 = f32[192,128]{1,0:T(8,128)S(1)} fusion(bf16[64,16384]{1,0:T(8,128)(2,1)S(1)} %get-tuple-element.20, bf16[64,16384]{1,0:T(8,128)(2,1)S(1)} %get-tuple-element.21, bf16[64,16384]{1,0:T(8,128)(2,1)S(1)} %get-tuple-element.19, s32[16384]{0:T(1024)S(1)} %get-tuple-element.17), kind=kOutput, calls=%fused_computation.2 | convolution fusion | flops 826277888 | bytes 6455296 | tf_op jit(solution)/shard_map/dot_general | solution.py:54
  15.1 0.3 collective-permute-done.2
  15.4 2.0 %collective-permute-start.3 = (f32[64,128]{1,0:T(8,128)S(1)}, f32[64,128]{1,0:T(8,128)S(1)}, u32[]{:S(2)}, u32[]{:S(2)}) collective-permute-start(f32[64,128]{1,0:T(8,128)S(1)} %add.73), channel_id=1, source_target_pairs={{0,1},{1,0},{2,3},{3,2},{4,5},{5,4},{6,7},{7,6},{8,9},{9,8},{10,11... | collective-permute-start | bytes 98312 | tf_op jit(solution)/shard_map/ppermute | solution.py:38
  17.4 1.9 %collective-permute-done.3 = f32[64,128]{1,0:T(8,128)S(1)} collective-permute-done((f32[64,128]{1,0:T(8,128)S(1)}, f32[64,128]{1,0:T(8,128)S(1)}, u32[]{:S(2)}, u32[]{:S(2)}) %collective-permute-start.3) | collective-permute-done | bytes 32800 | tf_op jit(solution)/shard_map/ppermute | solution.py:38
  19.3 4.1 %collective-permute-start.4 = (f32[64,128]{1,0:T(8,128)S(1)}, f32[64,128]{1,0:T(8,128)S(1)}, u32[]{:S(2)}, u32[]{:S(2)}) collective-permute-start(f32[64,128]{1,0:T(8,128)S(1)} %add.74), channel_id=1, source_target_pairs={{0,3},{1,2},{2,1},{3,0},{4,7},{5,6},{6,5},{7,4},{8,11},{9,10},{10,... | collective-permute-start | bytes 98312 | tf_op jit(solution)/shard_map/ppermute | solution.py:38
  23.4 1.9 %collective-permute-done.4 = f32[64,128]{1,0:T(8,128)S(1)} collective-permute-done((f32[64,128]{1,0:T(8,128)S(1)}, f32[64,128]{1,0:T(8,128)S(1)}, u32[]{:S(2)}, u32[]{:S(2)}) %collective-permute-start.4) | collective-permute-done | bytes 32800 | tf_op jit(solution)/shard_map/ppermute | solution.py:38
  25.3 0.6 add.79.joined_ref
  26.0 7.8 %shard_map.64 = f32[64,64]{1,0:T(8,128)} custom-call(f32[64,128]{1,0:T(8,128)} %add.79.joined_ref), custom_call_target="tpu_custom_call" | custom-call | tf_op jit(solution)/shard_map/pallas_call | solution.py:77
  33.8 1.0 %fusion.21 = f32[8,2,8,128]{3,2,1,0:T(8,128)S(1)} fusion(f32[64,64]{1,0:T(8,128)} %shard_map.64, f32[1,64,256]{2,1,0:T(8,128)S(1)} %copy-done, f32[1,64,256]{2,1,0:T(8,128)S(1)} %copy-done.1, f32[64]{0:T(128)S(1)} %copy-done.2), kind=kOutput, calls=%fused_computation.24 | convolution fusion | flops 12615680 | bytes 213248 | tf_op jit(solution)/shard_map/dot_general | solution.py:121
  34.9 1.1 %fusion.16 = (bf16[64,16384]{1,0:T(8,128)(2,1)S(1)}, bf16[64,16384]{1,0:T(8,128)(2,1)S(1)}, bf16[64,16384]{1,0:T(8,128)(2,1)S(1)}) fusion(s32[16384]{0:T(1024)S(1)} %get-tuple-element.18, bf16[16384]{0:T(1024)(128)(2,1)S(1)} %get-tuple-element.14, bf16[16384]{0:T(1024)(128)(2,1)S(1)} %get-tuple-element.15, bf16[16384]{0:T(1024)(128)(2,1)S(1)} %get-tuple-element.16), kind=kLoop, calls=%fused_computation.18 | loop fusion | flops 4194304 | bytes 6455296 | tf_op jit(solution)/shard_map/jit(_where)/select_n | solution.py:53
  36.0 1.9 %fusion = f32[192,128]{1,0:T(8,128)S(1)} fusion(bf16[64,16384]{1,0:T(8,128)(2,1)S(1)} %get-tuple-element.12, bf16[64,16384]{1,0:T(8,128)(2,1)S(1)} %get-tuple-element.13, bf16[64,16384]{1,0:T(8,128)(2,1)S(1)} %get-tuple-element.11, s32[16384]{0:T(1024)S(1)} %get-tuple-element.17), kind=kOutput, calls=%fused_computation.1 | convolution fusion | flops 826277888 | bytes 6455296 | tf_op jit(solution)/shard_map/dot_general | solution.py:54
  38.0 14.7 %all_to_all.9 = f32[16,1,1024]{2,1,0:T(1,128)S(1)} all-to-all(f32[16,1,1024]{2,1,0:T(1,128)S(1)} %all_to_all.6), channel_id=1, replica_groups=mesh['section'=8,'wafer'=4,'sub'=4] {'wafer','sub'}, dimensions={0} | all-to-all | bytes 131072 | tf_op jit(solution)/shard_map/all_to_all | solution.py:130
  52.9 1.2 %collective-permute-done.5 = f32[1024]{0:T(1024)S(1)} collective-permute-done((f32[1024]{0:T(1024)S(1)}, f32[1024]{0:T(1024)S(1)}, u32[]{:S(2)}, u32[]{:S(2)}) %collective-permute-start.5) | collective-permute-done | bytes 4128 | tf_op jit(solution)/shard_map/ppermute | solution.py:38
  54.0 0.3 collective-permute-start.6
  54.3 3.3 %collective-permute-done.6 = f32[1024]{0:T(1024)S(1)} collective-permute-done((f32[1024]{0:T(1024)S(1)}, f32[1024]{0:T(1024)S(1)}, u32[]{:S(2)}, u32[]{:S(2)}) %collective-permute-start.6) | collective-permute-done | bytes 4128 | tf_op jit(solution)/shard_map/ppermute | solution.py:38
  57.6 2.8 %collective-permute-start.7 = (f32[1024]{0:T(1024)S(1)}, f32[1024]{0:T(1024)S(1)}, u32[]{:S(2)}, u32[]{:S(2)}) collective-permute-start(f32[1024]{0:T(1024)S(1)} %add.84), channel_id=1, source_target_pairs={{0,96},{16,112},{32,64},{48,80},{64,32},{80,48},{96,0},{112,16},{1... | collective-permute-start | bytes 12296 | tf_op jit(solution)/shard_map/ppermute | solution.py:38
  60.4 2.1 %collective-permute-done.7 = f32[1024]{0:T(1024)S(1)} collective-permute-done((f32[1024]{0:T(1024)S(1)}, f32[1024]{0:T(1024)S(1)}, u32[]{:S(2)}, u32[]{:S(2)}) %collective-permute-start.7) | collective-permute-done | bytes 4128 | tf_op jit(solution)/shard_map/ppermute | solution.py:38
  62.5 0.6 maximum_divide_fusion
  (33 shorter events, 0.8 us)
Async XLA Ops:
  0.0 0.8 %copy-start = (f32[1,64,256]{2,1,0:T(8,128)S(1)}, f32[1,64,256]{2,1,0:T(8,128)}, u32[]{:S(2)}) copy-start(f32[1,64,256]{2,1,0:T(8,128)} %param.7) | copy-start | bytes 196612
  2.2 4.0 %collective-permute-start = (f32[64,128]{1,0:T(8,128)S(1)}, f32[64,128]{1,0:T(8,128)S(1)}, u32[]{:S(2)}, u32[]{:S(2)}) collective-permute-start(f32[64,128]{1,0:T(8,128)S(1)} %pad_maximum_fusion.1), channel_id=1, source_target_pairs={{0,16},{16,0},{32,48},{48,32},{64,80},{80,64},{96,112},{112,96},{1... | collective-permute-start | bytes 98312 | tf_op jit(solution)/shard_map/ppermute | solution.py:38
  6.3 3.9 %collective-permute-start.1 = (f32[64,128]{1,0:T(8,128)S(1)}, f32[64,128]{1,0:T(8,128)S(1)}, u32[]{:S(2)}, u32[]{:S(2)}) collective-permute-start(f32[64,128]{1,0:T(8,128)S(1)} %fusion.42), channel_id=1, source_target_pairs={{0,32},{16,48},{32,0},{48,16},{64,96},{80,112},{96,64},{112,80},{1... | collective-permute-start | bytes 98312 | tf_op jit(solution)/shard_map/ppermute | solution.py:38
  10.2 5.1 %collective-permute-start.2 = (f32[64,128]{1,0:T(8,128)S(1)}, f32[64,128]{1,0:T(8,128)S(1)}, u32[]{:S(2)}, u32[]{:S(2)}) collective-permute-start(f32[64,128]{1,0:T(8,128)S(1)} %add.72), channel_id=1, source_target_pairs={{0,96},{16,112},{32,64},{48,80},{64,32},{80,48},{96,0},{112,16},{1... | collective-permute-start | bytes 98312 | tf_op jit(solution)/shard_map/ppermute | solution.py:38
  13.1 20.6 %copy-start.1 = (f32[1,64,256]{2,1,0:T(8,128)S(1)}, f32[1,64,256]{2,1,0:T(8,128)}, u32[]{:S(2)}) copy-start(f32[1,64,256]{2,1,0:T(8,128)} %param.6) | copy-start | bytes 196612
  13.1 20.6 %copy-start.2 = (f32[64]{0:T(128)S(1)}, f32[64]{0:T(128)}, u32[]{:S(2)}) copy-start(f32[64]{0:T(128)} %param.8) | copy-start | bytes 772
  15.4 3.9 %collective-permute-start.3 = (f32[64,128]{1,0:T(8,128)S(1)}, f32[64,128]{1,0:T(8,128)S(1)}, u32[]{:S(2)}, u32[]{:S(2)}) collective-permute-start(f32[64,128]{1,0:T(8,128)S(1)} %add.73), channel_id=1, source_target_pairs={{0,1},{1,0},{2,3},{3,2},{4,5},{5,4},{6,7},{7,6},{8,9},{9,8},{10,11... | collective-permute-start | bytes 98312 | tf_op jit(solution)/shard_map/ppermute | solution.py:38
  19.3 6.0 %collective-permute-start.4 = (f32[64,128]{1,0:T(8,128)S(1)}, f32[64,128]{1,0:T(8,128)S(1)}, u32[]{:S(2)}, u32[]{:S(2)}) collective-permute-start(f32[64,128]{1,0:T(8,128)S(1)} %add.74), channel_id=1, source_target_pairs={{0,3},{1,2},{2,1},{3,0},{4,7},{5,6},{6,5},{7,4},{8,11},{9,10},{10,... | collective-permute-start | bytes 98312 | tf_op jit(solution)/shard_map/ppermute | solution.py:38
  52.8 1.2 %collective-permute-start.5 = (f32[1024]{0:T(1024)S(1)}, f32[1024]{0:T(1024)S(1)}, u32[]{:S(2)}, u32[]{:S(2)}) collective-permute-start(f32[1024]{0:T(1024)S(1)} %reduce_sum.19), channel_id=1, source_target_pairs={{0,16},{16,0},{32,48},{48,32},{64,80},{80,64},{96,112},{112,96},{1... | collective-permute-start | bytes 12296 | tf_op jit(solution)/shard_map/ppermute | solution.py:38
  54.0 3.6 %collective-permute-start.6 = (f32[1024]{0:T(1024)S(1)}, f32[1024]{0:T(1024)S(1)}, u32[]{:S(2)}, u32[]{:S(2)}) collective-permute-start(f32[1024]{0:T(1024)S(1)} %add.83), channel_id=1, source_target_pairs={{0,32},{16,48},{32,0},{48,16},{64,96},{80,112},{96,64},{112,80},{1... | collective-permute-start | bytes 12296 | tf_op jit(solution)/shard_map/ppermute | solution.py:38
  57.6 4.8 %collective-permute-start.7 = (f32[1024]{0:T(1024)S(1)}, f32[1024]{0:T(1024)S(1)}, u32[]{:S(2)}, u32[]{:S(2)}) collective-permute-start(f32[1024]{0:T(1024)S(1)} %add.84), channel_id=1, source_target_pairs={{0,96},{16,112},{32,64},{48,80},{64,32},{80,48},{96,0},{112,16},{1... | collective-permute-start | bytes 12296 | tf_op jit(solution)/shard_map/ppermute | solution.py:38

commit v7 on v6

--- a/solution.py
+++ b/solution.py
@@ -4,6 +4,7 @@
 from jax.experimental import pallas as pl
 from jax.experimental.pallas import tpu as pltpu
 from jax.sharding import PartitionSpec as P
+
 
 BL = 128
 TILE = 512
@@ -57,7 +58,7 @@
     return ((binned[0] + binned[1]) + binned[2]).reshape(owners, TILE)
 
 
-def solve_kernel(joined_ref, coef_ref):
+def fit_kernel(joined_ref, templates_ref, streams_ref, weight_ref, weighted_ref):
     n = joined_ref.shape[0]
     m = joined_ref[...]
     rows = lax.broadcasted_iota(jnp.int32, m.shape, 0)
@@ -69,20 +70,24 @@
         m = jnp.where(rows == k, scaled, m - column * scaled)
     lanes = lax.broadcasted_iota(jnp.int32, (n, n), 1)
     diag = jnp.sum(jnp.where(lanes == rows[:, :n], m[:, :n], 0.0), axis=1, keepdims=True)
-    coef_ref[...] = m[:, n:] / diag
+    coef = m[:, n:] / diag
+    removed = lax.dot_general(
+        coef, templates_ref[...], (((0,), (0,)), ((), ())),
+        precision=HIGHEST, preferred_element_type=jnp.float32,
+    )
+    weighted_ref[...] = (streams_ref[...] - removed) * weight_ref[...]
 
 
-def solve_fit(joined):
-    n = joined.shape[0]
+def fit_and_weight(joined, template_rows, streams, det_weight):
     return pl.pallas_call(
-        solve_kernel,
-        out_shape=jax.ShapeDtypeStruct((n, joined.shape[1] - n), jnp.float32),
-        in_specs=[pl.BlockSpec(memory_space=pltpu.VMEM)],
+        fit_kernel,
+        out_shape=jax.ShapeDtypeStruct(streams.shape, jnp.float32),
+        in_specs=[pl.BlockSpec(memory_space=pltpu.VMEM)] * 4,
         out_specs=pl.BlockSpec(memory_space=pltpu.VMEM),
-    )(joined)
+    )(joined, template_rows, streams, det_weight.reshape(-1, 1))
 
 
-def shards(tod, templates, det_weight, pixel, hitlist, counts):
+def filter_and_bin(tod, templates, det_weight, pixel, hitlist, counts):
     dets, samp_local = tod.shape[1], tod.shape[2]
     owners = hitlist.shape[1]
     slots = hitlist.shape[2]
@@ -113,17 +118,14 @@
         template_rows, streams, (((1,), (1,)), ((), ())),
         precision=HIGHEST, preferred_element_type=jnp.float32,
     )
+    def weight_map():
+        return bin_tiles(sample_weight, upper_hot, lower_hot, owners)
+
     joined, wgt_part = all_sum(
         jnp.concatenate([gram_sum, projection], axis=1), ("section", "sub"),
-        cover=lambda: bin_tiles(sample_weight, upper_hot, lower_hot, owners), cover_round=4,
+        cover=weight_map, cover_round=4,
     )
-    coef_fit = solve_fit(joined)
-    removed = lax.dot_general(
-        coef_fit, template_rows, (((0,), (0,)), ((), ())),
-        precision=HIGHEST, preferred_element_type=jnp.float32,
-    )
-    filtered = streams - removed
-    weighted = filtered * det_weight[:, None]
+    weighted = fit_and_weight(joined, template_rows, streams, det_weight)
 
     num_part = bin_tiles(weighted, upper_hot, lower_hot, owners)
     partial = jnp.concatenate([num_part, wgt_part], axis=1)
@@ -142,6 +144,4 @@
         P(None, "wafer", ("section", "sub")),
         P(None, "wafer", ("section", "sub")),
     )
-    return jax.shard_map(
-        shards, mesh=mesh, in_specs=placed, out_specs=P(("wafer", "sub")), check_vma=False
-    )
+    return jax.shard_map(filter_and_bin, mesh=mesh, in_specs=placed, out_specs=P(("wafer", "sub")), check_vma=False)

time: 63.5 us -> 63.8 us (level)
  waiting for transfers between devices: 11.8 us -> 11.1 us
  local copies, waits for them, and re-layouts: 3.17 us -> 3.87 us
    ppermute x8, waiting for transfers between devices: 11.8 us -> 11.1 us  [all_sum(): x = x + lax.ppermute(x, axis, pairs)]
    broadcast_in_dim x2 -> x3, local copies, waits for them, and re-layouts: 0.26 us -> 0.96 us  [the longest x1 0.7 us: filter_and_bin(): sample_weight = jnp.broadcast_to(det_weight[:, None], tod.shape[1:])]
    dot_general x3 -> x2, matrix products: 2.25 us -> 2.19 us  [the longest x1 1.11 us: filter_and_bin(): lax.dot_general(template_rows, template_rows, (((1,), (1,)), ((), ())), p...]
    unnamed x10 -> x6, local copies, waits for them, and re-layouts: 2.53 us -> 2.52 us
  transfers between devices with their start and end apart: 8 -> 8, of which waited for: 7 -> 7; matrix products, arithmetic and copies ran while one was open for 11% -> 12% of each run, Pallas kernels for 0% -> 0%
where the time goes in v7:
time: 63.8 us; the launch traced here: 63.3 us
  blocking collectives  14.7 us (23%)
  starting transfers between devices  13.8 us (22%)
  waiting for transfers between devices  11.1 us (17%)
  Pallas kernels  8.21 us (13%)
  matrix products  6.06 us (9%)
  other arithmetic  5.36 us (8%)
  local copies, waits for them, and re-layouts  3.87 us (6%)
    all_to_all x1, blocking collectives, filter_and_bin(): lax.all_to_all(partial, ('wafer', 'sub'), split_axis=0, concat_axis=0, ti...  14.7 us
    ppermute x8, starting transfers between devices, all_sum(): x = x + lax.ppermute(x, axis, pairs)  13.8 us
    ppermute x8, waiting for transfers between devices, all_sum(): x = x + lax.ppermute(x, axis, pairs)  11.1 us
    pallas_call x1, Pallas kernels, fit_and_weight(): pl.pallas_call(fit_kernel, out_shape=jax.ShapeDtypeStruct(streams.shape,...  8.21 us
    dot_general x2, matrix products, bin_tiles(): lax.dot_general(stacked, lower_hot, (((1,), (1,)), ((), ())), preferred_e...  3.88 us
    unnamed x6, local copies, waits for them, and re-layouts  2.52 us
    select_n x2, other arithmetic, bin_tiles(): jnp.where(upper_hot, p, jnp.bfloat16(0))  2.19 us
  transfers between devices with their start and end apart: 8, of which 7 were waited for; matrix products, arithmetic and copies ran while one was open for 12% of the time, Pallas kernels for 0%

profile of v7, /device:TPU:0, one launch (start us, length us, event | category | flops | bytes accessed | tf_op | source)
XLA Modules:
  0.0 63.3 jit_solution(548685111342905300)
XLA Ops:
  0.0 1.1 %fusion.36 = f32[64,64]{1,0:T(8,128)S(1)} fusion(f32[1,64,256]{2,1,0:T(8,128)} %param.7), kind=kOutput, calls=%fused_computation.66 | convolution fusion | flops 12582912 | bytes 81920 | tf_op jit(solution)/shard_map/dot_general | solution.py:113
  1.1 1.1 %fusion.33 = f32[64,64]{1,0:T(8,128)S(1)} fusion(f32[1,64,256]{2,1,0:T(8,128)} %param.6, f32[1,64,256]{2,1,0:T(8,128)} %param.7), kind=kOutput, calls=%fused_computation.63 | convolution fusion | flops 12582912 | bytes 147456 | tf_op jit(solution)/shard_map/dot_general | solution.py:117
  2.3 0.7 %iota_compare_fusion.5 = pred[16,16]{1,0:T(8,128)(4,1)S(1)} fusion(s32[16]{0:T(128)} %bitcast.29), kind=kLoop, calls=%fused_computation.56 | loop fusion | flops 256 | bytes 320 | tf_op jit(solution)/shard_map/lt | solution.py:98
  3.0 0.8 %fusion.21 = (pred[16,128]{1,0:T(8,128)(4,1)S(1)}, pred[128]{0:T(512)(128)(4,1)S(1)}) fusion(s32[16,16]{1,0:T(8,128)} %bitcast.27, pred[16,16]{1,0:T(8,128)(4,1)S(1)} %iota_compare_fusion.5), kind=kLoop, calls=%fused_computation.24 | loop fusion | flops 128896 | bytes 3456 | tf_op jit(solution)/shard_map/reduce_or | solution.py:100
  3.9 0.1 mul.19
  4.1 0.2 ge.21
  4.2 0.1 broadcast_in_dim.68
  4.4 0.9 %copy.11 = s32[8,2,8,128]{3,1,2,0:T(2,128)S(1)} copy(s32[8,2,8,128]{3,2,1,0:T(8,128)} %bitcast.26) | data formatting | bytes 131072
  5.3 0.7 %broadcast_bitcast_fusion = f32[8,2,8,128]{3,2,1,0:T(8,128)S(1)} fusion(f32[64]{0:T(128)} %param.8), kind=kLoop, calls=%fused_computation.54 | loop fusion | bytes 65792
  6.4 1.6 %collective-permute-start.1 = (f32[64,128]{1,0:T(8,128)S(1)}, f32[64,128]{1,0:T(8,128)S(1)}, u32[]{:S(2)}, u32[]{:S(2)}) collective-permute-start(f32[64,128]{1,0:T(8,128)S(1)} %fusion.38), channel_id=1, source_target_pairs={{0,32},{16,48},{32,0},{48,16},{64,96},{80,112},{96,64},{112,80},{1... | collective-permute-start | bytes 98312 | tf_op jit(solution)/shard_map/ppermute | solution.py:39
  8.0 1.1 %fusion.19 = (bf16[64,16384]{1,0:T(8,128)(2,1)S(1)}, bf16[64,16384]{1,0:T(8,128)(2,1)S(1)}, bf16[64,16384]{1,0:T(8,128)(2,1)S(1)}) fusion(s32[16384]{0:T(1024)S(1)} %get-tuple-element.18, bf16[16384]{0:T(1024)(128)(2,1)S(1)} %get-tuple-element.22, bf16[16384]{0:T(1024)(128)(2,1)S(1)} %get-tuple-element.23, bf16[16384]{0:T(1024)(128)(2,1)S(1)} %get-tuple-element.24), kind=kLoop, calls=%fused_computation.21 | loop fusion | flops 4194304 | bytes 6455296 | tf_op jit(solution)/shard_map/jit(_where)/select_n | solution.py:54
  9.1 1.2 %collective-permute-done.1 = f32[64,128]{1,0:T(8,128)S(1)} collective-permute-done((f32[64,128]{1,0:T(8,128)S(1)}, f32[64,128]{1,0:T(8,128)S(1)}, u32[]{:S(2)}, u32[]{:S(2)}) %collective-permute-start.1) | collective-permute-done | bytes 32800 | tf_op jit(solution)/shard_map/ppermute | solution.py:39
  10.4 2.9 %collective-permute-start.2 = (f32[64,128]{1,0:T(8,128)S(1)}, f32[64,128]{1,0:T(8,128)S(1)}, u32[]{:S(2)}, u32[]{:S(2)}) collective-permute-start(f32[64,128]{1,0:T(8,128)S(1)} %add.72), channel_id=1, source_target_pairs={{0,96},{16,112},{32,64},{48,80},{64,32},{80,48},{96,0},{112,16},{1... | collective-permute-start | bytes 98312 | tf_op jit(solution)/shard_map/ppermute | solution.py:39
  13.2 1.9 %fusion.1 = f32[192,128]{1,0:T(8,128)S(1)} fusion(bf16[64,16384]{1,0:T(8,128)(2,1)S(1)} %get-tuple-element.20, bf16[64,16384]{1,0:T(8,128)(2,1)S(1)} %get-tuple-element.21, bf16[64,16384]{1,0:T(8,128)(2,1)S(1)} %get-tuple-element.19, s32[16384]{0:T(1024)S(1)} %get-tuple-element.17), kind=kOutput, calls=%fused_computation.2 | convolution fusion | flops 826277888 | bytes 6455296 | tf_op jit(solution)/shard_map/dot_general | solution.py:55
  15.2 0.3 collective-permute-done.2
  15.5 2.0 %collective-permute-start.3 = (f32[64,128]{1,0:T(8,128)S(1)}, f32[64,128]{1,0:T(8,128)S(1)}, u32[]{:S(2)}, u32[]{:S(2)}) collective-permute-start(f32[64,128]{1,0:T(8,128)S(1)} %add.73), channel_id=1, source_target_pairs={{0,1},{1,0},{2,3},{3,2},{4,5},{5,4},{6,7},{7,6},{8,9},{9,8},{10,11... | collective-permute-start | bytes 98312 | tf_op jit(solution)/shard_map/ppermute | solution.py:39
  17.5 1.9 %collective-permute-done.3 = f32[64,128]{1,0:T(8,128)S(1)} collective-permute-done((f32[64,128]{1,0:T(8,128)S(1)}, f32[64,128]{1,0:T(8,128)S(1)}, u32[]{:S(2)}, u32[]{:S(2)}) %collective-permute-start.3) | collective-permute-done | bytes 32800 | tf_op jit(solution)/shard_map/ppermute | solution.py:39
  19.4 4.1 %collective-permute-start.4 = (f32[64,128]{1,0:T(8,128)S(1)}, f32[64,128]{1,0:T(8,128)S(1)}, u32[]{:S(2)}, u32[]{:S(2)}) collective-permute-start(f32[64,128]{1,0:T(8,128)S(1)} %add.74), channel_id=1, source_target_pairs={{0,3},{1,2},{2,1},{3,0},{4,7},{5,6},{6,5},{7,4},{8,11},{9,10},{10,... | collective-permute-start | bytes 98312 | tf_op jit(solution)/shard_map/ppermute | solution.py:39
  23.6 0.7 %copy.10.weight_ref = f32[64,1]{1,0:T(8,128)} copy(f32[64,1]{0,1:T(1,128)S(1)} %bitcast.28) | data formatting | bytes 512 | tf_op jit(solution)/shard_map/broadcast_in_dim | solution.py:110
  24.3 1.2 %collective-permute-done.4 = f32[64,128]{1,0:T(8,128)S(1)} collective-permute-done((f32[64,128]{1,0:T(8,128)S(1)}, f32[64,128]{1,0:T(8,128)S(1)}, u32[]{:S(2)}, u32[]{:S(2)}) %collective-permute-start.4) | collective-permute-done | bytes 32800 | tf_op jit(solution)/shard_map/ppermute | solution.py:39
  25.4 0.6 add.79.joined_ref
  26.1 8.2 %shard_map.64 = f32[64,256]{1,0:T(8,128)} custom-call(f32[64,128]{1,0:T(8,128)} %add.79.joined_ref, f32[64,256]{1,0:T(8,128)} %bitcast.19, f32[64,256]{1,0:T(8,128)} %bitcast.24, f32[64,1]{1,0:T(8,128)} %copy.10.weight_ref), custom_call_target="tpu_custom_call" | custom-call | tf_op jit(solution)/shard_map/pallas_call | solution.py:82
  34.3 0.9 %copy.13 = f32[8,2,8,128]{3,1,2,0:T(2,128)S(1)} copy(f32[8,2,8,128]{3,2,1,0:T(8,128)} %bitcast.25) | data formatting | bytes 131072
  35.2 1.1 %fusion.16 = (bf16[64,16384]{1,0:T(8,128)(2,1)S(1)}, bf16[64,16384]{1,0:T(8,128)(2,1)S(1)}, bf16[64,16384]{1,0:T(8,128)(2,1)S(1)}) fusion(s32[16384]{0:T(1024)S(1)} %get-tuple-element.18, bf16[16384]{0:T(1024)(128)(2,1)S(1)} %get-tuple-element.14, bf16[16384]{0:T(1024)(128)(2,1)S(1)} %get-tuple-element.15, bf16[16384]{0:T(1024)(128)(2,1)S(1)} %get-tuple-element.16), kind=kLoop, calls=%fused_computation.18 | loop fusion | flops 4194304 | bytes 6455296 | tf_op jit(solution)/shard_map/jit(_where)/select_n | solution.py:54
  36.3 1.9 %fusion = f32[192,128]{1,0:T(8,128)S(1)} fusion(bf16[64,16384]{1,0:T(8,128)(2,1)S(1)} %get-tuple-element.12, bf16[64,16384]{1,0:T(8,128)(2,1)S(1)} %get-tuple-element.13, bf16[64,16384]{1,0:T(8,128)(2,1)S(1)} %get-tuple-element.11, s32[16384]{0:T(1024)S(1)} %get-tuple-element.17), kind=kOutput, calls=%fused_computation.1 | convolution fusion | flops 826277888 | bytes 6455296 | tf_op jit(solution)/shard_map/dot_general | solution.py:55
  38.3 14.7 %all_to_all.9 = f32[16,1,1024]{2,1,0:T(1,128)S(1)} all-to-all(f32[16,1,1024]{2,1,0:T(1,128)S(1)} %all_to_all.6), channel_id=1, replica_groups=mesh['section'=8,'wafer'=4,'sub'=4] {'wafer','sub'}, dimensions={0} | all-to-all | bytes 131072 | tf_op jit(solution)/shard_map/all_to_all | solution.py:132
  53.2 1.2 %collective-permute-done.5 = f32[1024]{0:T(1024)S(1)} collective-permute-done((f32[1024]{0:T(1024)S(1)}, f32[1024]{0:T(1024)S(1)}, u32[]{:S(2)}, u32[]{:S(2)}) %collective-permute-start.5) | collective-permute-done | bytes 4128 | tf_op jit(solution)/shard_map/ppermute | solution.py:39
  54.3 0.3 collective-permute-start.6
  54.6 3.3 %collective-permute-done.6 = f32[1024]{0:T(1024)S(1)} collective-permute-done((f32[1024]{0:T(1024)S(1)}, f32[1024]{0:T(1024)S(1)}, u32[]{:S(2)}, u32[]{:S(2)}) %collective-permute-start.6) | collective-permute-done | bytes 4128 | tf_op jit(solution)/shard_map/ppermute | solution.py:39
  57.9 2.8 %collective-permute-start.7 = (f32[1024]{0:T(1024)S(1)}, f32[1024]{0:T(1024)S(1)}, u32[]{:S(2)}, u32[]{:S(2)}) collective-permute-start(f32[1024]{0:T(1024)S(1)} %add.84), channel_id=1, source_target_pairs={{0,96},{16,112},{32,64},{48,80},{64,32},{80,48},{96,0},{112,16},{1... | collective-permute-start | bytes 12296 | tf_op jit(solution)/shard_map/ppermute | solution.py:39
  60.7 2.1 %collective-permute-done.7 = f32[1024]{0:T(1024)S(1)} collective-permute-done((f32[1024]{0:T(1024)S(1)}, f32[1024]{0:T(1024)S(1)}, u32[]{:S(2)}, u32[]{:S(2)}) %collective-permute-start.7) | collective-permute-done | bytes 4128 | tf_op jit(solution)/shard_map/ppermute | solution.py:39
  62.8 0.6 maximum_divide_fusion
  (29 shorter events, 0.8 us)
Async XLA Ops:
  2.3 4.0 %collective-permute-start = (f32[64,128]{1,0:T(8,128)S(1)}, f32[64,128]{1,0:T(8,128)S(1)}, u32[]{:S(2)}, u32[]{:S(2)}) collective-permute-start(f32[64,128]{1,0:T(8,128)S(1)} %pad_maximum_fusion.1), channel_id=1, source_target_pairs={{0,16},{16,0},{32,48},{48,32},{64,80},{80,64},{96,112},{112,96},{1... | collective-permute-start | bytes 98312 | tf_op jit(solution)/shard_map/ppermute | solution.py:39
  6.4 3.9 %collective-permute-start.1 = (f32[64,128]{1,0:T(8,128)S(1)}, f32[64,128]{1,0:T(8,128)S(1)}, u32[]{:S(2)}, u32[]{:S(2)}) collective-permute-start(f32[64,128]{1,0:T(8,128)S(1)} %fusion.38), channel_id=1, source_target_pairs={{0,32},{16,48},{32,0},{48,16},{64,96},{80,112},{96,64},{112,80},{1... | collective-permute-start | bytes 98312 | tf_op jit(solution)/shard_map/ppermute | solution.py:39
  10.4 5.1 %collective-permute-start.2 = (f32[64,128]{1,0:T(8,128)S(1)}, f32[64,128]{1,0:T(8,128)S(1)}, u32[]{:S(2)}, u32[]{:S(2)}) collective-permute-start(f32[64,128]{1,0:T(8,128)S(1)} %add.72), channel_id=1, source_target_pairs={{0,96},{16,112},{32,64},{48,80},{64,32},{80,48},{96,0},{112,16},{1... | collective-permute-start | bytes 98312 | tf_op jit(solution)/shard_map/ppermute | solution.py:39
  13.2 10.3 %copy-start = (f32[64]{0:T(128)S(1)}, f32[64]{0:T(128)}, u32[]{:S(2)}) copy-start(f32[64]{0:T(128)} %param.8) | copy-start | bytes 772
  15.5 3.9 %collective-permute-start.3 = (f32[64,128]{1,0:T(8,128)S(1)}, f32[64,128]{1,0:T(8,128)S(1)}, u32[]{:S(2)}, u32[]{:S(2)}) collective-permute-start(f32[64,128]{1,0:T(8,128)S(1)} %add.73), channel_id=1, source_target_pairs={{0,1},{1,0},{2,3},{3,2},{4,5},{5,4},{6,7},{7,6},{8,9},{9,8},{10,11... | collective-permute-start | bytes 98312 | tf_op jit(solution)/shard_map/ppermute | solution.py:39
  19.4 6.0 %collective-permute-start.4 = (f32[64,128]{1,0:T(8,128)S(1)}, f32[64,128]{1,0:T(8,128)S(1)}, u32[]{:S(2)}, u32[]{:S(2)}) collective-permute-start(f32[64,128]{1,0:T(8,128)S(1)} %add.74), channel_id=1, source_target_pairs={{0,3},{1,2},{2,1},{3,0},{4,7},{5,6},{6,5},{7,4},{8,11},{9,10},{10,... | collective-permute-start | bytes 98312 | tf_op jit(solution)/shard_map/ppermute | solution.py:39
  53.1 1.2 %collective-permute-start.5 = (f32[1024]{0:T(1024)S(1)}, f32[1024]{0:T(1024)S(1)}, u32[]{:S(2)}, u32[]{:S(2)}) collective-permute-start(f32[1024]{0:T(1024)S(1)} %reduce_sum.19), channel_id=1, source_target_pairs={{0,16},{16,0},{32,48},{48,32},{64,80},{80,64},{96,112},{112,96},{1... | collective-permute-start | bytes 12296 | tf_op jit(solution)/shard_map/ppermute | solution.py:39
  54.3 3.6 %collective-permute-start.6 = (f32[1024]{0:T(1024)S(1)}, f32[1024]{0:T(1024)S(1)}, u32[]{:S(2)}, u32[]{:S(2)}) collective-permute-start(f32[1024]{0:T(1024)S(1)} %add.83), channel_id=1, source_target_pairs={{0,32},{16,48},{32,0},{48,16},{64,96},{80,112},{96,64},{112,80},{1... | collective-permute-start | bytes 12296 | tf_op jit(solution)/shard_map/ppermute | solution.py:39
  57.9 4.8 %collective-permute-start.7 = (f32[1024]{0:T(1024)S(1)}, f32[1024]{0:T(1024)S(1)}, u32[]{:S(2)}, u32[]{:S(2)}) collective-permute-start(f32[1024]{0:T(1024)S(1)} %add.84), channel_id=1, source_target_pairs={{0,96},{16,112},{32,64},{48,80},{64,32},{80,48},{96,0},{112,16},{1... | collective-permute-start | bytes 12296 | tf_op jit(solution)/shard_map/ppermute | solution.py:39

commit v8 on v6

--- a/solution.py
+++ b/solution.py
@@ -4,6 +4,7 @@
 from jax.experimental import pallas as pl
 from jax.experimental.pallas import tpu as pltpu
 from jax.sharding import PartitionSpec as P
+
 
 BL = 128
 TILE = 512
@@ -36,6 +37,8 @@
         if cover is not None and index == cover_round:
             x, covered = lax.optimization_barrier((x, cover()))
         x = x + lax.ppermute(x, axis, pairs)
+    if cover is not None and cover_round == len(rounds):
+        x, covered = lax.optimization_barrier((x, cover()))
     return x, covered
 
 
@@ -82,7 +85,7 @@
     )(joined)
 
 
-def shards(tod, templates, det_weight, pixel, hitlist, counts):
+def filter_and_bin(tod, templates, det_weight, pixel, hitlist, counts):
     dets, samp_local = tod.shape[1], tod.shape[2]
     owners = hitlist.shape[1]
     slots = hitlist.shape[2]
@@ -113,9 +116,12 @@
         template_rows, streams, (((1,), (1,)), ((), ())),
         precision=HIGHEST, preferred_element_type=jnp.float32,
     )
+    def weight_map():
+        return bin_tiles(sample_weight, upper_hot, lower_hot, owners)
+
     joined, wgt_part = all_sum(
         jnp.concatenate([gram_sum, projection], axis=1), ("section", "sub"),
-        cover=lambda: bin_tiles(sample_weight, upper_hot, lower_hot, owners), cover_round=4,
+        cover=weight_map, cover_round=5,
     )
     coef_fit = solve_fit(joined)
     removed = lax.dot_general(
@@ -142,6 +148,4 @@
         P(None, "wafer", ("section", "sub")),
         P(None, "wafer", ("section", "sub")),
     )
-    return jax.shard_map(
-        shards, mesh=mesh, in_specs=placed, out_specs=P(("wafer", "sub")), check_vma=False
-    )
+    return jax.shard_map(filter_and_bin, mesh=mesh, in_specs=placed, out_specs=P(("wafer", "sub")), check_vma=False)

time: 63.5 us -> 63.5 us (level)
  transfers between devices with their start and end apart: 8 -> 8, of which waited for: 7 -> 6; matrix products, arithmetic and copies ran while one was open for 11% -> 11% of each run, Pallas kernels for 0% -> 0%
where the time goes in v8:
time: 63.5 us; the launch traced here: 63 us
  blocking collectives  14.7 us (23%)
  starting transfers between devices  13.7 us (22%)
  waiting for transfers between devices  11.9 us (19%)
  Pallas kernels  7.81 us (12%)
  matrix products  6.13 us (10%)
  other arithmetic  5.37 us (8%)
  local copies, waits for them, and re-layouts  3.17 us (5%)
    all_to_all x1, blocking collectives, filter_and_bin(): lax.all_to_all(partial, ('wafer', 'sub'), split_axis=0, concat_axis=0, ti...  14.7 us
    ppermute x8, starting transfers between devices, all_sum(): x = x + lax.ppermute(x, axis, pairs)  13.7 us
    ppermute x8, waiting for transfers between devices, all_sum(): x = x + lax.ppermute(x, axis, pairs)  11.9 us
    pallas_call x1, Pallas kernels, solve_fit(): pl.pallas_call(solve_kernel, out_shape=jax.ShapeDtypeStruct((n, joined.sh...  7.81 us
    dot_general x2, matrix products, bin_tiles(): lax.dot_general(stacked, lower_hot, (((1,), (1,)), ((), ())), preferred_e...  3.87 us
    unnamed x10, local copies, waits for them, and re-layouts  2.53 us
    select_n x2, other arithmetic, bin_tiles(): jnp.where(upper_hot, p, jnp.bfloat16(0))  2.19 us
  transfers between devices with their start and end apart: 8, of which 6 were waited for; matrix products, arithmetic and copies ran while one was open for 11% of the time, Pallas kernels for 0%

profile of v8, /device:TPU:0, one launch (start us, length us, event | category | flops | bytes accessed | tf_op | source)
XLA Modules:
  0.0 63.0 jit_solution(8359701108410227486)
XLA Ops:
  0.0 0.8 %copy-done = f32[1,64,256]{2,1,0:T(8,128)S(1)} copy-done((f32[1,64,256]{2,1,0:T(8,128)S(1)}, f32[1,64,256]{2,1,0:T(8,128)}, u32[]{:S(2)}) %copy-start) | copy-done | bytes 65560
  0.8 0.2 fusion.34
  1.0 1.0 %fusion.32 = f32[64,64]{1,0:T(8,128)S(1)} fusion(f32[1,64,256]{2,1,0:T(8,128)S(1)} %copy-done, f32[1,64,256]{2,1,0:T(8,128)} %param.6), kind=kOutput, calls=%fused_computation.50 | convolution fusion | flops 12582912 | bytes 147456 | tf_op jit(solution)/shard_map/dot_general | solution.py:115
  2.2 0.7 %iota_compare_fusion.5 = pred[16,16]{1,0:T(8,128)(4,1)S(1)} fusion(s32[16]{0:T(128)} %bitcast.29), kind=kLoop, calls=%fused_computation.65 | loop fusion | flops 256 | bytes 320 | tf_op jit(solution)/shard_map/lt | solution.py:96
  2.9 0.8 %fusion.23 = (pred[16,128]{1,0:T(8,128)(4,1)S(1)}, pred[128]{0:T(512)(128)(4,1)S(1)}) fusion(s32[16,16]{1,0:T(8,128)} %bitcast.28, pred[16,16]{1,0:T(8,128)(4,1)S(1)} %iota_compare_fusion.5), kind=kLoop, calls=%fused_computation.27 | loop fusion | flops 128896 | bytes 3456 | tf_op jit(solution)/shard_map/reduce_or | solution.py:98
  3.8 0.1 ge.21
  4.0 0.1 broadcast_in_dim.67
  4.2 0.1 mul.25
  4.3 0.9 %copy.7 = s32[8,2,8,128]{3,1,2,0:T(2,128)S(1)} copy(s32[8,2,8,128]{3,2,1,0:T(8,128)} %bitcast.27) | data formatting | bytes 131072
  5.2 0.1 broadcast_in_dim.68
  5.4 0.7 %broadcast_bitcast_fusion = f32[8,2,8,128]{3,2,1,0:T(8,128)S(1)} fusion(f32[64]{0:T(128)} %param.8), kind=kLoop, calls=%fused_computation.63 | loop fusion | bytes 65792
  6.3 1.6 %collective-permute-start.1 = (f32[64,128]{1,0:T(8,128)S(1)}, f32[64,128]{1,0:T(8,128)S(1)}, u32[]{:S(2)}, u32[]{:S(2)}) collective-permute-start(f32[64,128]{1,0:T(8,128)S(1)} %fusion.42), channel_id=1, source_target_pairs={{0,32},{16,48},{32,0},{48,16},{64,96},{80,112},{96,64},{112,80},{1... | collective-permute-start | bytes 98312 | tf_op jit(solution)/shard_map/ppermute | solution.py:39
  7.9 2.3 %collective-permute-done.1 = f32[64,128]{1,0:T(8,128)S(1)} collective-permute-done((f32[64,128]{1,0:T(8,128)S(1)}, f32[64,128]{1,0:T(8,128)S(1)}, u32[]{:S(2)}, u32[]{:S(2)}) %collective-permute-start.1) | collective-permute-done | bytes 32800 | tf_op jit(solution)/shard_map/ppermute | solution.py:39
  10.2 2.9 %collective-permute-start.2 = (f32[64,128]{1,0:T(8,128)S(1)}, f32[64,128]{1,0:T(8,128)S(1)}, u32[]{:S(2)}, u32[]{:S(2)}) collective-permute-start(f32[64,128]{1,0:T(8,128)S(1)} %add.72), channel_id=1, source_target_pairs={{0,96},{16,112},{32,64},{48,80},{64,32},{80,48},{96,0},{112,16},{1... | collective-permute-start | bytes 98312 | tf_op jit(solution)/shard_map/ppermute | solution.py:39
  13.1 1.1 %fusion.19 = (bf16[64,16384]{1,0:T(8,128)(2,1)S(1)}, bf16[64,16384]{1,0:T(8,128)(2,1)S(1)}, bf16[64,16384]{1,0:T(8,128)(2,1)S(1)}) fusion(s32[16384]{0:T(1024)S(1)} %get-tuple-element.18, bf16[16384]{0:T(1024)(128)(2,1)S(1)} %get-tuple-element.22, bf16[16384]{0:T(1024)(128)(2,1)S(1)} %get-tuple-element.23, bf16[16384]{0:T(1024)(128)(2,1)S(1)} %get-tuple-element.24), kind=kLoop, calls=%fused_computation.21 | loop fusion | flops 4194304 | bytes 6455296 | tf_op jit(solution)/shard_map/jit(_where)/select_n | solution.py:56
  14.2 1.2 %collective-permute-done.2 = f32[64,128]{1,0:T(8,128)S(1)} collective-permute-done((f32[64,128]{1,0:T(8,128)S(1)}, f32[64,128]{1,0:T(8,128)S(1)}, u32[]{:S(2)}, u32[]{:S(2)}) %collective-permute-start.2) | collective-permute-done | bytes 32800 | tf_op jit(solution)/shard_map/ppermute | solution.py:39
  15.4 2.0 %collective-permute-start.3 = (f32[64,128]{1,0:T(8,128)S(1)}, f32[64,128]{1,0:T(8,128)S(1)}, u32[]{:S(2)}, u32[]{:S(2)}) collective-permute-start(f32[64,128]{1,0:T(8,128)S(1)} %add.73), channel_id=1, source_target_pairs={{0,1},{1,0},{2,3},{3,2},{4,5},{5,4},{6,7},{7,6},{8,9},{9,8},{10,11... | collective-permute-start | bytes 98312 | tf_op jit(solution)/shard_map/ppermute | solution.py:39
  17.4 1.9 %fusion.1 = f32[192,128]{1,0:T(8,128)S(1)} fusion(bf16[64,16384]{1,0:T(8,128)(2,1)S(1)} %get-tuple-element.20, bf16[64,16384]{1,0:T(8,128)(2,1)S(1)} %get-tuple-element.21, bf16[64,16384]{1,0:T(8,128)(2,1)S(1)} %get-tuple-element.19, s32[16384]{0:T(1024)S(1)} %get-tuple-element.17), kind=kOutput, calls=%fused_computation.2 | convolution fusion | flops 826277888 | bytes 6455296 | tf_op jit(solution)/shard_map/dot_general | solution.py:57
  19.4 4.1 %collective-permute-start.4 = (f32[64,128]{1,0:T(8,128)S(1)}, f32[64,128]{1,0:T(8,128)S(1)}, u32[]{:S(2)}, u32[]{:S(2)}) collective-permute-start(f32[64,128]{1,0:T(8,128)S(1)} %add.74), channel_id=1, source_target_pairs={{0,3},{1,2},{2,1},{3,0},{4,7},{5,6},{6,5},{7,4},{8,11},{9,10},{10,... | collective-permute-start | bytes 98312 | tf_op jit(solution)/shard_map/ppermute | solution.py:39
  23.4 1.9 %collective-permute-done.4 = f32[64,128]{1,0:T(8,128)S(1)} collective-permute-done((f32[64,128]{1,0:T(8,128)S(1)}, f32[64,128]{1,0:T(8,128)S(1)}, u32[]{:S(2)}, u32[]{:S(2)}) %collective-permute-start.4) | collective-permute-done | bytes 32800 | tf_op jit(solution)/shard_map/ppermute | solution.py:39
  25.3 0.6 add.75.joined_ref
  25.9 7.8 %shard_map.64 = f32[64,64]{1,0:T(8,128)} custom-call(f32[64,128]{1,0:T(8,128)} %add.75.joined_ref), custom_call_target="tpu_custom_call" | custom-call | tf_op jit(solution)/shard_map/pallas_call | solution.py:80
  33.7 1.0 %fusion.21 = f32[8,2,8,128]{3,2,1,0:T(8,128)S(1)} fusion(f32[64,64]{1,0:T(8,128)} %shard_map.64, f32[1,64,256]{2,1,0:T(8,128)S(1)} %copy-done, f32[1,64,256]{2,1,0:T(8,128)S(1)} %copy-done.1, f32[64]{0:T(128)S(1)} %copy-done.2), kind=kOutput, calls=%fused_computation.24 | convolution fusion | flops 12615680 | bytes 213248 | tf_op jit(solution)/shard_map/dot_general | solution.py:127
  34.8 1.1 %fusion.16 = (bf16[64,16384]{1,0:T(8,128)(2,1)S(1)}, bf16[64,16384]{1,0:T(8,128)(2,1)S(1)}, bf16[64,16384]{1,0:T(8,128)(2,1)S(1)}) fusion(s32[16384]{0:T(1024)S(1)} %get-tuple-element.18, bf16[16384]{0:T(1024)(128)(2,1)S(1)} %get-tuple-element.14, bf16[16384]{0:T(1024)(128)(2,1)S(1)} %get-tuple-element.15, bf16[16384]{0:T(1024)(128)(2,1)S(1)} %get-tuple-element.16), kind=kLoop, calls=%fused_computation.18 | loop fusion | flops 4194304 | bytes 6455296 | tf_op jit(solution)/shard_map/jit(_where)/select_n | solution.py:56
  35.9 1.9 %fusion = f32[192,128]{1,0:T(8,128)S(1)} fusion(bf16[64,16384]{1,0:T(8,128)(2,1)S(1)} %get-tuple-element.12, bf16[64,16384]{1,0:T(8,128)(2,1)S(1)} %get-tuple-element.13, bf16[64,16384]{1,0:T(8,128)(2,1)S(1)} %get-tuple-element.11, s32[16384]{0:T(1024)S(1)} %get-tuple-element.17), kind=kOutput, calls=%fused_computation.1 | convolution fusion | flops 826277888 | bytes 6455296 | tf_op jit(solution)/shard_map/dot_general | solution.py:57
  38.0 14.7 %all_to_all.9 = f32[16,1,1024]{2,1,0:T(1,128)S(1)} all-to-all(f32[16,1,1024]{2,1,0:T(1,128)S(1)} %all_to_all.6), channel_id=1, replica_groups=mesh['section'=8,'wafer'=4,'sub'=4] {'wafer','sub'}, dimensions={0} | all-to-all | bytes 131072 | tf_op jit(solution)/shard_map/all_to_all | solution.py:136
  52.8 1.2 %collective-permute-done.5 = f32[1024]{0:T(1024)S(1)} collective-permute-done((f32[1024]{0:T(1024)S(1)}, f32[1024]{0:T(1024)S(1)}, u32[]{:S(2)}, u32[]{:S(2)}) %collective-permute-start.5) | collective-permute-done | bytes 4128 | tf_op jit(solution)/shard_map/ppermute | solution.py:39
  54.0 0.3 collective-permute-start.6
  54.3 3.3 %collective-permute-done.6 = f32[1024]{0:T(1024)S(1)} collective-permute-done((f32[1024]{0:T(1024)S(1)}, f32[1024]{0:T(1024)S(1)}, u32[]{:S(2)}, u32[]{:S(2)}) %collective-permute-start.6) | collective-permute-done | bytes 4128 | tf_op jit(solution)/shard_map/ppermute | solution.py:39
  57.6 2.8 %collective-permute-start.7 = (f32[1024]{0:T(1024)S(1)}, f32[1024]{0:T(1024)S(1)}, u32[]{:S(2)}, u32[]{:S(2)}) collective-permute-start(f32[1024]{0:T(1024)S(1)} %add.84), channel_id=1, source_target_pairs={{0,96},{16,112},{32,64},{48,80},{64,32},{80,48},{96,0},{112,16},{1... | collective-permute-start | bytes 12296 | tf_op jit(solution)/shard_map/ppermute | solution.py:39
  60.4 2.1 %collective-permute-done.7 = f32[1024]{0:T(1024)S(1)} collective-permute-done((f32[1024]{0:T(1024)S(1)}, f32[1024]{0:T(1024)S(1)}, u32[]{:S(2)}, u32[]{:S(2)}) %collective-permute-start.7) | collective-permute-done | bytes 4128 | tf_op jit(solution)/shard_map/ppermute | solution.py:39
  62.4 0.6 maximum_divide_fusion
  (33 shorter events, 0.7 us)
Async XLA Ops:
  0.0 0.8 %copy-start = (f32[1,64,256]{2,1,0:T(8,128)S(1)}, f32[1,64,256]{2,1,0:T(8,128)}, u32[]{:S(2)}) copy-start(f32[1,64,256]{2,1,0:T(8,128)} %param.7) | copy-start | bytes 196612
  2.2 4.0 %collective-permute-start = (f32[64,128]{1,0:T(8,128)S(1)}, f32[64,128]{1,0:T(8,128)S(1)}, u32[]{:S(2)}, u32[]{:S(2)}) collective-permute-start(f32[64,128]{1,0:T(8,128)S(1)} %pad_maximum_fusion.1), channel_id=1, source_target_pairs={{0,16},{16,0},{32,48},{48,32},{64,80},{80,64},{96,112},{112,96},{1... | collective-permute-start | bytes 98312 | tf_op jit(solution)/shard_map/ppermute | solution.py:39
  6.3 3.9 %collective-permute-start.1 = (f32[64,128]{1,0:T(8,128)S(1)}, f32[64,128]{1,0:T(8,128)S(1)}, u32[]{:S(2)}, u32[]{:S(2)}) collective-permute-start(f32[64,128]{1,0:T(8,128)S(1)} %fusion.42), channel_id=1, source_target_pairs={{0,32},{16,48},{32,0},{48,16},{64,96},{80,112},{96,64},{112,80},{1... | collective-permute-start | bytes 98312 | tf_op jit(solution)/shard_map/ppermute | solution.py:39
  10.2 5.1 %collective-permute-start.2 = (f32[64,128]{1,0:T(8,128)S(1)}, f32[64,128]{1,0:T(8,128)S(1)}, u32[]{:S(2)}, u32[]{:S(2)}) collective-permute-start(f32[64,128]{1,0:T(8,128)S(1)} %add.72), channel_id=1, source_target_pairs={{0,96},{16,112},{32,64},{48,80},{64,32},{80,48},{96,0},{112,16},{1... | collective-permute-start | bytes 98312 | tf_op jit(solution)/shard_map/ppermute | solution.py:39
  15.4 4.0 %collective-permute-start.3 = (f32[64,128]{1,0:T(8,128)S(1)}, f32[64,128]{1,0:T(8,128)S(1)}, u32[]{:S(2)}, u32[]{:S(2)}) collective-permute-start(f32[64,128]{1,0:T(8,128)S(1)} %add.73), channel_id=1, source_target_pairs={{0,1},{1,0},{2,3},{3,2},{4,5},{5,4},{6,7},{7,6},{8,9},{9,8},{10,11... | collective-permute-start | bytes 98312 | tf_op jit(solution)/shard_map/ppermute | solution.py:39
  17.4 16.4 %copy-start.1 = (f32[1,64,256]{2,1,0:T(8,128)S(1)}, f32[1,64,256]{2,1,0:T(8,128)}, u32[]{:S(2)}) copy-start(f32[1,64,256]{2,1,0:T(8,128)} %param.6) | copy-start | bytes 196612
  17.4 16.4 %copy-start.2 = (f32[64]{0:T(128)S(1)}, f32[64]{0:T(128)}, u32[]{:S(2)}) copy-start(f32[64]{0:T(128)} %param.8) | copy-start | bytes 772
  19.4 6.0 %collective-permute-start.4 = (f32[64,128]{1,0:T(8,128)S(1)}, f32[64,128]{1,0:T(8,128)S(1)}, u32[]{:S(2)}, u32[]{:S(2)}) collective-permute-start(f32[64,128]{1,0:T(8,128)S(1)} %add.74), channel_id=1, source_target_pairs={{0,3},{1,2},{2,1},{3,0},{4,7},{5,6},{6,5},{7,4},{8,11},{9,10},{10,... | collective-permute-start | bytes 98312 | tf_op jit(solution)/shard_map/ppermute | solution.py:39
  52.7 1.2 %collective-permute-start.5 = (f32[1024]{0:T(1024)S(1)}, f32[1024]{0:T(1024)S(1)}, u32[]{:S(2)}, u32[]{:S(2)}) collective-permute-start(f32[1024]{0:T(1024)S(1)} %reduce_sum.19), channel_id=1, source_target_pairs={{0,16},{16,0},{32,48},{48,32},{64,80},{80,64},{96,112},{112,96},{1... | collective-permute-start | bytes 12296 | tf_op jit(solution)/shard_map/ppermute | solution.py:39
  54.0 3.6 %collective-permute-start.6 = (f32[1024]{0:T(1024)S(1)}, f32[1024]{0:T(1024)S(1)}, u32[]{:S(2)}, u32[]{:S(2)}) collective-permute-start(f32[1024]{0:T(1024)S(1)} %add.83), channel_id=1, source_target_pairs={{0,32},{16,48},{32,0},{48,16},{64,96},{80,112},{96,64},{112,80},{1... | collective-permute-start | bytes 12296 | tf_op jit(solution)/shard_map/ppermute | solution.py:39
  57.6 4.8 %collective-permute-start.7 = (f32[1024]{0:T(1024)S(1)}, f32[1024]{0:T(1024)S(1)}, u32[]{:S(2)}, u32[]{:S(2)}) collective-permute-start(f32[1024]{0:T(1024)S(1)} %add.84), channel_id=1, source_target_pairs={{0,96},{16,112},{32,64},{48,80},{64,32},{80,48},{96,0},{112,16},{1... | collective-permute-start | bytes 12296 | tf_op jit(solution)/shard_map/ppermute | solution.py:39

commit v9 on v8

--- a/solution.py
+++ b/solution.py
@@ -42,6 +42,15 @@
     return x, covered
 
 
+def all_sum_split(x, axes, cover):
+    rounds = [(axis, pairs) for axis in axes for pairs in partner_rounds(axis)]
+    for axis, pairs in rounds[:-1]:
+        x = x + lax.ppermute(x, axis, pairs)
+    axis, pairs = rounds[-1]
+    received = lax.ppermute(x, axis, pairs)
+    return lax.optimization_barrier((x, received, cover()))
+
+
 def split_bf16(x, parts):
     pieces = []
     for _ in range(parts):
@@ -51,18 +60,21 @@
     return pieces
 
 
-def bin_tiles(quantity, upper_hot, lower_hot, owners):
-    pieces = split_bf16(quantity.reshape(1, -1), 3)
+def bin_tiles(quantity, upper_hot, lower_hot, owners, parts):
+    pieces = split_bf16(quantity[None], parts)
     stacked = jnp.concatenate([jnp.where(upper_hot, p, jnp.bfloat16(0)) for p in pieces], axis=0)
     binned = lax.dot_general(
-        stacked, lower_hot, (((1,), (1,)), ((), ())), preferred_element_type=jnp.float32,
-    ).reshape(3, upper_hot.shape[0], 128)
-    return ((binned[0] + binned[1]) + binned[2]).reshape(owners, TILE)
+        stacked, lower_hot, (((1, 2), (1, 2)), ((), ())), preferred_element_type=jnp.float32,
+    ).reshape(parts, upper_hot.shape[0], 128)
+    total = binned[parts - 1]
+    for index in reversed(range(parts - 1)):
+        total = binned[index] + total
+    return total.reshape(owners, TILE)
 
 
-def solve_kernel(joined_ref, coef_ref):
-    n = joined_ref.shape[0]
-    m = joined_ref[...]
+def solve_kernel(own_ref, received_ref, coef_ref):
+    n = own_ref.shape[0]
+    m = own_ref[...] + received_ref[...]
     rows = lax.broadcasted_iota(jnp.int32, m.shape, 0)
     for k in range(n):
         row = m[k : k + 1, :]
@@ -75,14 +87,14 @@
     coef_ref[...] = m[:, n:] / diag
 
 
-def solve_fit(joined):
-    n = joined.shape[0]
+def solve_fit(own, received):
+    n = own.shape[0]
     return pl.pallas_call(
         solve_kernel,
-        out_shape=jax.ShapeDtypeStruct((n, joined.shape[1] - n), jnp.float32),
-        in_specs=[pl.BlockSpec(memory_space=pltpu.VMEM)],
+        out_shape=jax.ShapeDtypeStruct((n, own.shape[1] - n), jnp.float32),
+        in_specs=[pl.BlockSpec(memory_space=pltpu.VMEM)] * 2,
         out_specs=pl.BlockSpec(memory_space=pltpu.VMEM),
-    )(joined)
+    )(own, received)
 
 
 def filter_and_bin(tod, templates, det_weight, pixel, hitlist, counts):
@@ -101,10 +113,10 @@
     tile_of_sample = jnp.repeat(tile_of_block.reshape(dets, per_det), BL, axis=1)
 
     uppers = owners * (TILE // 128)
-    upper = jnp.where(tile_of_sample >= 0, tile_of_sample * (TILE // 128) + pixel[0] // 128, -1).reshape(1, -1)
-    lower = (pixel[0] % 128).reshape(1, -1)
-    upper_hot = lax.broadcasted_iota(jnp.int32, (uppers, upper.shape[1]), 0) == upper
-    lower_hot = (lax.broadcasted_iota(jnp.int32, (128, upper.shape[1]), 0) == lower).astype(jnp.bfloat16)
+    upper = jnp.where(tile_of_sample >= 0, tile_of_sample * (TILE // 128) + pixel[0] // 128, -1)[None]
+    lower = (pixel[0] % 128)[None]
+    upper_hot = lax.broadcasted_iota(jnp.int32, (uppers,) + upper.shape[1:], 0) == upper
+    lower_hot = (lax.broadcasted_iota(jnp.int32, (128,) + lower.shape[1:], 0) == lower).astype(jnp.bfloat16)
     sample_weight = jnp.broadcast_to(det_weight[:, None], tod.shape[1:])
     template_rows = templates[0]
     streams = tod[0]
@@ -117,13 +129,12 @@
         precision=HIGHEST, preferred_element_type=jnp.float32,
     )
     def weight_map():
-        return bin_tiles(sample_weight, upper_hot, lower_hot, owners)
+        return bin_tiles(sample_weight, upper_hot, lower_hot, owners, 3)
 
-    joined, wgt_part = all_sum(
-        jnp.concatenate([gram_sum, projection], axis=1), ("section", "sub"),
-        cover=weight_map, cover_round=5,
+    own, received, wgt_part = all_sum_split(
+        jnp.concatenate([gram_sum, projection], axis=1), ("section", "sub"), cover=weight_map
     )
-    coef_fit = solve_fit(joined)
+    coef_fit = solve_fit(own, received)
     removed = lax.dot_general(
         coef_fit, template_rows, (((0,), (0,)), ((), ())),
         precision=HIGHEST, preferred_element_type=jnp.float32,
@@ -131,7 +142,7 @@
     filtered = streams - removed
     weighted = filtered * det_weight[:, None]
 
-    num_part = bin_tiles(weighted, upper_hot, lower_hot, owners)
+    num_part = bin_tiles(weighted, upper_hot, lower_hot, owners, 2)
     partial = jnp.concatenate([num_part, wgt_part], axis=1)
     got = lax.all_to_all(partial, ("wafer", "sub"), split_axis=0, concat_axis=0, tiled=True)
     tile_sum, _ = all_sum(jnp.sum(got, axis=0), ("section",))

time: 63.5 us -> 62.7 us (0.987)
  other arithmetic: 5.37 us -> 6.67 us
  local copies, waits for them, and re-layouts: 3.17 us -> 2.17 us
  matrix products: 6.13 us -> 5.46 us
    ppermute x0 -> x5, starting transfers between devices: none -> 10.8 us  [the longest x4 6.56 us: all_sum_split(): x = x + lax.ppermute(x, axis, pairs)]
    ppermute x8 -> x3, starting transfers between devices: 13.7 us -> 3.12 us  [all_sum(): x = x + lax.ppermute(x, axis, pairs)]
    ppermute x8 -> x3, waiting for transfers between devices: 11.9 us -> 6.54 us  [all_sum(): x = x + lax.ppermute(x, axis, pairs)]
    ppermute x0 -> x5, waiting for transfers between devices: none -> 4.74 us  [the longest x4 2.87 us: all_sum_split(): x = x + lax.ppermute(x, axis, pairs)]
    unnamed x10, local copies, waits for them, and re-layouts: 2.53 us -> 1.46 us
    eq x0 -> x1, other arithmetic: none -> 0.91 us  [filter_and_bin(): lax.broadcasted_iota(jnp.int32, (uppers,) + upper.shape[1:], 0) == upper]
    add x8 -> x3, other arithmetic: 0.72 us -> 0.01 us  [all_sum(): x = x + lax.ppermute(x, axis, pairs)]
    dot_general x2, matrix products: 3.87 us -> 3.2 us  [bin_tiles(): lax.dot_general(stacked, lower_hot, (((1, 2), (1, 2)), ((), ())), preferr...]
  transfers between devices with their start and end apart: 8 -> 8, of which waited for: 6 -> 7; matrix products, arithmetic and copies ran while one was open for 11% -> 11% of each run, Pallas kernels for 0% -> 0%
where the time goes in v9:
time: 62.7 us; the launch traced here: 62.2 us
  blocking collectives  14.7 us (23%)
  starting transfers between devices  13.9 us (22%)
  waiting for transfers between devices  11.3 us (18%)
  Pallas kernels  7.83 us (12%)
  other arithmetic  6.67 us (11%)
  matrix products  5.46 us (9%)
  local copies, waits for them, and re-layouts  2.17 us (3%)
    all_to_all x1, blocking collectives, filter_and_bin(): lax.all_to_all(partial, ('wafer', 'sub'), split_axis=0, concat_axis=0, ti...  14.7 us
    pallas_call x1, Pallas kernels, solve_fit(): pl.pallas_call(solve_kernel, out_shape=jax.ShapeDtypeStruct((n, own.shape...  7.83 us
    ppermute x4, starting transfers between devices, all_sum_split(): x = x + lax.ppermute(x, axis, pairs)  6.56 us
    ppermute x3, waiting for transfers between devices, all_sum(): x = x + lax.ppermute(x, axis, pairs)  6.54 us
    ppermute x1, starting transfers between devices, all_sum_split(): received = lax.ppermute(x, axis, pairs)  4.22 us
    dot_general x2, matrix products, bin_tiles(): lax.dot_general(stacked, lower_hot, (((1, 2), (1, 2)), ((), ())), preferr...  3.2 us
    ppermute x3, starting transfers between devices, all_sum(): x = x + lax.ppermute(x, axis, pairs)  3.12 us
    ppermute x4, waiting for transfers between devices, all_sum_split(): x = x + lax.ppermute(x, axis, pairs)  2.87 us
  transfers between devices with their start and end apart: 8, of which 7 were waited for; matrix products, arithmetic and copies ran while one was open for 11% of the time, Pallas kernels for 0%

profile of v9, /device:TPU:0, one launch (start us, length us, event | category | flops | bytes accessed | tf_op | source)
XLA Modules:
  0.0 62.2 jit_solution(52427723129619659)
XLA Ops:
  0.0 0.8 %copy-done = f32[1,64,256]{2,1,0:T(8,128)S(1)} copy-done((f32[1,64,256]{2,1,0:T(8,128)S(1)}, f32[1,64,256]{2,1,0:T(8,128)}, u32[]{:S(2)}) %copy-start) | copy-done | bytes 65560
  0.8 0.2 fusion.36
  1.0 1.0 %fusion.34 = f32[64,64]{1,0:T(8,128)S(1)} fusion(f32[1,64,256]{2,1,0:T(8,128)S(1)} %copy-done, f32[1,64,256]{2,1,0:T(8,128)} %param.6), kind=kOutput, calls=%fused_computation.42 | convolution fusion | flops 12582912 | bytes 147456 | tf_op jit(solution)/shard_map/dot_general | solution.py:127
  2.2 0.7 %iota_compare_fusion.9 = pred[16,16]{1,0:T(8,128)(4,1)S(1)} fusion(s32[16]{0:T(128)} %bitcast.25), kind=kLoop, calls=%fused_computation.55 | loop fusion | flops 256 | bytes 320 | tf_op jit(solution)/shard_map/lt | solution.py:108
  2.9 0.8 %fusion.25 = (pred[16,128]{1,0:T(8,128)(4,1)S(1)}, pred[128]{0:T(512)(128)(4,1)S(1)}) fusion(s32[16,16]{1,0:T(8,128)} %bitcast.24, pred[16,16]{1,0:T(8,128)(4,1)S(1)} %iota_compare_fusion.9), kind=kLoop, calls=%fused_computation.25 | loop fusion | flops 128896 | bytes 3456 | tf_op jit(solution)/shard_map/reduce_or | solution.py:110
  3.8 0.1 mul.30
  4.0 0.1 broadcast_in_dim.60
  4.2 0.1 ge.24
  4.3 0.1 broadcast_in_dim.59
  4.5 0.9 %fusion.31 = (s32[64,256]{1,0:T(8,128)S(1)}, s32[64,256]{1,0:T(8,128)S(1)}) fusion(pred[1,64,256]{2,1,0:T(8,128)(4,1)S(1)} %ge.25, s32[1,64,256]{2,1,0:T(8,128)S(1)} %mul.31, s32[1,64,256]{2,1,0:T(8,128)} %param.9), kind=kLoop, calls=%fused_computation.38 | loop fusion | flops 344064 | bytes 278528 | tf_op jit(solution)/shard_map/eq | solution.py:118
  5.5 1.6 %collective-permute-start.1 = (f32[64,128]{1,0:T(8,128)S(1)}, f32[64,128]{1,0:T(8,128)S(1)}, u32[]{:S(2)}, u32[]{:S(2)}) collective-permute-start(f32[64,128]{1,0:T(8,128)S(1)} %fusion.47), channel_id=1, source_target_pairs={{0,32},{16,48},{32,0},{48,16},{64,96},{80,112},{96,64},{112,80},{1... | collective-permute-start | bytes 98312 | tf_op jit(solution)/shard_map/ppermute | solution.py:48
  7.2 0.7 %reduce-precision_convert_fusion.2 = (bf16[64]{0:T(256)(128)(2,1)S(1)}, bf16[64]{0:T(256)(128)(2,1)S(1)}, bf16[64]{0:T(256)(128)(2,1)S(1)}) fusion(f32[64]{0:T(128)} %param.8), kind=kLoop, calls=%fused_computation.60 | loop fusion | flops 512 | bytes 640 | tf_op jit(solution)/shard_map/convert_element_type | solution.py:58
  7.8 1.6 %collective-permute-done.1 = f32[64,128]{1,0:T(8,128)S(1)} collective-permute-done((f32[64,128]{1,0:T(8,128)S(1)}, f32[64,128]{1,0:T(8,128)S(1)}, u32[]{:S(2)}, u32[]{:S(2)}) %collective-permute-start.1) | collective-permute-done | bytes 32800 | tf_op jit(solution)/shard_map/ppermute | solution.py:48
  9.5 2.9 %collective-permute-start.2 = (f32[64,128]{1,0:T(8,128)S(1)}, f32[64,128]{1,0:T(8,128)S(1)}, u32[]{:S(2)}, u32[]{:S(2)}) collective-permute-start(f32[64,128]{1,0:T(8,128)S(1)} %add.55), channel_id=1, source_target_pairs={{0,96},{16,112},{32,64},{48,80},{64,32},{80,48},{96,0},{112,16},{1... | collective-permute-start | bytes 98312 | tf_op jit(solution)/shard_map/ppermute | solution.py:48
  12.4 1.1 %fusion.16 = (bf16[64,64,256]{2,0,1:T(8,128)(2,1)S(1)}, bf16[64,64,256]{2,0,1:T(8,128)(2,1)S(1)}, bf16[64,64,256]{2,0,1:T(8,128)(2,1)S(1)}) fusion(s32[64,256]{1,0:T(8,128)S(1)} %get-tuple-element.20, bf16[64]{0:T(256)(128)(2,1)S(1)} %get-tuple-element.22, bf16[64]{0:T(256)(128)(2,1)S(1)} %get-tuple-element.23, bf16[64]{0:T(256)(128)(2,1)S(1)} %get-tuple-element.24), kind=kLoop, calls=%fused_computation.18 | loop fusion | flops 4194304 | bytes 6357376 | tf_op jit(solution)/shard_map/jit(_where)/select_n | solution.py:65
  13.5 1.1 %collective-permute-done.2 = f32[64,128]{1,0:T(8,128)S(1)} collective-permute-done((f32[64,128]{1,0:T(8,128)S(1)}, f32[64,128]{1,0:T(8,128)S(1)}, u32[]{:S(2)}, u32[]{:S(2)}) %collective-permute-start.2) | collective-permute-done | bytes 32800 | tf_op jit(solution)/shard_map/ppermute | solution.py:48
  14.6 2.0 %collective-permute-start.3 = (f32[64,128]{1,0:T(8,128)S(1)}, f32[64,128]{1,0:T(8,128)S(1)}, u32[]{:S(2)}, u32[]{:S(2)}) collective-permute-start(f32[64,128]{1,0:T(8,128)S(1)} %add.56), channel_id=1, source_target_pairs={{0,1},{1,0},{2,3},{3,2},{4,5},{5,4},{6,7},{7,6},{8,9},{9,8},{10,11... | collective-permute-start | bytes 98312 | tf_op jit(solution)/shard_map/ppermute | solution.py:48
  16.6 1.8 %fusion.17 = f32[192,128]{1,0:T(8,128)S(1)} fusion(s32[64,256]{1,0:T(8,128)S(1)} %get-tuple-element.21, bf16[64,64,256]{2,0,1:T(8,128)(2,1)S(1)} %get-tuple-element.18, bf16[64,64,256]{2,0,1:T(8,128)(2,1)S(1)} %get-tuple-element.19, bf16[64,64,256]{2,0,1:T(8,128)(2,1)S(1)} %get-tuple-element.17), kind=kOutput, calls=%fused_computation.19 | convolution fusion | flops 826277888 | bytes 6455296 | tf_op jit(solution)/shard_map/dot_general | solution.py:66
  18.5 4.2 %collective-permute-start.4 = (f32[64,128]{1,0:T(8,128)S(1)}, f32[64,128]{1,0:T(8,128)S(1)}, u32[]{:S(2)}, u32[]{:S(2)}) collective-permute-start(f32[64,128]{1,0:T(8,128)S(1)} %add.57.own_ref), channel_id=1, source_target_pairs={{0,3},{1,2},{2,1},{3,0},{4,7},{5,6},{6,5},{7,4},{8,11},{9,10},{10,... | collective-permute-start | bytes 98312 | tf_op jit(solution)/shard_map/ppermute | solution.py:50
  22.8 1.9 %collective-permute-done.4.received_ref = f32[64,128]{1,0:T(8,128)S(1)} collective-permute-done((f32[64,128]{1,0:T(8,128)S(1)}, f32[64,128]{1,0:T(8,128)S(1)}, u32[]{:S(2)}, u32[]{:S(2)}) %collective-permute-start.4) | collective-permute-done | bytes 32800 | tf_op jit(solution)/shard_map/ppermute | solution.py:50
  24.7 0.6 copy-done.3
  25.3 7.8 %shard_map.64 = f32[64,64]{1,0:T(8,128)} custom-call(f32[64,128]{1,0:T(8,128)} %copy-done.2, f32[64,128]{1,0:T(8,128)} %copy-done.3), custom_call_target="tpu_custom_call" | custom-call | tf_op jit(solution)/shard_map/pallas_call | solution.py:92
  33.1 1.0 %reduce-precision_convert_fusion = (bf16[64,256]{1,0:T(8,128)(2,1)S(1)}, bf16[64,256]{1,0:T(8,128)(2,1)S(1)}) fusion(f32[64]{0:T(128)S(1)} %copy-done.4, f32[64,64]{1,0:T(8,128)} %shard_map.64, f32[1,64,256]{2,1,0:T(8,128)S(1)} %copy-done, f32[1,64,256]{2,1,0:T(8,128)S(1)} %copy-done.1), kind=kOutput, calls=%fused_computation.33 | convolution fusion | flops 12697600 | bytes 213248 | tf_op jit(solution)/shard_map/dot_general | solution.py:138
  34.1 1.5 %fusion.13 = (bf16[64,64,256]{2,0,1:T(8,128)(2,1)S(1)}, bf16[64,64,256]{2,0,1:T(8,128)(2,1)S(1)}) fusion(s32[64,256]{1,0:T(8,128)S(1)} %get-tuple-element.20, bf16[64,256]{1,0:T(8,128)(2,1)S(1)} %get-tuple-element.15, bf16[64,256]{1,0:T(8,128)(2,1)S(1)} %get-tuple-element.16), kind=kLoop, calls=%fused_computation.15 | loop fusion | flops 3145728 | bytes 4325376 | tf_op jit(solution)/shard_map/jit(_where)/select_n | solution.py:65
  35.7 1.4 %fusion.20 = f32[128,128]{1,0:T(8,128)S(1)} fusion(s32[64,256]{1,0:T(8,128)S(1)} %get-tuple-element.21, bf16[64,64,256]{2,0,1:T(8,128)(2,1)S(1)} %get-tuple-element.14, bf16[64,64,256]{2,0,1:T(8,128)(2,1)S(1)} %get-tuple-element.13), kind=kOutput, calls=%fused_computation.20 | convolution fusion | flops 547356672 | bytes 4325376 | tf_op jit(solution)/shard_map/dot_general | solution.py:66
  37.2 14.7 %all_to_all.9 = f32[16,1,1024]{2,1,0:T(1,128)S(1)} all-to-all(f32[16,1,1024]{2,1,0:T(1,128)S(1)} %all_to_all.6), channel_id=1, replica_groups=mesh['section'=8,'wafer'=4,'sub'=4] {'wafer','sub'}, dimensions={0} | all-to-all | bytes 131072 | tf_op jit(solution)/shard_map/all_to_all | solution.py:147
  52.0 1.2 %collective-permute-done.5 = f32[1024]{0:T(1024)S(1)} collective-permute-done((f32[1024]{0:T(1024)S(1)}, f32[1024]{0:T(1024)S(1)}, u32[]{:S(2)}, u32[]{:S(2)}) %collective-permute-start.5) | collective-permute-done | bytes 4128 | tf_op jit(solution)/shard_map/ppermute | solution.py:39
  53.2 0.3 collective-permute-start.6
  53.5 3.3 %collective-permute-done.6 = f32[1024]{0:T(1024)S(1)} collective-permute-done((f32[1024]{0:T(1024)S(1)}, f32[1024]{0:T(1024)S(1)}, u32[]{:S(2)}, u32[]{:S(2)}) %collective-permute-start.6) | collective-permute-done | bytes 4128 | tf_op jit(solution)/shard_map/ppermute | solution.py:39
  56.8 2.8 %collective-permute-start.7 = (f32[1024]{0:T(1024)S(1)}, f32[1024]{0:T(1024)S(1)}, u32[]{:S(2)}, u32[]{:S(2)}) collective-permute-start(f32[1024]{0:T(1024)S(1)} %add.65), channel_id=1, source_target_pairs={{0,96},{16,112},{32,64},{48,80},{64,32},{80,48},{96,0},{112,16},{1... | collective-permute-start | bytes 12296 | tf_op jit(solution)/shard_map/ppermute | solution.py:39
  59.6 2.1 %collective-permute-done.7 = f32[1024]{0:T(1024)S(1)} collective-permute-done((f32[1024]{0:T(1024)S(1)}, f32[1024]{0:T(1024)S(1)}, u32[]{:S(2)}, u32[]{:S(2)}) %collective-permute-start.7) | collective-permute-done | bytes 4128 | tf_op jit(solution)/shard_map/ppermute | solution.py:39
  61.6 0.6 maximum_divide_fusion
  (32 shorter events, 0.7 us)
Async XLA Ops:
  0.0 0.8 %copy-start = (f32[1,64,256]{2,1,0:T(8,128)S(1)}, f32[1,64,256]{2,1,0:T(8,128)}, u32[]{:S(2)}) copy-start(f32[1,64,256]{2,1,0:T(8,128)} %param.7) | copy-start | bytes 196612
  2.2 3.3 %collective-permute-start = (f32[64,128]{1,0:T(8,128)S(1)}, f32[64,128]{1,0:T(8,128)S(1)}, u32[]{:S(2)}, u32[]{:S(2)}) collective-permute-start(f32[64,128]{1,0:T(8,128)S(1)} %pad_maximum_fusion.1), channel_id=1, source_target_pairs={{0,16},{16,0},{32,48},{48,32},{64,80},{80,64},{96,112},{112,96},{1... | collective-permute-start | bytes 98312 | tf_op jit(solution)/shard_map/ppermute | solution.py:48
  5.5 3.9 %collective-permute-start.1 = (f32[64,128]{1,0:T(8,128)S(1)}, f32[64,128]{1,0:T(8,128)S(1)}, u32[]{:S(2)}, u32[]{:S(2)}) collective-permute-start(f32[64,128]{1,0:T(8,128)S(1)} %fusion.47), channel_id=1, source_target_pairs={{0,32},{16,48},{32,0},{48,16},{64,96},{80,112},{96,64},{112,80},{1... | collective-permute-start | bytes 98312 | tf_op jit(solution)/shard_map/ppermute | solution.py:48
  9.5 5.1 %collective-permute-start.2 = (f32[64,128]{1,0:T(8,128)S(1)}, f32[64,128]{1,0:T(8,128)S(1)}, u32[]{:S(2)}, u32[]{:S(2)}) collective-permute-start(f32[64,128]{1,0:T(8,128)S(1)} %add.55), channel_id=1, source_target_pairs={{0,96},{16,112},{32,64},{48,80},{64,32},{80,48},{96,0},{112,16},{1... | collective-permute-start | bytes 98312 | tf_op jit(solution)/shard_map/ppermute | solution.py:48
  14.6 3.9 %collective-permute-start.3 = (f32[64,128]{1,0:T(8,128)S(1)}, f32[64,128]{1,0:T(8,128)S(1)}, u32[]{:S(2)}, u32[]{:S(2)}) collective-permute-start(f32[64,128]{1,0:T(8,128)S(1)} %add.56), channel_id=1, source_target_pairs={{0,1},{1,0},{2,3},{3,2},{4,5},{5,4},{6,7},{7,6},{8,9},{9,8},{10,11... | collective-permute-start | bytes 98312 | tf_op jit(solution)/shard_map/ppermute | solution.py:48
  16.6 16.5 %copy-start.1 = (f32[1,64,256]{2,1,0:T(8,128)S(1)}, f32[1,64,256]{2,1,0:T(8,128)}, u32[]{:S(2)}) copy-start(f32[1,64,256]{2,1,0:T(8,128)} %param.6) | copy-start | bytes 196612
  16.6 16.5 %copy-start.4 = (f32[64]{0:T(128)S(1)}, f32[64]{0:T(128)}, u32[]{:S(2)}) copy-start(f32[64]{0:T(128)} %param.8) | copy-start | bytes 772
  18.5 6.1 %copy-start.2 = (f32[64,128]{1,0:T(8,128)}, f32[64,128]{1,0:T(8,128)S(1)}, u32[]{:S(2)}) copy-start(f32[64,128]{1,0:T(8,128)S(1)} %add.57.own_ref) | copy-start | bytes 98308
  18.5 6.1 %collective-permute-start.4 = (f32[64,128]{1,0:T(8,128)S(1)}, f32[64,128]{1,0:T(8,128)S(1)}, u32[]{:S(2)}, u32[]{:S(2)}) collective-permute-start(f32[64,128]{1,0:T(8,128)S(1)} %add.57.own_ref), channel_id=1, source_target_pairs={{0,3},{1,2},{2,1},{3,0},{4,7},{5,6},{6,5},{7,4},{8,11},{9,10},{10,... | collective-permute-start | bytes 98312 | tf_op jit(solution)/shard_map/ppermute | solution.py:50
  24.7 0.6 copy-start.3
  51.9 1.2 %collective-permute-start.5 = (f32[1024]{0:T(1024)S(1)}, f32[1024]{0:T(1024)S(1)}, u32[]{:S(2)}, u32[]{:S(2)}) collective-permute-start(f32[1024]{0:T(1024)S(1)} %reduce_sum.19), channel_id=1, source_target_pairs={{0,16},{16,0},{32,48},{48,32},{64,80},{80,64},{96,112},{112,96},{1... | collective-permute-start | bytes 12296 | tf_op jit(solution)/shard_map/ppermute | solution.py:39
  53.2 3.6 %collective-permute-start.6 = (f32[1024]{0:T(1024)S(1)}, f32[1024]{0:T(1024)S(1)}, u32[]{:S(2)}, u32[]{:S(2)}) collective-permute-start(f32[1024]{0:T(1024)S(1)} %add.64), channel_id=1, source_target_pairs={{0,32},{16,48},{32,0},{48,16},{64,96},{80,112},{96,64},{112,80},{1... | collective-permute-start | bytes 12296 | tf_op jit(solution)/shard_map/ppermute | solution.py:39
  56.8 4.8 %collective-permute-start.7 = (f32[1024]{0:T(1024)S(1)}, f32[1024]{0:T(1024)S(1)}, u32[]{:S(2)}, u32[]{:S(2)}) collective-permute-start(f32[1024]{0:T(1024)S(1)} %add.65), channel_id=1, source_target_pairs={{0,96},{16,112},{32,64},{48,80},{64,32},{80,48},{96,0},{112,16},{1... | collective-permute-start | bytes 12296 | tf_op jit(solution)/shard_map/ppermute | solution.py:39

commit v10 on v9

--- a/solution.py
+++ b/solution.py
@@ -61,10 +61,10 @@
 
 
 def bin_tiles(quantity, upper_hot, lower_hot, owners, parts):
-    pieces = split_bf16(quantity[None], parts)
+    pieces = split_bf16(quantity.reshape(1, -1), parts)
     stacked = jnp.concatenate([jnp.where(upper_hot, p, jnp.bfloat16(0)) for p in pieces], axis=0)
     binned = lax.dot_general(
-        stacked, lower_hot, (((1, 2), (1, 2)), ((), ())), preferred_element_type=jnp.float32,
+        stacked, lower_hot, (((1,), (1,)), ((), ())), preferred_element_type=jnp.float32,
     ).reshape(parts, upper_hot.shape[0], 128)
     total = binned[parts - 1]
     for index in reversed(range(parts - 1)):
@@ -113,10 +113,10 @@
     tile_of_sample = jnp.repeat(tile_of_block.reshape(dets, per_det), BL, axis=1)
 
     uppers = owners * (TILE // 128)
-    upper = jnp.where(tile_of_sample >= 0, tile_of_sample * (TILE // 128) + pixel[0] // 128, -1)[None]
-    lower = (pixel[0] % 128)[None]
-    upper_hot = lax.broadcasted_iota(jnp.int32, (uppers,) + upper.shape[1:], 0) == upper
-    lower_hot = (lax.broadcasted_iota(jnp.int32, (128,) + lower.shape[1:], 0) == lower).astype(jnp.bfloat16)
+    upper = jnp.where(tile_of_sample >= 0, tile_of_sample * (TILE // 128) + pixel[0] // 128, -1).reshape(1, -1)
+    lower = (pixel[0] % 128).reshape(1, -1)
+    upper_hot = lax.broadcasted_iota(jnp.int32, (uppers, upper.shape[1]), 0) == upper
+    lower_hot = (lax.broadcasted_iota(jnp.int32, (128, upper.shape[1]), 0) == lower).astype(jnp.bfloat16)
     sample_weight = jnp.broadcast_to(det_weight[:, None], tod.shape[1:])
     template_rows = templates[0]
     streams = tod[0]
@@ -129,7 +129,7 @@
         precision=HIGHEST, preferred_element_type=jnp.float32,
     )
     def weight_map():
-        return bin_tiles(sample_weight, upper_hot, lower_hot, owners, 3)
+        return bin_tiles(sample_weight, upper_hot, lower_hot, owners, 2)
 
     own, received, wgt_part = all_sum_split(
         jnp.concatenate([gram_sum, projection], axis=1), ("section", "sub"), cover=weight_map

time: 62.7 us -> 62.9 us (level)
  other arithmetic: 6.67 us -> 3.91 us
  local copies, waits for them, and re-layouts: 2.17 us -> 3.78 us
  waiting for transfers between devices: 11.3 us -> 12.5 us
    unnamed x10 -> x14, local copies, waits for them, and re-layouts: 1.46 us -> 3.14 us
    select_n x2, other arithmetic: 2.64 us -> 1.36 us  [bin_tiles(): jnp.where(upper_hot, p, jnp.bfloat16(0))]
    ppermute x4, waiting for transfers between devices: 2.87 us -> 4.1 us  [all_sum_split(): x = x + lax.ppermute(x, axis, pairs)]
    eq x1 -> x0, other arithmetic: 0.91 us -> none  [filter_and_bin(): lax.broadcasted_iota(jnp.int32, (uppers,) + upper.shape[1:], 0) == upper]
    convert_element_type x1 -> x2, other arithmetic: 0.66 us -> 0.02 us  [split_bf16(): pieces.append(head.astype(jnp.bfloat16))]
  transfers between devices with their start and end apart: 8 -> 8, of which waited for: 7 -> 7; matrix products, arithmetic and copies ran while one was open for 11% -> 10% of each run, Pallas kernels for 0% -> 0%
where the time goes in v10:
time: 62.9 us; the launch traced here: 62.4 us
  blocking collectives  14.7 us (23%)
  starting transfers between devices  13.9 us (22%)
  waiting for transfers between devices  12.5 us (20%)
  Pallas kernels  7.83 us (12%)
  matrix products  5.55 us (9%)
  other arithmetic  3.91 us (6%)
  local copies, waits for them, and re-layouts  3.78 us (6%)
    all_to_all x1, blocking collectives, filter_and_bin(): lax.all_to_all(partial, ('wafer', 'sub'), split_axis=0, concat_axis=0, ti...  14.7 us
    pallas_call x1, Pallas kernels, solve_fit(): pl.pallas_call(solve_kernel, out_shape=jax.ShapeDtypeStruct((n, own.shape...  7.83 us
    ppermute x4, starting transfers between devices, all_sum_split(): x = x + lax.ppermute(x, axis, pairs)  6.56 us
    ppermute x3, waiting for transfers between devices, all_sum(): x = x + lax.ppermute(x, axis, pairs)  6.55 us
    ppermute x1, starting transfers between devices, all_sum_split(): received = lax.ppermute(x, axis, pairs)  4.22 us
    ppermute x4, waiting for transfers between devices, all_sum_split(): x = x + lax.ppermute(x, axis, pairs)  4.1 us
    dot_general x2, matrix products, bin_tiles(): lax.dot_general(stacked, lower_hot, (((1,), (1,)), ((), ())), preferred_e...  3.29 us
    unnamed x14, local copies, waits for them, and re-layouts  3.14 us
  transfers between devices with their start and end apart: 8, of which 7 were waited for; matrix products, arithmetic and copies ran while one was open for 10% of the time, Pallas kernels for 0%

profile of v10, /device:TPU:0, one launch (start us, length us, event | category | flops | bytes accessed | tf_op | source)
XLA Modules:
  0.0 62.4 jit_solution(4125750560136581962)
XLA Ops:
  0.0 0.8 %copy-done = f32[1,64,256]{2,1,0:T(8,128)S(1)} copy-done((f32[1,64,256]{2,1,0:T(8,128)S(1)}, f32[1,64,256]{2,1,0:T(8,128)}, u32[]{:S(2)}) %copy-start) | copy-done | bytes 65560
  0.8 0.2 fusion.28
  1.0 1.0 %fusion.26 = f32[64,64]{1,0:T(8,128)S(1)} fusion(f32[1,64,256]{2,1,0:T(8,128)S(1)} %copy-done, f32[1,64,256]{2,1,0:T(8,128)} %param.6), kind=kOutput, calls=%fused_computation.40 | convolution fusion | flops 12582912 | bytes 147456 | tf_op jit(solution)/shard_map/dot_general | solution.py:127
  2.2 0.7 %iota_compare_fusion.5 = pred[16,16]{1,0:T(8,128)(4,1)S(1)} fusion(s32[16]{0:T(128)} %bitcast.29), kind=kLoop, calls=%fused_computation.53 | loop fusion | flops 256 | bytes 320 | tf_op jit(solution)/shard_map/lt | solution.py:108
  2.9 0.8 %fusion.17 = (pred[16,128]{1,0:T(8,128)(4,1)S(1)}, pred[128]{0:T(512)(128)(4,1)S(1)}) fusion(s32[16,16]{1,0:T(8,128)} %bitcast.28, pred[16,16]{1,0:T(8,128)(4,1)S(1)} %iota_compare_fusion.5), kind=kLoop, calls=%fused_computation.21 | loop fusion | flops 128896 | bytes 3456 | tf_op jit(solution)/shard_map/reduce_or | solution.py:110
  3.8 0.1 ge.21
  4.0 0.1 broadcast_in_dim.55
  4.2 0.1 mul.25
  4.3 0.9 %copy.7 = s32[8,2,8,128]{3,1,2,0:T(2,128)S(1)} copy(s32[8,2,8,128]{3,2,1,0:T(8,128)} %bitcast.27) | data formatting | bytes 131072
  5.4 0.7 %broadcast_bitcast_fusion = f32[8,2,8,128]{3,2,1,0:T(8,128)S(1)} fusion(f32[64]{0:T(128)} %param.8), kind=kLoop, calls=%fused_computation.51 | loop fusion | bytes 65792
  6.3 1.6 %collective-permute-start.1 = (f32[64,128]{1,0:T(8,128)S(1)}, f32[64,128]{1,0:T(8,128)S(1)}, u32[]{:S(2)}, u32[]{:S(2)}) collective-permute-start(f32[64,128]{1,0:T(8,128)S(1)} %fusion.36), channel_id=1, source_target_pairs={{0,32},{16,48},{32,0},{48,16},{64,96},{80,112},{96,64},{112,80},{1... | collective-permute-start | bytes 98312 | tf_op jit(solution)/shard_map/ppermute | solution.py:48
  7.9 2.3 %collective-permute-done.1 = f32[64,128]{1,0:T(8,128)S(1)} collective-permute-done((f32[64,128]{1,0:T(8,128)S(1)}, f32[64,128]{1,0:T(8,128)S(1)}, u32[]{:S(2)}, u32[]{:S(2)}) %collective-permute-start.1) | collective-permute-done | bytes 32800 | tf_op jit(solution)/shard_map/ppermute | solution.py:48
  10.2 2.9 %collective-permute-start.2 = (f32[64,128]{1,0:T(8,128)S(1)}, f32[64,128]{1,0:T(8,128)S(1)}, u32[]{:S(2)}, u32[]{:S(2)}) collective-permute-start(f32[64,128]{1,0:T(8,128)S(1)} %add.59), channel_id=1, source_target_pairs={{0,96},{16,112},{32,64},{48,80},{64,32},{80,48},{96,0},{112,16},{1... | collective-permute-start | bytes 98312 | tf_op jit(solution)/shard_map/ppermute | solution.py:48
  13.1 0.7 %fusion.13 = (bf16[64,16384]{1,0:T(8,128)(2,1)S(1)}, bf16[64,16384]{1,0:T(8,128)(2,1)S(1)}) fusion(s32[16384]{0:T(1024)S(1)} %get-tuple-element.18, bf16[16384]{0:T(1024)(128)(2,1)S(1)} %get-tuple-element.21, bf16[16384]{0:T(1024)(128)(2,1)S(1)} %get-tuple-element.22), kind=kLoop, calls=%fused_computation.15 | loop fusion | flops 3145728 | bytes 4325376 | tf_op jit(solution)/shard_map/jit(_where)/select_n | solution.py:65
  13.8 1.6 %collective-permute-done.2 = f32[64,128]{1,0:T(8,128)S(1)} collective-permute-done((f32[64,128]{1,0:T(8,128)S(1)}, f32[64,128]{1,0:T(8,128)S(1)}, u32[]{:S(2)}, u32[]{:S(2)}) %collective-permute-start.2) | collective-permute-done | bytes 32800 | tf_op jit(solution)/shard_map/ppermute | solution.py:48
  15.4 2.0 %collective-permute-start.3 = (f32[64,128]{1,0:T(8,128)S(1)}, f32[64,128]{1,0:T(8,128)S(1)}, u32[]{:S(2)}, u32[]{:S(2)}) collective-permute-start(f32[64,128]{1,0:T(8,128)S(1)} %add.60), channel_id=1, source_target_pairs={{0,1},{1,0},{2,3},{3,2},{4,5},{5,4},{6,7},{7,6},{8,9},{9,8},{10,11... | collective-permute-start | bytes 98312 | tf_op jit(solution)/shard_map/ppermute | solution.py:48
  17.4 1.6 %fusion.1 = f32[128,128]{1,0:T(8,128)S(1)} fusion(bf16[64,16384]{1,0:T(8,128)(2,1)S(1)} %get-tuple-element.20, bf16[64,16384]{1,0:T(8,128)(2,1)S(1)} %get-tuple-element.19, s32[16384]{0:T(1024)S(1)} %get-tuple-element.17), kind=kOutput, calls=%fused_computation.2 | convolution fusion | flops 547356672 | bytes 4325376 | tf_op jit(solution)/shard_map/dot_general | solution.py:66
  19.0 0.2 collective-permute-done.3
  19.3 4.2 %collective-permute-start.4 = (f32[64,128]{1,0:T(8,128)S(1)}, f32[64,128]{1,0:T(8,128)S(1)}, u32[]{:S(2)}, u32[]{:S(2)}) collective-permute-start(f32[64,128]{1,0:T(8,128)S(1)} %add.61.own_ref), channel_id=1, source_target_pairs={{0,3},{1,2},{2,1},{3,0},{4,7},{5,6},{6,5},{7,4},{8,11},{9,10},{10,... | collective-permute-start | bytes 98312 | tf_op jit(solution)/shard_map/ppermute | solution.py:50
  23.5 1.9 %collective-permute-done.4.received_ref = f32[64,128]{1,0:T(8,128)S(1)} collective-permute-done((f32[64,128]{1,0:T(8,128)S(1)}, f32[64,128]{1,0:T(8,128)S(1)}, u32[]{:S(2)}, u32[]{:S(2)}) %collective-permute-start.4) | collective-permute-done | bytes 32800 | tf_op jit(solution)/shard_map/ppermute | solution.py:50
  25.4 0.6 copy-done.3
  26.0 7.8 %shard_map.64 = f32[64,64]{1,0:T(8,128)} custom-call(f32[64,128]{1,0:T(8,128)} %copy-done.2, f32[64,128]{1,0:T(8,128)} %copy-done.3), custom_call_target="tpu_custom_call" | custom-call | tf_op jit(solution)/shard_map/pallas_call | solution.py:92
  33.9 1.0 %fusion.15 = f32[8,2,8,128]{3,2,1,0:T(8,128)S(1)} fusion(f32[64,64]{1,0:T(8,128)} %shard_map.64, f32[1,64,256]{2,1,0:T(8,128)S(1)} %copy-done, f32[1,64,256]{2,1,0:T(8,128)S(1)} %copy-done.1, f32[64]{0:T(128)S(1)} %copy-done.4), kind=kOutput, calls=%fused_computation.18 | convolution fusion | flops 12615680 | bytes 213248 | tf_op jit(solution)/shard_map/dot_general | solution.py:138
  34.9 0.7 %fusion.11 = (bf16[64,16384]{1,0:T(8,128)(2,1)S(1)}, bf16[64,16384]{1,0:T(8,128)(2,1)S(1)}) fusion(s32[16384]{0:T(1024)S(1)} %get-tuple-element.18, bf16[16384]{0:T(1024)(128)(2,1)S(1)} %get-tuple-element.15, bf16[16384]{0:T(1024)(128)(2,1)S(1)} %get-tuple-element.16), kind=kLoop, calls=%fused_computation.13 | loop fusion | flops 3145728 | bytes 4325376 | tf_op jit(solution)/shard_map/jit(_where)/select_n | solution.py:65
  35.6 1.6 %fusion = f32[128,128]{1,0:T(8,128)S(1)} fusion(bf16[64,16384]{1,0:T(8,128)(2,1)S(1)} %get-tuple-element.14, bf16[64,16384]{1,0:T(8,128)(2,1)S(1)} %get-tuple-element.13, s32[16384]{0:T(1024)S(1)} %get-tuple-element.17), kind=kOutput, calls=%fused_computation.1 | convolution fusion | flops 547356672 | bytes 4325376 | tf_op jit(solution)/shard_map/dot_general | solution.py:66
  37.4 14.7 %all_to_all.9 = f32[16,1,1024]{2,1,0:T(1,128)S(1)} all-to-all(f32[16,1,1024]{2,1,0:T(1,128)S(1)} %all_to_all.6), channel_id=1, replica_groups=mesh['section'=8,'wafer'=4,'sub'=4] {'wafer','sub'}, dimensions={0} | all-to-all | bytes 131072 | tf_op jit(solution)/shard_map/all_to_all | solution.py:147
  52.2 1.2 %collective-permute-done.5 = f32[1024]{0:T(1024)S(1)} collective-permute-done((f32[1024]{0:T(1024)S(1)}, f32[1024]{0:T(1024)S(1)}, u32[]{:S(2)}, u32[]{:S(2)}) %collective-permute-start.5) | collective-permute-done | bytes 4128 | tf_op jit(solution)/shard_map/ppermute | solution.py:39
  53.4 0.3 collective-permute-start.6
  53.7 3.3 %collective-permute-done.6 = f32[1024]{0:T(1024)S(1)} collective-permute-done((f32[1024]{0:T(1024)S(1)}, f32[1024]{0:T(1024)S(1)}, u32[]{:S(2)}, u32[]{:S(2)}) %collective-permute-start.6) | collective-permute-done | bytes 4128 | tf_op jit(solution)/shard_map/ppermute | solution.py:39
  57.0 2.8 %collective-permute-start.7 = (f32[1024]{0:T(1024)S(1)}, f32[1024]{0:T(1024)S(1)}, u32[]{:S(2)}, u32[]{:S(2)}) collective-permute-start(f32[1024]{0:T(1024)S(1)} %add.68), channel_id=1, source_target_pairs={{0,96},{16,112},{32,64},{48,80},{64,32},{80,48},{96,0},{112,16},{1... | collective-permute-start | bytes 12296 | tf_op jit(solution)/shard_map/ppermute | solution.py:39
  59.8 2.1 %collective-permute-done.7 = f32[1024]{0:T(1024)S(1)} collective-permute-done((f32[1024]{0:T(1024)S(1)}, f32[1024]{0:T(1024)S(1)}, u32[]{:S(2)}, u32[]{:S(2)}) %collective-permute-start.7) | collective-permute-done | bytes 4128 | tf_op jit(solution)/shard_map/ppermute | solution.py:39
  61.8 0.6 maximum_divide_fusion
  (36 shorter events, 0.8 us)
Async XLA Ops:
  0.0 0.8 %copy-start = (f32[1,64,256]{2,1,0:T(8,128)S(1)}, f32[1,64,256]{2,1,0:T(8,128)}, u32[]{:S(2)}) copy-start(f32[1,64,256]{2,1,0:T(8,128)} %param.7) | copy-start | bytes 196612
  2.2 4.0 %collective-permute-start = (f32[64,128]{1,0:T(8,128)S(1)}, f32[64,128]{1,0:T(8,128)S(1)}, u32[]{:S(2)}, u32[]{:S(2)}) collective-permute-start(f32[64,128]{1,0:T(8,128)S(1)} %pad_maximum_fusion.1), channel_id=1, source_target_pairs={{0,16},{16,0},{32,48},{48,32},{64,80},{80,64},{96,112},{112,96},{1... | collective-permute-start | bytes 98312 | tf_op jit(solution)/shard_map/ppermute | solution.py:48
  6.3 3.9 %collective-permute-start.1 = (f32[64,128]{1,0:T(8,128)S(1)}, f32[64,128]{1,0:T(8,128)S(1)}, u32[]{:S(2)}, u32[]{:S(2)}) collective-permute-start(f32[64,128]{1,0:T(8,128)S(1)} %fusion.36), channel_id=1, source_target_pairs={{0,32},{16,48},{32,0},{48,16},{64,96},{80,112},{96,64},{112,80},{1... | collective-permute-start | bytes 98312 | tf_op jit(solution)/shard_map/ppermute | solution.py:48
  10.2 5.1 %collective-permute-start.2 = (f32[64,128]{1,0:T(8,128)S(1)}, f32[64,128]{1,0:T(8,128)S(1)}, u32[]{:S(2)}, u32[]{:S(2)}) collective-permute-start(f32[64,128]{1,0:T(8,128)S(1)} %add.59), channel_id=1, source_target_pairs={{0,96},{16,112},{32,64},{48,80},{64,32},{80,48},{96,0},{112,16},{1... | collective-permute-start | bytes 98312 | tf_op jit(solution)/shard_map/ppermute | solution.py:48
  15.4 3.9 %collective-permute-start.3 = (f32[64,128]{1,0:T(8,128)S(1)}, f32[64,128]{1,0:T(8,128)S(1)}, u32[]{:S(2)}, u32[]{:S(2)}) collective-permute-start(f32[64,128]{1,0:T(8,128)S(1)} %add.60), channel_id=1, source_target_pairs={{0,1},{1,0},{2,3},{3,2},{4,5},{5,4},{6,7},{7,6},{8,9},{9,8},{10,11... | collective-permute-start | bytes 98312 | tf_op jit(solution)/shard_map/ppermute | solution.py:48
  17.4 16.5 %copy-start.1 = (f32[1,64,256]{2,1,0:T(8,128)S(1)}, f32[1,64,256]{2,1,0:T(8,128)}, u32[]{:S(2)}) copy-start(f32[1,64,256]{2,1,0:T(8,128)} %param.6) | copy-start | bytes 196612
  17.4 16.5 %copy-start.4 = (f32[64]{0:T(128)S(1)}, f32[64]{0:T(128)}, u32[]{:S(2)}) copy-start(f32[64]{0:T(128)} %param.8) | copy-start | bytes 772
  19.3 6.1 %copy-start.2 = (f32[64,128]{1,0:T(8,128)}, f32[64,128]{1,0:T(8,128)S(1)}, u32[]{:S(2)}) copy-start(f32[64,128]{1,0:T(8,128)S(1)} %add.61.own_ref) | copy-start | bytes 98308
  19.3 6.1 %collective-permute-start.4 = (f32[64,128]{1,0:T(8,128)S(1)}, f32[64,128]{1,0:T(8,128)S(1)}, u32[]{:S(2)}, u32[]{:S(2)}) collective-permute-start(f32[64,128]{1,0:T(8,128)S(1)} %add.61.own_ref), channel_id=1, source_target_pairs={{0,3},{1,2},{2,1},{3,0},{4,7},{5,6},{6,5},{7,4},{8,11},{9,10},{10,... | collective-permute-start | bytes 98312 | tf_op jit(solution)/shard_map/ppermute | solution.py:50
  25.4 0.6 copy-start.3
  52.1 1.2 %collective-permute-start.5 = (f32[1024]{0:T(1024)S(1)}, f32[1024]{0:T(1024)S(1)}, u32[]{:S(2)}, u32[]{:S(2)}) collective-permute-start(f32[1024]{0:T(1024)S(1)} %reduce_sum.19), channel_id=1, source_target_pairs={{0,16},{16,0},{32,48},{48,32},{64,80},{80,64},{96,112},{112,96},{1... | collective-permute-start | bytes 12296 | tf_op jit(solution)/shard_map/ppermute | solution.py:39
  53.4 3.6 %collective-permute-start.6 = (f32[1024]{0:T(1024)S(1)}, f32[1024]{0:T(1024)S(1)}, u32[]{:S(2)}, u32[]{:S(2)}) collective-permute-start(f32[1024]{0:T(1024)S(1)} %add.67), channel_id=1, source_target_pairs={{0,32},{16,48},{32,0},{48,16},{64,96},{80,112},{96,64},{112,80},{1... | collective-permute-start | bytes 12296 | tf_op jit(solution)/shard_map/ppermute | solution.py:39
  57.0 4.8 %collective-permute-start.7 = (f32[1024]{0:T(1024)S(1)}, f32[1024]{0:T(1024)S(1)}, u32[]{:S(2)}, u32[]{:S(2)}) collective-permute-start(f32[1024]{0:T(1024)S(1)} %add.68), channel_id=1, source_target_pairs={{0,96},{16,112},{32,64},{48,80},{64,32},{80,48},{96,0},{112,16},{1... | collective-permute-start | bytes 12296 | tf_op jit(solution)/shard_map/ppermute | solution.py:39

commit v11 on v10

--- a/solution.py
+++ b/solution.py
@@ -129,7 +129,7 @@
         precision=HIGHEST, preferred_element_type=jnp.float32,
     )
     def weight_map():
-        return bin_tiles(sample_weight, upper_hot, lower_hot, owners, 2)
+        return bin_tiles(sample_weight, upper_hot, lower_hot, owners, 3)
 
     own, received, wgt_part = all_sum_split(
         jnp.concatenate([gram_sum, projection], axis=1), ("section", "sub"), cover=weight_map
@@ -144,8 +144,9 @@
 
     num_part = bin_tiles(weighted, upper_hot, lower_hot, owners, 2)
     partial = jnp.concatenate([num_part, wgt_part], axis=1)
-    got = lax.all_to_all(partial, ("wafer", "sub"), split_axis=0, concat_axis=0, tiled=True)
-    tile_sum, _ = all_sum(jnp.sum(got, axis=0), ("section",))
+    section_sum, _ = all_sum(partial, ("section",))
+    got = lax.all_to_all(section_sum, ("wafer", "sub"), split_axis=0, concat_axis=0, tiled=True)
+    tile_sum = jnp.sum(got, axis=0)
     num_tile, wgt_tile = tile_sum[:TILE], tile_sum[TILE:]
     return num_tile / jnp.maximum(wgt_tile, 1.0)
 

time: 62.9 us -> 64.5 us (1.025)
  waiting for transfers between devices: 12.5 us -> 13.3 us
    ppermute x3, waiting for transfers between devices: 6.55 us -> 7.95 us  [all_sum(): x = x + lax.ppermute(x, axis, pairs)]
    ppermute x4, waiting for transfers between devices: 4.1 us -> 3.45 us  [all_sum_split(): x = x + lax.ppermute(x, axis, pairs)]
    unnamed x14 -> x15, local copies, waits for them, and re-layouts: 3.14 us -> 3.14 us
  transfers between devices with their start and end apart: 8 -> 8, of which waited for: 7 -> 6; matrix products, arithmetic and copies ran while one was open for 10% -> 11% of each run, Pallas kernels for 0% -> 0%
where the time goes in v11:
time: 64.5 us; the launch traced here: 64 us
  blocking collectives  14.7 us (23%)
  starting transfers between devices  14 us (22%)
  waiting for transfers between devices  13.3 us (21%)
  Pallas kernels  7.83 us (12%)
  matrix products  5.84 us (9%)
  other arithmetic  4.35 us (7%)
  local copies, waits for them, and re-layouts  3.79 us (6%)
    all_to_all x1, blocking collectives, filter_and_bin(): lax.all_to_all(section_sum, ('wafer', 'sub'), split_axis=0, concat_axis=0...  14.7 us
    ppermute x3, waiting for transfers between devices, all_sum(): x = x + lax.ppermute(x, axis, pairs)  7.95 us
    pallas_call x1, Pallas kernels, solve_fit(): pl.pallas_call(solve_kernel, out_shape=jax.ShapeDtypeStruct((n, own.shape...  7.83 us
    ppermute x4, starting transfers between devices, all_sum_split(): x = x + lax.ppermute(x, axis, pairs)  6.56 us
    ppermute x1, starting transfers between devices, all_sum_split(): received = lax.ppermute(x, axis, pairs)  4.14 us
    dot_general x2, matrix products, bin_tiles(): lax.dot_general(stacked, lower_hot, (((1,), (1,)), ((), ())), preferred_e...  3.59 us
    ppermute x4, waiting for transfers between devices, all_sum_split(): x = x + lax.ppermute(x, axis, pairs)  3.45 us
    ppermute x3, starting transfers between devices, all_sum(): x = x + lax.ppermute(x, axis, pairs)  3.28 us
  transfers between devices with their start and end apart: 8, of which 6 were waited for; matrix products, arithmetic and copies ran while one was open for 11% of the time, Pallas kernels for 0%

profile of v11, /device:TPU:0, one launch (start us, length us, event | category | flops | bytes accessed | tf_op | source)
XLA Modules:
  0.0 64.0 jit_solution(3490727023818016566)
XLA Ops:
  0.0 0.8 %copy-done = f32[1,64,256]{2,1,0:T(8,128)S(1)} copy-done((f32[1,64,256]{2,1,0:T(8,128)S(1)}, f32[1,64,256]{2,1,0:T(8,128)}, u32[]{:S(2)}) %copy-start) | copy-done | bytes 65560
  0.8 0.2 fusion.31
  1.0 1.0 %fusion.29 = f32[64,64]{1,0:T(8,128)S(1)} fusion(f32[1,64,256]{2,1,0:T(8,128)S(1)} %copy-done, f32[1,64,256]{2,1,0:T(8,128)} %param.6), kind=kOutput, calls=%fused_computation.44 | convolution fusion | flops 12582912 | bytes 147456 | tf_op jit(solution)/shard_map/dot_general | solution.py:127
  2.2 0.7 %iota_compare_fusion.5 = pred[16,16]{1,0:T(8,128)(4,1)S(1)} fusion(s32[16]{0:T(128)} %bitcast.29), kind=kLoop, calls=%fused_computation.58 | loop fusion | flops 256 | bytes 320 | tf_op jit(solution)/shard_map/lt | solution.py:108
  2.9 0.8 %fusion.20 = (pred[16,128]{1,0:T(8,128)(4,1)S(1)}, pred[128]{0:T(512)(128)(4,1)S(1)}) fusion(s32[16,16]{1,0:T(8,128)} %bitcast.28, pred[16,16]{1,0:T(8,128)(4,1)S(1)} %iota_compare_fusion.5), kind=kLoop, calls=%fused_computation.24 | loop fusion | flops 128896 | bytes 3456 | tf_op jit(solution)/shard_map/reduce_or | solution.py:110
  3.8 0.1 mul.25
  4.0 0.2 ge.21
  4.1 0.1 broadcast_in_dim.61
  4.3 0.9 %copy.7 = s32[8,2,8,128]{3,1,2,0:T(2,128)S(1)} copy(s32[8,2,8,128]{3,2,1,0:T(8,128)} %bitcast.27) | data formatting | bytes 131072
  5.2 0.1 broadcast_in_dim.62
  5.4 0.7 %broadcast_bitcast_fusion = f32[8,2,8,128]{3,2,1,0:T(8,128)S(1)} fusion(f32[64]{0:T(128)} %param.8), kind=kLoop, calls=%fused_computation.56 | loop fusion | bytes 65792
  6.3 1.6 %collective-permute-start.1 = (f32[64,128]{1,0:T(8,128)S(1)}, f32[64,128]{1,0:T(8,128)S(1)}, u32[]{:S(2)}, u32[]{:S(2)}) collective-permute-start(f32[64,128]{1,0:T(8,128)S(1)} %fusion.40), channel_id=1, source_target_pairs={{0,32},{16,48},{32,0},{48,16},{64,96},{80,112},{96,64},{112,80},{1... | collective-permute-start | bytes 98312 | tf_op jit(solution)/shard_map/ppermute | solution.py:48
  7.9 2.3 %collective-permute-done.1 = f32[64,128]{1,0:T(8,128)S(1)} collective-permute-done((f32[64,128]{1,0:T(8,128)S(1)}, f32[64,128]{1,0:T(8,128)S(1)}, u32[]{:S(2)}, u32[]{:S(2)}) %collective-permute-start.1) | collective-permute-done | bytes 32800 | tf_op jit(solution)/shard_map/ppermute | solution.py:48
  10.2 2.9 %collective-permute-start.2 = (f32[64,128]{1,0:T(8,128)S(1)}, f32[64,128]{1,0:T(8,128)S(1)}, u32[]{:S(2)}, u32[]{:S(2)}) collective-permute-start(f32[64,128]{1,0:T(8,128)S(1)} %add.64), channel_id=1, source_target_pairs={{0,96},{16,112},{32,64},{48,80},{64,32},{80,48},{96,0},{112,16},{1... | collective-permute-start | bytes 98312 | tf_op jit(solution)/shard_map/ppermute | solution.py:48
  13.1 1.1 %fusion.16 = (bf16[64,16384]{1,0:T(8,128)(2,1)S(1)}, bf16[64,16384]{1,0:T(8,128)(2,1)S(1)}, bf16[64,16384]{1,0:T(8,128)(2,1)S(1)}) fusion(s32[16384]{0:T(1024)S(1)} %get-tuple-element.18, bf16[16384]{0:T(1024)(128)(2,1)S(1)} %get-tuple-element.22, bf16[16384]{0:T(1024)(128)(2,1)S(1)} %get-tuple-element.23, bf16[16384]{0:T(1024)(128)(2,1)S(1)} %get-tuple-element.24), kind=kLoop, calls=%fused_computation.18 | loop fusion | flops 4194304 | bytes 6455296 | tf_op jit(solution)/shard_map/jit(_where)/select_n | solution.py:65
  14.2 1.2 %collective-permute-done.2 = f32[64,128]{1,0:T(8,128)S(1)} collective-permute-done((f32[64,128]{1,0:T(8,128)S(1)}, f32[64,128]{1,0:T(8,128)S(1)}, u32[]{:S(2)}, u32[]{:S(2)}) %collective-permute-start.2) | collective-permute-done | bytes 32800 | tf_op jit(solution)/shard_map/ppermute | solution.py:48
  15.4 2.0 %collective-permute-start.3 = (f32[64,128]{1,0:T(8,128)S(1)}, f32[64,128]{1,0:T(8,128)S(1)}, u32[]{:S(2)}, u32[]{:S(2)}) collective-permute-start(f32[64,128]{1,0:T(8,128)S(1)} %add.65), channel_id=1, source_target_pairs={{0,1},{1,0},{2,3},{3,2},{4,5},{5,4},{6,7},{7,6},{8,9},{9,8},{10,11... | collective-permute-start | bytes 98312 | tf_op jit(solution)/shard_map/ppermute | solution.py:48
  17.4 1.9 %fusion.1 = f32[192,128]{1,0:T(8,128)S(1)} fusion(bf16[64,16384]{1,0:T(8,128)(2,1)S(1)} %get-tuple-element.20, bf16[64,16384]{1,0:T(8,128)(2,1)S(1)} %get-tuple-element.21, bf16[64,16384]{1,0:T(8,128)(2,1)S(1)} %get-tuple-element.19, s32[16384]{0:T(1024)S(1)} %get-tuple-element.17), kind=kOutput, calls=%fused_computation.2 | convolution fusion | flops 826277888 | bytes 6455296 | tf_op jit(solution)/shard_map/dot_general | solution.py:66
  19.4 4.1 %collective-permute-start.4 = (f32[64,128]{1,0:T(8,128)S(1)}, f32[64,128]{1,0:T(8,128)S(1)}, u32[]{:S(2)}, u32[]{:S(2)}) collective-permute-start(f32[64,128]{1,0:T(8,128)S(1)} %add.66.own_ref), channel_id=1, source_target_pairs={{0,3},{1,2},{2,1},{3,0},{4,7},{5,6},{6,5},{7,4},{8,11},{9,10},{10,... | collective-permute-start | bytes 98312 | tf_op jit(solution)/shard_map/ppermute | solution.py:50
  23.5 1.9 %collective-permute-done.4.received_ref = f32[64,128]{1,0:T(8,128)S(1)} collective-permute-done((f32[64,128]{1,0:T(8,128)S(1)}, f32[64,128]{1,0:T(8,128)S(1)}, u32[]{:S(2)}, u32[]{:S(2)}) %collective-permute-start.4) | collective-permute-done | bytes 32800 | tf_op jit(solution)/shard_map/ppermute | solution.py:50
  25.4 0.6 copy-done.3
  26.0 7.8 %shard_map.64 = f32[64,64]{1,0:T(8,128)} custom-call(f32[64,128]{1,0:T(8,128)} %copy-done.2, f32[64,128]{1,0:T(8,128)} %copy-done.3), custom_call_target="tpu_custom_call" | custom-call | tf_op jit(solution)/shard_map/pallas_call | solution.py:92
  33.9 1.0 %fusion.18 = f32[8,2,8,128]{3,2,1,0:T(8,128)S(1)} fusion(f32[64,64]{1,0:T(8,128)} %shard_map.64, f32[1,64,256]{2,1,0:T(8,128)S(1)} %copy-done, f32[1,64,256]{2,1,0:T(8,128)S(1)} %copy-done.1, f32[64]{0:T(128)S(1)} %copy-done.4), kind=kOutput, calls=%fused_computation.21 | convolution fusion | flops 12615680 | bytes 213248 | tf_op jit(solution)/shard_map/dot_general | solution.py:138
  34.9 0.7 %fusion.13 = (bf16[64,16384]{1,0:T(8,128)(2,1)S(1)}, bf16[64,16384]{1,0:T(8,128)(2,1)S(1)}) fusion(s32[16384]{0:T(1024)S(1)} %get-tuple-element.18, bf16[16384]{0:T(1024)(128)(2,1)S(1)} %get-tuple-element.15, bf16[16384]{0:T(1024)(128)(2,1)S(1)} %get-tuple-element.16), kind=kLoop, calls=%fused_computation.15 | loop fusion | flops 3145728 | bytes 4325376 | tf_op jit(solution)/shard_map/jit(_where)/select_n | solution.py:65
  35.6 1.7 %fusion = f32[128,128]{1,0:T(8,128)S(1)} fusion(bf16[64,16384]{1,0:T(8,128)(2,1)S(1)} %get-tuple-element.14, bf16[64,16384]{1,0:T(8,128)(2,1)S(1)} %get-tuple-element.13, s32[16384]{0:T(1024)S(1)} %get-tuple-element.17), kind=kOutput, calls=%fused_computation.1 | convolution fusion | flops 547356672 | bytes 4325376 | tf_op jit(solution)/shard_map/dot_general | solution.py:66
  37.4 1.2 %collective-permute-done.5 = f32[16,1024]{1,0:T(8,128)S(1)} collective-permute-done((f32[16,1024]{1,0:T(8,128)S(1)}, f32[16,1024]{1,0:T(8,128)S(1)}, u32[]{:S(2)}, u32[]{:S(2)}) %collective-permute-start.5) | collective-permute-done | bytes 65568 | tf_op jit(solution)/shard_map/ppermute | solution.py:39
  38.7 0.4 collective-permute-start.6
  39.0 4.0 %collective-permute-done.6 = f32[16,1024]{1,0:T(8,128)S(1)} collective-permute-done((f32[16,1024]{1,0:T(8,128)S(1)}, f32[16,1024]{1,0:T(8,128)S(1)}, u32[]{:S(2)}, u32[]{:S(2)}) %collective-permute-start.6) | collective-permute-done | bytes 65568 | tf_op jit(solution)/shard_map/ppermute | solution.py:39
  43.0 2.8 %collective-permute-start.7 = (f32[16,1024]{1,0:T(8,128)S(1)}, f32[16,1024]{1,0:T(8,128)S(1)}, u32[]{:S(2)}, u32[]{:S(2)}) collective-permute-start(f32[16,1024]{1,0:T(8,128)S(1)} %add.74), channel_id=1, source_target_pairs={{0,96},{16,112},{32,64},{48,80},{64,32},{80,48},{96,0},{112,16},{1... | collective-permute-start | bytes 196616 | tf_op jit(solution)/shard_map/ppermute | solution.py:39
  45.9 2.7 %collective-permute-done.7 = f32[16,1024]{1,0:T(8,128)S(1)} collective-permute-done((f32[16,1024]{1,0:T(8,128)S(1)}, f32[16,1024]{1,0:T(8,128)S(1)}, u32[]{:S(2)}, u32[]{:S(2)}) %collective-permute-start.7) | collective-permute-done | bytes 65568 | tf_op jit(solution)/shard_map/ppermute | solution.py:39
  48.7 14.7 %all_to_all.9 = f32[16,1,1024]{2,1,0:T(1,128)S(1)} all-to-all(f32[16,1,1024]{2,1,0:T(1,128)S(1)} %all_to_all.6), channel_id=1, replica_groups=mesh['section'=8,'wafer'=4,'sub'=4] {'wafer','sub'}, dimensions={0} | all-to-all | bytes 131072 | tf_op jit(solution)/shard_map/all_to_all | solution.py:148
  63.4 0.6 maximum_divide_fusion
  (37 shorter events, 0.7 us)
Async XLA Ops:
  0.0 0.8 %copy-start = (f32[1,64,256]{2,1,0:T(8,128)S(1)}, f32[1,64,256]{2,1,0:T(8,128)}, u32[]{:S(2)}) copy-start(f32[1,64,256]{2,1,0:T(8,128)} %param.7) | copy-start | bytes 196612
  2.2 4.0 %collective-permute-start = (f32[64,128]{1,0:T(8,128)S(1)}, f32[64,128]{1,0:T(8,128)S(1)}, u32[]{:S(2)}, u32[]{:S(2)}) collective-permute-start(f32[64,128]{1,0:T(8,128)S(1)} %pad_maximum_fusion), channel_id=1, source_target_pairs={{0,16},{16,0},{32,48},{48,32},{64,80},{80,64},{96,112},{112,96},{1... | collective-permute-start | bytes 98312 | tf_op jit(solution)/shard_map/ppermute | solution.py:48
  6.3 3.9 %collective-permute-start.1 = (f32[64,128]{1,0:T(8,128)S(1)}, f32[64,128]{1,0:T(8,128)S(1)}, u32[]{:S(2)}, u32[]{:S(2)}) collective-permute-start(f32[64,128]{1,0:T(8,128)S(1)} %fusion.40), channel_id=1, source_target_pairs={{0,32},{16,48},{32,0},{48,16},{64,96},{80,112},{96,64},{112,80},{1... | collective-permute-start | bytes 98312 | tf_op jit(solution)/shard_map/ppermute | solution.py:48
  10.2 5.1 %collective-permute-start.2 = (f32[64,128]{1,0:T(8,128)S(1)}, f32[64,128]{1,0:T(8,128)S(1)}, u32[]{:S(2)}, u32[]{:S(2)}) collective-permute-start(f32[64,128]{1,0:T(8,128)S(1)} %add.64), channel_id=1, source_target_pairs={{0,96},{16,112},{32,64},{48,80},{64,32},{80,48},{96,0},{112,16},{1... | collective-permute-start | bytes 98312 | tf_op jit(solution)/shard_map/ppermute | solution.py:48
  15.4 4.0 %collective-permute-start.3 = (f32[64,128]{1,0:T(8,128)S(1)}, f32[64,128]{1,0:T(8,128)S(1)}, u32[]{:S(2)}, u32[]{:S(2)}) collective-permute-start(f32[64,128]{1,0:T(8,128)S(1)} %add.65), channel_id=1, source_target_pairs={{0,1},{1,0},{2,3},{3,2},{4,5},{5,4},{6,7},{7,6},{8,9},{9,8},{10,11... | collective-permute-start | bytes 98312 | tf_op jit(solution)/shard_map/ppermute | solution.py:48
  17.4 16.5 %copy-start.1 = (f32[1,64,256]{2,1,0:T(8,128)S(1)}, f32[1,64,256]{2,1,0:T(8,128)}, u32[]{:S(2)}) copy-start(f32[1,64,256]{2,1,0:T(8,128)} %param.6) | copy-start | bytes 196612
  17.4 16.5 %copy-start.4 = (f32[64]{0:T(128)S(1)}, f32[64]{0:T(128)}, u32[]{:S(2)}) copy-start(f32[64]{0:T(128)} %param.8) | copy-start | bytes 772
  19.4 6.0 %copy-start.2 = (f32[64,128]{1,0:T(8,128)}, f32[64,128]{1,0:T(8,128)S(1)}, u32[]{:S(2)}) copy-start(f32[64,128]{1,0:T(8,128)S(1)} %add.66.own_ref) | copy-start | bytes 98308
  19.4 6.0 %collective-permute-start.4 = (f32[64,128]{1,0:T(8,128)S(1)}, f32[64,128]{1,0:T(8,128)S(1)}, u32[]{:S(2)}, u32[]{:S(2)}) collective-permute-start(f32[64,128]{1,0:T(8,128)S(1)} %add.66.own_ref), channel_id=1, source_target_pairs={{0,3},{1,2},{2,1},{3,0},{4,7},{5,6},{6,5},{7,4},{8,11},{9,10},{10,... | collective-permute-start | bytes 98312 | tf_op jit(solution)/shard_map/ppermute | solution.py:50
  25.4 0.6 copy-start.3
  37.3 1.3 %collective-permute-start.5 = (f32[16,1024]{1,0:T(8,128)S(1)}, f32[16,1024]{1,0:T(8,128)S(1)}, u32[]{:S(2)}, u32[]{:S(2)}) collective-permute-start(f32[16,1024]{1,0:T(8,128)S(1)} %constant_dynamic-update-slice_fusion), channel_id=1, source_target_pairs={{0,16},{16,0},{32,48},{48,32},{64,80},{80,64},{96,112},{112,96},{1... | collective-permute-start | bytes 196616 | tf_op jit(solution)/shard_map/ppermute | solution.py:39
  38.7 4.3 %collective-permute-start.6 = (f32[16,1024]{1,0:T(8,128)S(1)}, f32[16,1024]{1,0:T(8,128)S(1)}, u32[]{:S(2)}, u32[]{:S(2)}) collective-permute-start(f32[16,1024]{1,0:T(8,128)S(1)} %add.73), channel_id=1, source_target_pairs={{0,32},{16,48},{32,0},{48,16},{64,96},{80,112},{96,64},{112,80},{1... | collective-permute-start | bytes 196616 | tf_op jit(solution)/shard_map/ppermute | solution.py:39
  43.0 5.6 %collective-permute-start.7 = (f32[16,1024]{1,0:T(8,128)S(1)}, f32[16,1024]{1,0:T(8,128)S(1)}, u32[]{:S(2)}, u32[]{:S(2)}) collective-permute-start(f32[16,1024]{1,0:T(8,128)S(1)} %add.74), channel_id=1, source_target_pairs={{0,96},{16,112},{32,64},{48,80},{64,32},{80,48},{96,0},{112,16},{1... | collective-permute-start | bytes 196616 | tf_op jit(solution)/shard_map/ppermute | solution.py:39

commit v12 on v10

--- a/solution.py
+++ b/solution.py
@@ -30,8 +30,10 @@
             bit *= 2
 
 
-def all_sum(x, axes, cover=None, cover_round=0):
+def all_sum(x, axes, cover=None, cover_round=0, chips_first=False):
     rounds = [(axis, pairs) for axis in axes for pairs in partner_rounds(axis)]
+    if chips_first and axes == ("section",):
+        rounds = rounds[1:] + rounds[:1]
     covered = None
     for index, (axis, pairs) in enumerate(rounds):
         if cover is not None and index == cover_round:
@@ -129,7 +131,7 @@
         precision=HIGHEST, preferred_element_type=jnp.float32,
     )
     def weight_map():
-        return bin_tiles(sample_weight, upper_hot, lower_hot, owners, 2)
+        return bin_tiles(sample_weight, upper_hot, lower_hot, owners, 3)
 
     own, received, wgt_part = all_sum_split(
         jnp.concatenate([gram_sum, projection], axis=1), ("section", "sub"), cover=weight_map
@@ -145,7 +147,7 @@
     num_part = bin_tiles(weighted, upper_hot, lower_hot, owners, 2)
     partial = jnp.concatenate([num_part, wgt_part], axis=1)
     got = lax.all_to_all(partial, ("wafer", "sub"), split_axis=0, concat_axis=0, tiled=True)
-    tile_sum, _ = all_sum(jnp.sum(got, axis=0), ("section",))
+    tile_sum, _ = all_sum(jnp.sum(got, axis=0), ("section",), chips_first=True)
     num_tile, wgt_tile = tile_sum[:TILE], tile_sum[TILE:]
     return num_tile / jnp.maximum(wgt_tile, 1.0)
 

time: 62.9 us -> 63.9 us (1.016)
  the two profiles are of different devices: /device:TPU:0 before, /device:TPU:1 now
where the time goes in v12:
time: 63.9 us; the launch traced here: 63.5 us
  starting transfers between devices  20.7 us (32%)
  blocking collectives  13 us (20%)
  Pallas kernels  7.83 us (12%)
  waiting for transfers between devices  7.75 us (12%)
  matrix products  5.84 us (9%)
  other arithmetic  4.33 us (7%)
  local copies, waits for them, and re-layouts  3.78 us (6%)
    all_to_all x1, blocking collectives, filter_and_bin(): lax.all_to_all(partial, ('wafer', 'sub'), split_axis=0, concat_axis=0, ti...  13 us
    ppermute x3, starting transfers between devices, all_sum(): x = x + lax.ppermute(x, axis, pairs)  10.6 us
    pallas_call x1, Pallas kernels, solve_fit(): pl.pallas_call(solve_kernel, out_shape=jax.ShapeDtypeStruct((n, own.shape...  7.83 us
    ppermute x4, starting transfers between devices, all_sum_split(): x = x + lax.ppermute(x, axis, pairs)  7.09 us
    ppermute x3, waiting for transfers between devices, all_sum(): x = x + lax.ppermute(x, axis, pairs)  4.75 us
    dot_general x2, matrix products, bin_tiles(): lax.dot_general(stacked, lower_hot, (((1,), (1,)), ((), ())), preferred_e...  3.58 us
    unnamed x14, local copies, waits for them, and re-layouts  3.13 us
    ppermute x1, starting transfers between devices, all_sum_split(): received = lax.ppermute(x, axis, pairs)  2.99 us
  transfers between devices with their start and end apart: 8, of which 6 were waited for; matrix products, arithmetic and copies ran while one was open for 11% of the time, Pallas kernels for 0%

profile of v12, /device:TPU:1, one launch (start us, length us, event | category | flops | bytes accessed | tf_op | source)
XLA Modules:
  0.0 63.5 jit_solution(4398379631742240724)
XLA Ops:
  0.0 0.8 %copy-done = f32[1,64,256]{2,1,0:T(8,128)S(1)} copy-done((f32[1,64,256]{2,1,0:T(8,128)S(1)}, f32[1,64,256]{2,1,0:T(8,128)}, u32[]{:S(2)}) %copy-start) | copy-done | bytes 65560
  0.8 0.2 fusion.31
  1.0 1.0 %fusion.29 = f32[64,64]{1,0:T(8,128)S(1)} fusion(f32[1,64,256]{2,1,0:T(8,128)S(1)} %copy-done, f32[1,64,256]{2,1,0:T(8,128)} %param.6), kind=kOutput, calls=%fused_computation.45 | convolution fusion | flops 12582912 | bytes 147456 | tf_op jit(solution)/shard_map/dot_general | solution.py:129
  2.2 1.4 %collective-permute-start = (f32[64,128]{1,0:T(8,128)S(1)}, f32[64,128]{1,0:T(8,128)S(1)}, u32[]{:S(2)}, u32[]{:S(2)}) collective-permute-start(f32[64,128]{1,0:T(8,128)S(1)} %pad_maximum_fusion.1), channel_id=1, source_target_pairs={{0,16},{16,0},{32,48},{48,32},{64,80},{80,64},{96,112},{112,96},{1... | collective-permute-start | bytes 98312 | tf_op jit(solution)/shard_map/ppermute | solution.py:50
  3.6 0.7 %iota_compare_fusion.5 = pred[16,16]{1,0:T(8,128)(4,1)S(1)} fusion(s32[16]{0:T(128)} %bitcast.29), kind=kLoop, calls=%fused_computation.59 | loop fusion | flops 256 | bytes 320 | tf_op jit(solution)/shard_map/lt | solution.py:110
  4.3 0.8 %fusion.20 = (pred[16,128]{1,0:T(8,128)(4,1)S(1)}, pred[128]{0:T(512)(128)(4,1)S(1)}) fusion(s32[16,16]{1,0:T(8,128)} %bitcast.28, pred[16,16]{1,0:T(8,128)(4,1)S(1)} %iota_compare_fusion.5), kind=kLoop, calls=%fused_computation.24 | loop fusion | flops 128896 | bytes 3456 | tf_op jit(solution)/shard_map/reduce_or | solution.py:112
  5.2 0.1 mul.25
  5.3 0.2 ge.21
  5.5 0.1 broadcast_in_dim.61
  5.7 0.9 %copy.7 = s32[8,2,8,128]{3,1,2,0:T(2,128)S(1)} copy(s32[8,2,8,128]{3,2,1,0:T(8,128)} %bitcast.27) | data formatting | bytes 131072
  6.8 0.7 %broadcast_bitcast_fusion = f32[8,2,8,128]{3,2,1,0:T(8,128)S(1)} fusion(f32[64]{0:T(128)} %param.8), kind=kLoop, calls=%fused_computation.57 | loop fusion | bytes 65792
  7.6 1.3 %collective-permute-start.1 = (f32[64,128]{1,0:T(8,128)S(1)}, f32[64,128]{1,0:T(8,128)S(1)}, u32[]{:S(2)}, u32[]{:S(2)}) collective-permute-start(f32[64,128]{1,0:T(8,128)S(1)} %fusion.40), channel_id=1, source_target_pairs={{0,32},{16,48},{32,0},{48,16},{64,96},{80,112},{96,64},{112,80},{1... | collective-permute-start | bytes 98312 | tf_op jit(solution)/shard_map/ppermute | solution.py:50
  9.0 1.4 %collective-permute-done.1 = f32[64,128]{1,0:T(8,128)S(1)} collective-permute-done((f32[64,128]{1,0:T(8,128)S(1)}, f32[64,128]{1,0:T(8,128)S(1)}, u32[]{:S(2)}, u32[]{:S(2)}) %collective-permute-start.1) | collective-permute-done | bytes 32800 | tf_op jit(solution)/shard_map/ppermute | solution.py:50
  10.4 2.6 %collective-permute-start.2 = (f32[64,128]{1,0:T(8,128)S(1)}, f32[64,128]{1,0:T(8,128)S(1)}, u32[]{:S(2)}, u32[]{:S(2)}) collective-permute-start(f32[64,128]{1,0:T(8,128)S(1)} %add.64), channel_id=1, source_target_pairs={{0,96},{16,112},{32,64},{48,80},{64,32},{80,48},{96,0},{112,16},{1... | collective-permute-start | bytes 98312 | tf_op jit(solution)/shard_map/ppermute | solution.py:50
  13.0 1.1 %fusion.16 = (bf16[64,16384]{1,0:T(8,128)(2,1)S(1)}, bf16[64,16384]{1,0:T(8,128)(2,1)S(1)}, bf16[64,16384]{1,0:T(8,128)(2,1)S(1)}) fusion(s32[16384]{0:T(1024)S(1)} %get-tuple-element.18, bf16[16384]{0:T(1024)(128)(2,1)S(1)} %get-tuple-element.22, bf16[16384]{0:T(1024)(128)(2,1)S(1)} %get-tuple-element.23, bf16[16384]{0:T(1024)(128)(2,1)S(1)} %get-tuple-element.24), kind=kLoop, calls=%fused_computation.18 | loop fusion | flops 4194304 | bytes 6455296 | tf_op jit(solution)/shard_map/jit(_where)/select_n | solution.py:67
  14.1 0.3 collective-permute-done.2
  14.4 1.7 %collective-permute-start.3 = (f32[64,128]{1,0:T(8,128)S(1)}, f32[64,128]{1,0:T(8,128)S(1)}, u32[]{:S(2)}, u32[]{:S(2)}) collective-permute-start(f32[64,128]{1,0:T(8,128)S(1)} %add.65), channel_id=1, source_target_pairs={{0,1},{1,0},{2,3},{3,2},{4,5},{5,4},{6,7},{7,6},{8,9},{9,8},{10,11... | collective-permute-start | bytes 98312 | tf_op jit(solution)/shard_map/ppermute | solution.py:50
  16.2 1.9 %fusion.1 = f32[192,128]{1,0:T(8,128)S(1)} fusion(bf16[64,16384]{1,0:T(8,128)(2,1)S(1)} %get-tuple-element.20, bf16[64,16384]{1,0:T(8,128)(2,1)S(1)} %get-tuple-element.21, bf16[64,16384]{1,0:T(8,128)(2,1)S(1)} %get-tuple-element.19, s32[16384]{0:T(1024)S(1)} %get-tuple-element.17), kind=kOutput, calls=%fused_computation.2 | convolution fusion | flops 826277888 | bytes 6455296 | tf_op jit(solution)/shard_map/dot_general | solution.py:68
  18.2 3.0 %collective-permute-start.4 = (f32[64,128]{1,0:T(8,128)S(1)}, f32[64,128]{1,0:T(8,128)S(1)}, u32[]{:S(2)}, u32[]{:S(2)}) collective-permute-start(f32[64,128]{1,0:T(8,128)S(1)} %add.66.own_ref), channel_id=1, source_target_pairs={{0,3},{1,2},{2,1},{3,0},{4,7},{5,6},{6,5},{7,4},{8,11},{9,10},{10,... | collective-permute-start | bytes 98312 | tf_op jit(solution)/shard_map/ppermute | solution.py:52
  21.2 1.3 %collective-permute-done.4.received_ref = f32[64,128]{1,0:T(8,128)S(1)} collective-permute-done((f32[64,128]{1,0:T(8,128)S(1)}, f32[64,128]{1,0:T(8,128)S(1)}, u32[]{:S(2)}, u32[]{:S(2)}) %collective-permute-start.4) | collective-permute-done | bytes 32800 | tf_op jit(solution)/shard_map/ppermute | solution.py:52
  22.5 0.6 copy-done.3
  23.1 7.8 %shard_map.64 = f32[64,64]{1,0:T(8,128)} custom-call(f32[64,128]{1,0:T(8,128)} %copy-done.2, f32[64,128]{1,0:T(8,128)} %copy-done.3), custom_call_target="tpu_custom_call" | custom-call | tf_op jit(solution)/shard_map/pallas_call | solution.py:94
  30.9 1.0 %fusion.18 = f32[8,2,8,128]{3,2,1,0:T(8,128)S(1)} fusion(f32[64,64]{1,0:T(8,128)} %shard_map.64, f32[1,64,256]{2,1,0:T(8,128)S(1)} %copy-done, f32[1,64,256]{2,1,0:T(8,128)S(1)} %copy-done.1, f32[64]{0:T(128)S(1)} %copy-done.4), kind=kOutput, calls=%fused_computation.21 | convolution fusion | flops 12615680 | bytes 213248 | tf_op jit(solution)/shard_map/dot_general | solution.py:140
  32.0 0.7 %fusion.13 = (bf16[64,16384]{1,0:T(8,128)(2,1)S(1)}, bf16[64,16384]{1,0:T(8,128)(2,1)S(1)}) fusion(s32[16384]{0:T(1024)S(1)} %get-tuple-element.18, bf16[16384]{0:T(1024)(128)(2,1)S(1)} %get-tuple-element.15, bf16[16384]{0:T(1024)(128)(2,1)S(1)} %get-tuple-element.16), kind=kLoop, calls=%fused_computation.15 | loop fusion | flops 3145728 | bytes 4325376 | tf_op jit(solution)/shard_map/jit(_where)/select_n | solution.py:67
  32.7 1.6 %fusion = f32[128,128]{1,0:T(8,128)S(1)} fusion(bf16[64,16384]{1,0:T(8,128)(2,1)S(1)} %get-tuple-element.14, bf16[64,16384]{1,0:T(8,128)(2,1)S(1)} %get-tuple-element.13, s32[16384]{0:T(1024)S(1)} %get-tuple-element.17), kind=kOutput, calls=%fused_computation.1 | convolution fusion | flops 547356672 | bytes 4325376 | tf_op jit(solution)/shard_map/dot_general | solution.py:68
  34.4 13.0 %all_to_all.9 = f32[16,1,1024]{2,1,0:T(1,128)S(1)} all-to-all(f32[16,1,1024]{2,1,0:T(1,128)S(1)} %all_to_all.6), channel_id=1, replica_groups=mesh['section'=8,'wafer'=4,'sub'=4] {'wafer','sub'}, dimensions={0} | all-to-all | bytes 131072 | tf_op jit(solution)/shard_map/all_to_all | solution.py:149
  47.6 2.7 %collective-permute-done.5 = f32[1024]{0:T(1024)S(1)} collective-permute-done((f32[1024]{0:T(1024)S(1)}, f32[1024]{0:T(1024)S(1)}, u32[]{:S(2)}, u32[]{:S(2)}) %collective-permute-start.5) | collective-permute-done | bytes 4128 | tf_op jit(solution)/shard_map/ppermute | solution.py:41
  50.3 2.5 %collective-permute-start.6 = (f32[1024]{0:T(1024)S(1)}, f32[1024]{0:T(1024)S(1)}, u32[]{:S(2)}, u32[]{:S(2)}) collective-permute-start(f32[1024]{0:T(1024)S(1)} %add.73), channel_id=1, source_target_pairs={{0,96},{16,112},{32,64},{48,80},{64,32},{80,48},{96,0},{112,16},{1... | collective-permute-start | bytes 12296 | tf_op jit(solution)/shard_map/ppermute | solution.py:41
  52.8 1.2 %collective-permute-done.6 = f32[1024]{0:T(1024)S(1)} collective-permute-done((f32[1024]{0:T(1024)S(1)}, f32[1024]{0:T(1024)S(1)}, u32[]{:S(2)}, u32[]{:S(2)}) %collective-permute-start.6) | collective-permute-done | bytes 4128 | tf_op jit(solution)/shard_map/ppermute | solution.py:41
  54.0 8.0 %collective-permute-start.7 = (f32[1024]{0:T(1024)S(1)}, f32[1024]{0:T(1024)S(1)}, u32[]{:S(2)}, u32[]{:S(2)}) collective-permute-start(f32[1024]{0:T(1024)S(1)} %add.74), channel_id=1, source_target_pairs={{0,16},{16,0},{32,48},{48,32},{64,80},{80,64},{96,112},{112,96},{1... | collective-permute-start | bytes 12296 | tf_op jit(solution)/shard_map/ppermute | solution.py:41
  62.0 0.8 %collective-permute-done.7 = f32[1024]{0:T(1024)S(1)} collective-permute-done((f32[1024]{0:T(1024)S(1)}, f32[1024]{0:T(1024)S(1)}, u32[]{:S(2)}, u32[]{:S(2)}) %collective-permute-start.7) | collective-permute-done | bytes 4128 | tf_op jit(solution)/shard_map/ppermute | solution.py:41
  62.9 0.6 maximum_divide_fusion
  (36 shorter events, 0.8 us)
Async XLA Ops:
  0.0 0.8 %copy-start = (f32[1,64,256]{2,1,0:T(8,128)S(1)}, f32[1,64,256]{2,1,0:T(8,128)}, u32[]{:S(2)}) copy-start(f32[1,64,256]{2,1,0:T(8,128)} %param.7) | copy-start | bytes 196612
  2.2 5.4 %collective-permute-start = (f32[64,128]{1,0:T(8,128)S(1)}, f32[64,128]{1,0:T(8,128)S(1)}, u32[]{:S(2)}, u32[]{:S(2)}) collective-permute-start(f32[64,128]{1,0:T(8,128)S(1)} %pad_maximum_fusion.1), channel_id=1, source_target_pairs={{0,16},{16,0},{32,48},{48,32},{64,80},{80,64},{96,112},{112,96},{1... | collective-permute-start | bytes 98312 | tf_op jit(solution)/shard_map/ppermute | solution.py:50
  7.6 2.8 %collective-permute-start.1 = (f32[64,128]{1,0:T(8,128)S(1)}, f32[64,128]{1,0:T(8,128)S(1)}, u32[]{:S(2)}, u32[]{:S(2)}) collective-permute-start(f32[64,128]{1,0:T(8,128)S(1)} %fusion.40), channel_id=1, source_target_pairs={{0,32},{16,48},{32,0},{48,16},{64,96},{80,112},{96,64},{112,80},{1... | collective-permute-start | bytes 98312 | tf_op jit(solution)/shard_map/ppermute | solution.py:50
  10.4 4.0 %collective-permute-start.2 = (f32[64,128]{1,0:T(8,128)S(1)}, f32[64,128]{1,0:T(8,128)S(1)}, u32[]{:S(2)}, u32[]{:S(2)}) collective-permute-start(f32[64,128]{1,0:T(8,128)S(1)} %add.64), channel_id=1, source_target_pairs={{0,96},{16,112},{32,64},{48,80},{64,32},{80,48},{96,0},{112,16},{1... | collective-permute-start | bytes 98312 | tf_op jit(solution)/shard_map/ppermute | solution.py:50
  14.4 3.7 %collective-permute-start.3 = (f32[64,128]{1,0:T(8,128)S(1)}, f32[64,128]{1,0:T(8,128)S(1)}, u32[]{:S(2)}, u32[]{:S(2)}) collective-permute-start(f32[64,128]{1,0:T(8,128)S(1)} %add.65), channel_id=1, source_target_pairs={{0,1},{1,0},{2,3},{3,2},{4,5},{5,4},{6,7},{7,6},{8,9},{9,8},{10,11... | collective-permute-start | bytes 98312 | tf_op jit(solution)/shard_map/ppermute | solution.py:50
  16.2 14.7 %copy-start.1 = (f32[1,64,256]{2,1,0:T(8,128)S(1)}, f32[1,64,256]{2,1,0:T(8,128)}, u32[]{:S(2)}) copy-start(f32[1,64,256]{2,1,0:T(8,128)} %param.6) | copy-start | bytes 196612
  16.2 14.7 %copy-start.4 = (f32[64]{0:T(128)S(1)}, f32[64]{0:T(128)}, u32[]{:S(2)}) copy-start(f32[64]{0:T(128)} %param.8) | copy-start | bytes 772
  18.1 4.3 %copy-start.2 = (f32[64,128]{1,0:T(8,128)}, f32[64,128]{1,0:T(8,128)S(1)}, u32[]{:S(2)}) copy-start(f32[64,128]{1,0:T(8,128)S(1)} %add.66.own_ref) | copy-start | bytes 98308
  18.2 4.3 %collective-permute-start.4 = (f32[64,128]{1,0:T(8,128)S(1)}, f32[64,128]{1,0:T(8,128)S(1)}, u32[]{:S(2)}, u32[]{:S(2)}) collective-permute-start(f32[64,128]{1,0:T(8,128)S(1)} %add.66.own_ref), channel_id=1, source_target_pairs={{0,3},{1,2},{2,1},{3,0},{4,7},{5,6},{6,5},{7,4},{8,11},{9,10},{10,... | collective-permute-start | bytes 98312 | tf_op jit(solution)/shard_map/ppermute | solution.py:52
  22.5 0.6 copy-start.3
  47.5 2.8 %collective-permute-start.5 = (f32[1024]{0:T(1024)S(1)}, f32[1024]{0:T(1024)S(1)}, u32[]{:S(2)}, u32[]{:S(2)}) collective-permute-start(f32[1024]{0:T(1024)S(1)} %reduce_sum.19), channel_id=1, source_target_pairs={{0,32},{16,48},{32,0},{48,16},{64,96},{80,112},{96,64},{112,80},{1... | collective-permute-start | bytes 12296 | tf_op jit(solution)/shard_map/ppermute | solution.py:41
  50.3 3.7 %collective-permute-start.6 = (f32[1024]{0:T(1024)S(1)}, f32[1024]{0:T(1024)S(1)}, u32[]{:S(2)}, u32[]{:S(2)}) collective-permute-start(f32[1024]{0:T(1024)S(1)} %add.73), channel_id=1, source_target_pairs={{0,96},{16,112},{32,64},{48,80},{64,32},{80,48},{96,0},{112,16},{1... | collective-permute-start | bytes 12296 | tf_op jit(solution)/shard_map/ppermute | solution.py:41
  54.0 8.9 %collective-permute-start.7 = (f32[1024]{0:T(1024)S(1)}, f32[1024]{0:T(1024)S(1)}, u32[]{:S(2)}, u32[]{:S(2)}) collective-permute-start(f32[1024]{0:T(1024)S(1)} %add.74), channel_id=1, source_target_pairs={{0,16},{16,0},{32,48},{48,32},{64,80},{80,64},{96,112},{112,96},{1... | collective-permute-start | bytes 12296 | tf_op jit(solution)/shard_map/ppermute | solution.py:41

commit v13 on v10

--- a/solution.py
+++ b/solution.py
@@ -78,13 +78,9 @@
     rows = lax.broadcasted_iota(jnp.int32, m.shape, 0)
     for k in range(n):
         row = m[k : k + 1, :]
-        inv_root = 1.0 / jnp.sqrt(row[:, k : k + 1])
-        scaled = row * inv_root
-        column = m[:, k : k + 1] * inv_root
-        m = jnp.where(rows == k, scaled, m - column * scaled)
-    lanes = lax.broadcasted_iota(jnp.int32, (n, n), 1)
-    diag = jnp.sum(jnp.where(lanes == rows[:, :n], m[:, :n], 0.0), axis=1, keepdims=True)
-    coef_ref[...] = m[:, n:] / diag
+        scaled = row * (1.0 / row[:, k : k + 1])
+        m = jnp.where(rows == k, scaled, m - m[:, k : k + 1] * scaled)
+    coef_ref[...] = m[:, n:]
 
 
 def solve_fit(own, received):
@@ -129,10 +125,10 @@
         precision=HIGHEST, preferred_element_type=jnp.float32,
     )
     def weight_map():
-        return bin_tiles(sample_weight, upper_hot, lower_hot, owners, 2)
+        return bin_tiles(sample_weight, upper_hot, lower_hot, owners, 3)
 
     own, received, wgt_part = all_sum_split(
-        jnp.concatenate([gram_sum, projection], axis=1), ("section", "sub"), cover=weight_map
+        jnp.concatenate([gram_sum, projection], axis=1), ("sub", "section"), cover=weight_map
     )
     coef_fit = solve_fit(own, received)
     removed = lax.dot_general(

time: 62.9 us -> 59.6 us (0.948)
  starting transfers between devices: 13.9 us -> 12.1 us
  Pallas kernels: 7.83 us -> 6.86 us
  blocking collectives: 14.7 us -> 14 us
    ppermute x1, starting transfers between devices: 4.22 us -> 2.84 us  [all_sum_split(): received = lax.ppermute(x, axis, pairs)]
    pallas_call x1, Pallas kernels: 7.83 us -> 6.86 us  [solve_fit(): pl.pallas_call(solve_kernel, out_shape=jax.ShapeDtypeStruct((n, own.shape...]
    ppermute x4, waiting for transfers between devices: 4.1 us -> 3.15 us  [all_sum_split(): x = x + lax.ppermute(x, axis, pairs)]
    all_to_all x1, blocking collectives: 14.7 us -> 14 us  [filter_and_bin(): lax.all_to_all(partial, ('wafer', 'sub'), split_axis=0, concat_axis=0, ti...]
  transfers between devices with their start and end apart: 8 -> 8, of which waited for: 7 -> 7; matrix products, arithmetic and copies ran while one was open for 10% -> 12% of each run, Pallas kernels for 0% -> 0%
where the time goes in v13:
time: 59.6 us; the launch traced here: 59.2 us
  blocking collectives  14 us (23%)
  starting transfers between devices  12.1 us (20%)
  waiting for transfers between devices  12 us (20%)
  Pallas kernels  6.86 us (12%)
  matrix products  5.84 us (10%)
  other arithmetic  4.33 us (7%)
  local copies, waits for them, and re-layouts  3.78 us (6%)
    all_to_all x1, blocking collectives, filter_and_bin(): lax.all_to_all(partial, ('wafer', 'sub'), split_axis=0, concat_axis=0, ti...  14 us
    pallas_call x1, Pallas kernels, solve_fit(): pl.pallas_call(solve_kernel, out_shape=jax.ShapeDtypeStruct((n, own.shape...  6.86 us
    ppermute x3, waiting for transfers between devices, all_sum(): x = x + lax.ppermute(x, axis, pairs)  6.54 us
    ppermute x4, starting transfers between devices, all_sum_split(): x = x + lax.ppermute(x, axis, pairs)  6.12 us
    dot_general x2, matrix products, bin_tiles(): lax.dot_general(stacked, lower_hot, (((1,), (1,)), ((), ())), preferred_e...  3.59 us
    ppermute x4, waiting for transfers between devices, all_sum_split(): x = x + lax.ppermute(x, axis, pairs)  3.15 us
    unnamed x14, local copies, waits for them, and re-layouts  3.13 us
    ppermute x3, starting transfers between devices, all_sum(): x = x + lax.ppermute(x, axis, pairs)  3.12 us
  transfers between devices with their start and end apart: 8, of which 7 were waited for; matrix products, arithmetic and copies ran while one was open for 12% of the time, Pallas kernels for 0%

profile of v13, /device:TPU:0, one launch (start us, length us, event | category | flops | bytes accessed | tf_op | source)
XLA Modules:
  0.0 59.2 jit_solution(9995253371081598543)
XLA Ops:
  0.0 0.8 %copy-done = f32[1,64,256]{2,1,0:T(8,128)S(1)} copy-done((f32[1,64,256]{2,1,0:T(8,128)S(1)}, f32[1,64,256]{2,1,0:T(8,128)}, u32[]{:S(2)}) %copy-start) | copy-done | bytes 65560
  0.8 0.2 fusion.31
  1.0 1.0 %fusion.29 = f32[64,64]{1,0:T(8,128)S(1)} fusion(f32[1,64,256]{2,1,0:T(8,128)S(1)} %copy-done, f32[1,64,256]{2,1,0:T(8,128)} %param.6), kind=kOutput, calls=%fused_computation.45 | convolution fusion | flops 12582912 | bytes 147456 | tf_op jit(solution)/shard_map/dot_general | solution.py:123
  2.2 2.1 %collective-permute-start = (f32[64,128]{1,0:T(8,128)S(1)}, f32[64,128]{1,0:T(8,128)S(1)}, u32[]{:S(2)}, u32[]{:S(2)}) collective-permute-start(f32[64,128]{1,0:T(8,128)S(1)} %pad_maximum_fusion.1), channel_id=1, source_target_pairs={{0,1},{1,0},{2,3},{3,2},{4,5},{5,4},{6,7},{7,6},{8,9},{9,8},{10,11... | collective-permute-start | bytes 98312 | tf_op jit(solution)/shard_map/ppermute | solution.py:48
  4.2 0.7 %iota_compare_fusion.5 = pred[16,16]{1,0:T(8,128)(4,1)S(1)} fusion(s32[16]{0:T(128)} %bitcast.29), kind=kLoop, calls=%fused_computation.59 | loop fusion | flops 256 | bytes 320 | tf_op jit(solution)/shard_map/lt | solution.py:104
  5.0 0.8 %fusion.20 = (pred[16,128]{1,0:T(8,128)(4,1)S(1)}, pred[128]{0:T(512)(128)(4,1)S(1)}) fusion(s32[16,16]{1,0:T(8,128)} %bitcast.28, pred[16,16]{1,0:T(8,128)(4,1)S(1)} %iota_compare_fusion.5), kind=kLoop, calls=%fused_computation.24 | loop fusion | flops 128896 | bytes 3456 | tf_op jit(solution)/shard_map/reduce_or | solution.py:106
  5.9 0.1 mul.25
  6.0 0.2 ge.21
  6.1 0.1 broadcast_in_dim.61
  6.3 0.9 %copy.7 = s32[8,2,8,128]{3,1,2,0:T(2,128)S(1)} copy(s32[8,2,8,128]{3,2,1,0:T(8,128)} %bitcast.27) | data formatting | bytes 131072
  7.2 0.1 broadcast_in_dim.62
  7.4 0.7 %broadcast_bitcast_fusion = f32[8,2,8,128]{3,2,1,0:T(8,128)S(1)} fusion(f32[64]{0:T(128)} %param.8), kind=kLoop, calls=%fused_computation.57 | loop fusion | bytes 65792
  8.3 2.5 %collective-permute-start.1 = (f32[64,128]{1,0:T(8,128)S(1)}, f32[64,128]{1,0:T(8,128)S(1)}, u32[]{:S(2)}, u32[]{:S(2)}) collective-permute-start(f32[64,128]{1,0:T(8,128)S(1)} %fusion.40), channel_id=1, source_target_pairs={{0,3},{1,2},{2,1},{3,0},{4,7},{5,6},{6,5},{7,4},{8,11},{9,10},{10,... | collective-permute-start | bytes 98312 | tf_op jit(solution)/shard_map/ppermute | solution.py:48
  10.9 2.6 %collective-permute-done.1 = f32[64,128]{1,0:T(8,128)S(1)} collective-permute-done((f32[64,128]{1,0:T(8,128)S(1)}, f32[64,128]{1,0:T(8,128)S(1)}, u32[]{:S(2)}, u32[]{:S(2)}) %collective-permute-start.1) | collective-permute-done | bytes 32800 | tf_op jit(solution)/shard_map/ppermute | solution.py:48
  13.5 1.1 %fusion.16 = (bf16[64,16384]{1,0:T(8,128)(2,1)S(1)}, bf16[64,16384]{1,0:T(8,128)(2,1)S(1)}, bf16[64,16384]{1,0:T(8,128)(2,1)S(1)}) fusion(s32[16384]{0:T(1024)S(1)} %get-tuple-element.18, bf16[16384]{0:T(1024)(128)(2,1)S(1)} %get-tuple-element.22, bf16[16384]{0:T(1024)(128)(2,1)S(1)} %get-tuple-element.23, bf16[16384]{0:T(1024)(128)(2,1)S(1)} %get-tuple-element.24), kind=kLoop, calls=%fused_computation.18 | loop fusion | flops 4194304 | bytes 6455296 | tf_op jit(solution)/shard_map/jit(_where)/select_n | solution.py:65
  14.7 1.5 %collective-permute-start.3 = (f32[64,128]{1,0:T(8,128)S(1)}, f32[64,128]{1,0:T(8,128)S(1)}, u32[]{:S(2)}, u32[]{:S(2)}) collective-permute-start(f32[64,128]{1,0:T(8,128)S(1)} %add.65), channel_id=1, source_target_pairs={{0,32},{16,48},{32,0},{48,16},{64,96},{80,112},{96,64},{112,80},{1... | collective-permute-start | bytes 98312 | tf_op jit(solution)/shard_map/ppermute | solution.py:48
  16.2 1.9 %fusion.1 = f32[192,128]{1,0:T(8,128)S(1)} fusion(bf16[64,16384]{1,0:T(8,128)(2,1)S(1)} %get-tuple-element.20, bf16[64,16384]{1,0:T(8,128)(2,1)S(1)} %get-tuple-element.21, bf16[64,16384]{1,0:T(8,128)(2,1)S(1)} %get-tuple-element.19, s32[16384]{0:T(1024)S(1)} %get-tuple-element.17), kind=kOutput, calls=%fused_computation.2 | convolution fusion | flops 826277888 | bytes 6455296 | tf_op jit(solution)/shard_map/dot_general | solution.py:66
  18.1 0.5 collective-permute-done.3
  18.6 2.8 %collective-permute-start.4 = (f32[64,128]{1,0:T(8,128)S(1)}, f32[64,128]{1,0:T(8,128)S(1)}, u32[]{:S(2)}, u32[]{:S(2)}) collective-permute-start(f32[64,128]{1,0:T(8,128)S(1)} %add.66.own_ref), channel_id=1, source_target_pairs={{0,96},{16,112},{32,64},{48,80},{64,32},{80,48},{96,0},{112,16},{1... | collective-permute-start | bytes 98312 | tf_op jit(solution)/shard_map/ppermute | solution.py:50
  21.5 2.3 %collective-permute-done.4.received_ref = f32[64,128]{1,0:T(8,128)S(1)} collective-permute-done((f32[64,128]{1,0:T(8,128)S(1)}, f32[64,128]{1,0:T(8,128)S(1)}, u32[]{:S(2)}, u32[]{:S(2)}) %collective-permute-start.4) | collective-permute-done | bytes 32800 | tf_op jit(solution)/shard_map/ppermute | solution.py:50
  23.8 0.6 %copy-done.3 = f32[64,128]{1,0:T(8,128)} copy-done((f32[64,128]{1,0:T(8,128)}, f32[64,128]{1,0:T(8,128)S(1)}, u32[]{:S(2)}) %copy-start.3) | copy-done | bytes 32792
  24.4 6.9 %shard_map.64 = f32[64,64]{1,0:T(8,128)} custom-call(f32[64,128]{1,0:T(8,128)} %copy-done.2, f32[64,128]{1,0:T(8,128)} %copy-done.3), custom_call_target="tpu_custom_call" | custom-call | tf_op jit(solution)/shard_map/pallas_call | solution.py:88
  31.3 1.0 %fusion.18 = f32[8,2,8,128]{3,2,1,0:T(8,128)S(1)} fusion(f32[64,64]{1,0:T(8,128)} %shard_map.64, f32[1,64,256]{2,1,0:T(8,128)S(1)} %copy-done, f32[1,64,256]{2,1,0:T(8,128)S(1)} %copy-done.1, f32[64]{0:T(128)S(1)} %copy-done.4), kind=kOutput, calls=%fused_computation.21 | convolution fusion | flops 12615680 | bytes 213248 | tf_op jit(solution)/shard_map/dot_general | solution.py:134
  32.4 0.7 %fusion.13 = (bf16[64,16384]{1,0:T(8,128)(2,1)S(1)}, bf16[64,16384]{1,0:T(8,128)(2,1)S(1)}) fusion(s32[16384]{0:T(1024)S(1)} %get-tuple-element.18, bf16[16384]{0:T(1024)(128)(2,1)S(1)} %get-tuple-element.15, bf16[16384]{0:T(1024)(128)(2,1)S(1)} %get-tuple-element.16), kind=kLoop, calls=%fused_computation.15 | loop fusion | flops 3145728 | bytes 4325376 | tf_op jit(solution)/shard_map/jit(_where)/select_n | solution.py:65
  33.1 1.6 %fusion = f32[128,128]{1,0:T(8,128)S(1)} fusion(bf16[64,16384]{1,0:T(8,128)(2,1)S(1)} %get-tuple-element.14, bf16[64,16384]{1,0:T(8,128)(2,1)S(1)} %get-tuple-element.13, s32[16384]{0:T(1024)S(1)} %get-tuple-element.17), kind=kOutput, calls=%fused_computation.1 | convolution fusion | flops 547356672 | bytes 4325376 | tf_op jit(solution)/shard_map/dot_general | solution.py:66
  34.8 14.0 %all_to_all.9 = f32[16,1,1024]{2,1,0:T(1,128)S(1)} all-to-all(f32[16,1,1024]{2,1,0:T(1,128)S(1)} %all_to_all.6), channel_id=1, replica_groups=mesh['section'=8,'wafer'=4,'sub'=4] {'wafer','sub'}, dimensions={0} | all-to-all | bytes 131072 | tf_op jit(solution)/shard_map/all_to_all | solution.py:143
  49.0 1.2 %collective-permute-done.5 = f32[1024]{0:T(1024)S(1)} collective-permute-done((f32[1024]{0:T(1024)S(1)}, f32[1024]{0:T(1024)S(1)}, u32[]{:S(2)}, u32[]{:S(2)}) %collective-permute-start.5) | collective-permute-done | bytes 4128 | tf_op jit(solution)/shard_map/ppermute | solution.py:39
  50.1 0.3 collective-permute-start.6
  50.4 3.3 %collective-permute-done.6 = f32[1024]{0:T(1024)S(1)} collective-permute-done((f32[1024]{0:T(1024)S(1)}, f32[1024]{0:T(1024)S(1)}, u32[]{:S(2)}, u32[]{:S(2)}) %collective-permute-start.6) | collective-permute-done | bytes 4128 | tf_op jit(solution)/shard_map/ppermute | solution.py:39
  53.7 2.8 %collective-permute-start.7 = (f32[1024]{0:T(1024)S(1)}, f32[1024]{0:T(1024)S(1)}, u32[]{:S(2)}, u32[]{:S(2)}) collective-permute-start(f32[1024]{0:T(1024)S(1)} %add.74), channel_id=1, source_target_pairs={{0,96},{16,112},{32,64},{48,80},{64,32},{80,48},{96,0},{112,16},{1... | collective-permute-start | bytes 12296 | tf_op jit(solution)/shard_map/ppermute | solution.py:39
  56.5 2.1 %collective-permute-done.7 = f32[1024]{0:T(1024)S(1)} collective-permute-done((f32[1024]{0:T(1024)S(1)}, f32[1024]{0:T(1024)S(1)}, u32[]{:S(2)}, u32[]{:S(2)}) %collective-permute-start.7) | collective-permute-done | bytes 4128 | tf_op jit(solution)/shard_map/ppermute | solution.py:39
  58.6 0.6 %maximum_divide_fusion = f32[512]{0:T(512)} fusion(f32[1024]{0:T(1024)S(1)} %add.75), kind=kLoop, calls=%fused_computation.60 | loop fusion | flops 1024 | bytes 6144 | tf_op jit(solution)/shard_map/div | solution.py:146
  (36 shorter events, 0.8 us)
Async XLA Ops:
  0.0 0.8 %copy-start = (f32[1,64,256]{2,1,0:T(8,128)S(1)}, f32[1,64,256]{2,1,0:T(8,128)}, u32[]{:S(2)}) copy-start(f32[1,64,256]{2,1,0:T(8,128)} %param.7) | copy-start | bytes 196612
  2.2 6.0 %collective-permute-start = (f32[64,128]{1,0:T(8,128)S(1)}, f32[64,128]{1,0:T(8,128)S(1)}, u32[]{:S(2)}, u32[]{:S(2)}) collective-permute-start(f32[64,128]{1,0:T(8,128)S(1)} %pad_maximum_fusion.1), channel_id=1, source_target_pairs={{0,1},{1,0},{2,3},{3,2},{4,5},{5,4},{6,7},{7,6},{8,9},{9,8},{10,11... | collective-permute-start | bytes 98312 | tf_op jit(solution)/shard_map/ppermute | solution.py:48
  8.3 5.2 %collective-permute-start.1 = (f32[64,128]{1,0:T(8,128)S(1)}, f32[64,128]{1,0:T(8,128)S(1)}, u32[]{:S(2)}, u32[]{:S(2)}) collective-permute-start(f32[64,128]{1,0:T(8,128)S(1)} %fusion.40), channel_id=1, source_target_pairs={{0,3},{1,2},{2,1},{3,0},{4,7},{5,6},{6,5},{7,4},{8,11},{9,10},{10,... | collective-permute-start | bytes 98312 | tf_op jit(solution)/shard_map/ppermute | solution.py:48
  13.4 1.2 %collective-permute-start.2 = (f32[64,128]{1,0:T(8,128)S(1)}, f32[64,128]{1,0:T(8,128)S(1)}, u32[]{:S(2)}, u32[]{:S(2)}) collective-permute-start(f32[64,128]{1,0:T(8,128)S(1)} %add.64), channel_id=1, source_target_pairs={{0,16},{16,0},{32,48},{48,32},{64,80},{80,64},{96,112},{112,96},{1... | collective-permute-start | bytes 98312 | tf_op jit(solution)/shard_map/ppermute | solution.py:48
  14.7 3.9 %collective-permute-start.3 = (f32[64,128]{1,0:T(8,128)S(1)}, f32[64,128]{1,0:T(8,128)S(1)}, u32[]{:S(2)}, u32[]{:S(2)}) collective-permute-start(f32[64,128]{1,0:T(8,128)S(1)} %add.65), channel_id=1, source_target_pairs={{0,32},{16,48},{32,0},{48,16},{64,96},{80,112},{96,64},{112,80},{1... | collective-permute-start | bytes 98312 | tf_op jit(solution)/shard_map/ppermute | solution.py:48
  16.2 15.1 %copy-start.1 = (f32[1,64,256]{2,1,0:T(8,128)S(1)}, f32[1,64,256]{2,1,0:T(8,128)}, u32[]{:S(2)}) copy-start(f32[1,64,256]{2,1,0:T(8,128)} %param.6) | copy-start | bytes 196612
  16.2 15.1 %copy-start.4 = (f32[64]{0:T(128)S(1)}, f32[64]{0:T(128)}, u32[]{:S(2)}) copy-start(f32[64]{0:T(128)} %param.8) | copy-start | bytes 772
  18.6 5.2 %copy-start.2 = (f32[64,128]{1,0:T(8,128)}, f32[64,128]{1,0:T(8,128)S(1)}, u32[]{:S(2)}) copy-start(f32[64,128]{1,0:T(8,128)S(1)} %add.66.own_ref) | copy-start | bytes 98308
  18.6 5.2 %collective-permute-start.4 = (f32[64,128]{1,0:T(8,128)S(1)}, f32[64,128]{1,0:T(8,128)S(1)}, u32[]{:S(2)}, u32[]{:S(2)}) collective-permute-start(f32[64,128]{1,0:T(8,128)S(1)} %add.66.own_ref), channel_id=1, source_target_pairs={{0,96},{16,112},{32,64},{48,80},{64,32},{80,48},{96,0},{112,16},{1... | collective-permute-start | bytes 98312 | tf_op jit(solution)/shard_map/ppermute | solution.py:50
  23.8 0.6 %copy-start.3 = (f32[64,128]{1,0:T(8,128)}, f32[64,128]{1,0:T(8,128)S(1)}, u32[]{:S(2)}) copy-start(f32[64,128]{1,0:T(8,128)S(1)} %collective-permute-done.4.received_ref) | copy-start | bytes 98308
  48.9 1.2 %collective-permute-start.5 = (f32[1024]{0:T(1024)S(1)}, f32[1024]{0:T(1024)S(1)}, u32[]{:S(2)}, u32[]{:S(2)}) collective-permute-start(f32[1024]{0:T(1024)S(1)} %reduce_sum.19), channel_id=1, source_target_pairs={{0,16},{16,0},{32,48},{48,32},{64,80},{80,64},{96,112},{112,96},{1... | collective-permute-start | bytes 12296 | tf_op jit(solution)/shard_map/ppermute | solution.py:39
  50.1 3.6 %collective-permute-start.6 = (f32[1024]{0:T(1024)S(1)}, f32[1024]{0:T(1024)S(1)}, u32[]{:S(2)}, u32[]{:S(2)}) collective-permute-start(f32[1024]{0:T(1024)S(1)} %add.73), channel_id=1, source_target_pairs={{0,32},{16,48},{32,0},{48,16},{64,96},{80,112},{96,64},{112,80},{1... | collective-permute-start | bytes 12296 | tf_op jit(solution)/shard_map/ppermute | solution.py:39
  53.7 4.8 %collective-permute-start.7 = (f32[1024]{0:T(1024)S(1)}, f32[1024]{0:T(1024)S(1)}, u32[]{:S(2)}, u32[]{:S(2)}) collective-permute-start(f32[1024]{0:T(1024)S(1)} %add.74), channel_id=1, source_target_pairs={{0,96},{16,112},{32,64},{48,80},{64,32},{80,48},{96,0},{112,16},{1... | collective-permute-start | bytes 12296 | tf_op jit(solution)/shard_map/ppermute | solution.py:39

commit v14 on v13

--- a/solution.py
+++ b/solution.py
@@ -72,9 +72,9 @@
     return total.reshape(owners, TILE)
 
 
-def solve_kernel(own_ref, received_ref, coef_ref):
-    n = own_ref.shape[0]
-    m = own_ref[...] + received_ref[...]
+def solve_kernel(joined_ref, coef_ref):
+    n = joined_ref.shape[0]
+    m = joined_ref[...]
     rows = lax.broadcasted_iota(jnp.int32, m.shape, 0)
     for k in range(n):
         row = m[k : k + 1, :]
@@ -88,9 +88,10 @@
     return pl.pallas_call(
         solve_kernel,
         out_shape=jax.ShapeDtypeStruct((n, own.shape[1] - n), jnp.float32),
-        in_specs=[pl.BlockSpec(memory_space=pltpu.VMEM)] * 2,
+        in_specs=[pl.BlockSpec(memory_space=pltpu.VMEM)],
         out_specs=pl.BlockSpec(memory_space=pltpu.VMEM),
-    )(own, received)
+        compiler_params=pltpu.CompilerParams(allow_input_fusion=[True]),
+    )(own + received)
 
 
 def filter_and_bin(tod, templates, det_weight, pixel, hitlist, counts):
@@ -125,10 +126,10 @@
         precision=HIGHEST, preferred_element_type=jnp.float32,
     )
     def weight_map():
-        return bin_tiles(sample_weight, upper_hot, lower_hot, owners, 3)
+        return bin_tiles(sample_weight, upper_hot, lower_hot, owners, 2)
 
     own, received, wgt_part = all_sum_split(
-        jnp.concatenate([gram_sum, projection], axis=1), ("sub", "section"), cover=weight_map
+        jnp.concatenate([gram_sum, projection], axis=1), ("section", "sub"), cover=weight_map
     )
     coef_fit = solve_fit(own, received)
     removed = lax.dot_general(

time: 59.6 us -> 61.8 us (1.037)
  starting transfers between devices: 12.1 us -> 13.8 us
  blocking collectives: 14 us -> 14.7 us
    ppermute x1, starting transfers between devices: 2.84 us -> 4.14 us  [all_sum_split(): received = lax.ppermute(x, axis, pairs)]
    ppermute x4, waiting for transfers between devices: 3.15 us -> 4.1 us  [all_sum_split(): x = x + lax.ppermute(x, axis, pairs)]
    all_to_all x1, blocking collectives: 14 us -> 14.7 us  [filter_and_bin(): lax.all_to_all(partial, ('wafer', 'sub'), split_axis=0, concat_axis=0, ti...]
    unnamed x14 -> x10, local copies, waits for them, and re-layouts: 3.13 us -> 2.53 us
  transfers between devices with their start and end apart: 8 -> 8, of which waited for: 7 -> 7; matrix products, arithmetic and copies ran while one was open for 12% -> 10% of each run, Pallas kernels for 0% -> 0%
where the time goes in v14:
time: 61.8 us; the launch traced here: 61.3 us
  blocking collectives  14.7 us (24%)
  starting transfers between devices  13.8 us (22%)
  waiting for transfers between devices  12.5 us (20%)
  Pallas kernels  6.84 us (11%)
  matrix products  5.56 us (9%)
  other arithmetic  4.52 us (7%)
  local copies, waits for them, and re-layouts  3.17 us (5%)
    all_to_all x1, blocking collectives, filter_and_bin(): lax.all_to_all(partial, ('wafer', 'sub'), split_axis=0, concat_axis=0, ti...  14.7 us
    pallas_call x1, Pallas kernels, solve_fit(): pl.pallas_call(solve_kernel, out_shape=jax.ShapeDtypeStruct((n, own.shape...  6.84 us
    ppermute x4, starting transfers between devices, all_sum_split(): x = x + lax.ppermute(x, axis, pairs)  6.56 us
    ppermute x3, waiting for transfers between devices, all_sum(): x = x + lax.ppermute(x, axis, pairs)  6.53 us
    ppermute x1, starting transfers between devices, all_sum_split(): received = lax.ppermute(x, axis, pairs)  4.14 us
    ppermute x4, waiting for transfers between devices, all_sum_split(): x = x + lax.ppermute(x, axis, pairs)  4.1 us
    dot_general x2, matrix products, bin_tiles(): lax.dot_general(stacked, lower_hot, (((1,), (1,)), ((), ())), preferred_e...  3.3 us
    ppermute x3, starting transfers between devices, all_sum(): x = x + lax.ppermute(x, axis, pairs)  3.13 us
  transfers between devices with their start and end apart: 8, of which 7 were waited for; matrix products, arithmetic and copies ran while one was open for 10% of the time, Pallas kernels for 0%

profile of v14, /device:TPU:0, one launch (start us, length us, event | category | flops | bytes accessed | tf_op | source)
XLA Modules:
  0.0 61.3 jit_solution(16570828604159455902)
XLA Ops:
  0.0 0.8 %copy-done = f32[1,64,256]{2,1,0:T(8,128)S(1)} copy-done((f32[1,64,256]{2,1,0:T(8,128)S(1)}, f32[1,64,256]{2,1,0:T(8,128)}, u32[]{:S(2)}) %copy-start) | copy-done | bytes 65560
  0.8 0.2 fusion.28
  1.0 1.0 %fusion.26 = f32[64,64]{1,0:T(8,128)S(1)} fusion(f32[1,64,256]{2,1,0:T(8,128)S(1)} %copy-done, f32[1,64,256]{2,1,0:T(8,128)} %param.6), kind=kOutput, calls=%fused_computation.40 | convolution fusion | flops 12582912 | bytes 147456 | tf_op jit(solution)/shard_map/dot_general | solution.py:124
  2.2 0.7 %iota_compare_fusion.5 = pred[16,16]{1,0:T(8,128)(4,1)S(1)} fusion(s32[16]{0:T(128)} %bitcast.29), kind=kLoop, calls=%fused_computation.53 | loop fusion | flops 256 | bytes 320 | tf_op jit(solution)/shard_map/lt | solution.py:105
  2.9 0.8 %fusion.17 = (pred[16,128]{1,0:T(8,128)(4,1)S(1)}, pred[128]{0:T(512)(128)(4,1)S(1)}) fusion(s32[16,16]{1,0:T(8,128)} %bitcast.28, pred[16,16]{1,0:T(8,128)(4,1)S(1)} %iota_compare_fusion.5), kind=kLoop, calls=%fused_computation.21 | loop fusion | flops 128896 | bytes 3456 | tf_op jit(solution)/shard_map/reduce_or | solution.py:107
  3.8 0.1 ge.21
  4.0 0.1 broadcast_in_dim.55
  4.2 0.1 mul.25
  4.3 0.9 %copy.7 = s32[8,2,8,128]{3,1,2,0:T(2,128)S(1)} copy(s32[8,2,8,128]{3,2,1,0:T(8,128)} %bitcast.27) | data formatting | bytes 131072
  5.4 0.7 %broadcast_bitcast_fusion = f32[8,2,8,128]{3,2,1,0:T(8,128)S(1)} fusion(f32[64]{0:T(128)} %param.8), kind=kLoop, calls=%fused_computation.51 | loop fusion | bytes 65792
  6.3 1.6 %collective-permute-start.1 = (f32[64,128]{1,0:T(8,128)S(1)}, f32[64,128]{1,0:T(8,128)S(1)}, u32[]{:S(2)}, u32[]{:S(2)}) collective-permute-start(f32[64,128]{1,0:T(8,128)S(1)} %fusion.36), channel_id=1, source_target_pairs={{0,32},{16,48},{32,0},{48,16},{64,96},{80,112},{96,64},{112,80},{1... | collective-permute-start | bytes 98312 | tf_op jit(solution)/shard_map/ppermute | solution.py:48
  7.9 2.3 %collective-permute-done.1 = f32[64,128]{1,0:T(8,128)S(1)} collective-permute-done((f32[64,128]{1,0:T(8,128)S(1)}, f32[64,128]{1,0:T(8,128)S(1)}, u32[]{:S(2)}, u32[]{:S(2)}) %collective-permute-start.1) | collective-permute-done | bytes 32800 | tf_op jit(solution)/shard_map/ppermute | solution.py:48
  10.2 2.9 %collective-permute-start.2 = (f32[64,128]{1,0:T(8,128)S(1)}, f32[64,128]{1,0:T(8,128)S(1)}, u32[]{:S(2)}, u32[]{:S(2)}) collective-permute-start(f32[64,128]{1,0:T(8,128)S(1)} %add.62), channel_id=1, source_target_pairs={{0,96},{16,112},{32,64},{48,80},{64,32},{80,48},{96,0},{112,16},{1... | collective-permute-start | bytes 98312 | tf_op jit(solution)/shard_map/ppermute | solution.py:48
  13.1 0.7 %fusion.13 = (bf16[64,16384]{1,0:T(8,128)(2,1)S(1)}, bf16[64,16384]{1,0:T(8,128)(2,1)S(1)}) fusion(s32[16384]{0:T(1024)S(1)} %get-tuple-element.18, bf16[16384]{0:T(1024)(128)(2,1)S(1)} %get-tuple-element.21, bf16[16384]{0:T(1024)(128)(2,1)S(1)} %get-tuple-element.22), kind=kLoop, calls=%fused_computation.15 | loop fusion | flops 3145728 | bytes 4325376 | tf_op jit(solution)/shard_map/jit(_where)/select_n | solution.py:65
  13.8 1.6 %collective-permute-done.2 = f32[64,128]{1,0:T(8,128)S(1)} collective-permute-done((f32[64,128]{1,0:T(8,128)S(1)}, f32[64,128]{1,0:T(8,128)S(1)}, u32[]{:S(2)}, u32[]{:S(2)}) %collective-permute-start.2) | collective-permute-done | bytes 32800 | tf_op jit(solution)/shard_map/ppermute | solution.py:48
  15.4 2.0 %collective-permute-start.3 = (f32[64,128]{1,0:T(8,128)S(1)}, f32[64,128]{1,0:T(8,128)S(1)}, u32[]{:S(2)}, u32[]{:S(2)}) collective-permute-start(f32[64,128]{1,0:T(8,128)S(1)} %add.63), channel_id=1, source_target_pairs={{0,1},{1,0},{2,3},{3,2},{4,5},{5,4},{6,7},{7,6},{8,9},{9,8},{10,11... | collective-permute-start | bytes 98312 | tf_op jit(solution)/shard_map/ppermute | solution.py:48
  17.4 1.6 %fusion.1 = f32[128,128]{1,0:T(8,128)S(1)} fusion(bf16[64,16384]{1,0:T(8,128)(2,1)S(1)} %get-tuple-element.20, bf16[64,16384]{1,0:T(8,128)(2,1)S(1)} %get-tuple-element.19, s32[16384]{0:T(1024)S(1)} %get-tuple-element.17), kind=kOutput, calls=%fused_computation.2 | convolution fusion | flops 547356672 | bytes 4325376 | tf_op jit(solution)/shard_map/dot_general | solution.py:66
  19.0 0.2 collective-permute-done.3
  19.3 4.1 %collective-permute-start.4 = (f32[64,128]{1,0:T(8,128)S(1)}, f32[64,128]{1,0:T(8,128)S(1)}, u32[]{:S(2)}, u32[]{:S(2)}) collective-permute-start(f32[64,128]{1,0:T(8,128)S(1)} %add.64), channel_id=1, source_target_pairs={{0,3},{1,2},{2,1},{3,0},{4,7},{5,6},{6,5},{7,4},{8,11},{9,10},{10,... | collective-permute-start | bytes 98312 | tf_op jit(solution)/shard_map/ppermute | solution.py:50
  23.4 1.9 %collective-permute-done.4 = f32[64,128]{1,0:T(8,128)S(1)} collective-permute-done((f32[64,128]{1,0:T(8,128)S(1)}, f32[64,128]{1,0:T(8,128)S(1)}, u32[]{:S(2)}, u32[]{:S(2)}) %collective-permute-start.4) | collective-permute-done | bytes 32800 | tf_op jit(solution)/shard_map/ppermute | solution.py:50
  25.3 0.6 add.68.joined_ref
  25.9 6.8 %shard_map.64 = f32[64,64]{1,0:T(8,128)} custom-call(f32[64,128]{1,0:T(8,128)} %add.68.joined_ref), custom_call_target="tpu_custom_call" | custom-call | tf_op jit(solution)/shard_map/pallas_call | solution.py:88
  32.8 1.0 %fusion.15 = f32[8,2,8,128]{3,2,1,0:T(8,128)S(1)} fusion(f32[64,64]{1,0:T(8,128)} %shard_map.64, f32[1,64,256]{2,1,0:T(8,128)S(1)} %copy-done, f32[1,64,256]{2,1,0:T(8,128)S(1)} %copy-done.1, f32[64]{0:T(128)S(1)} %copy-done.2), kind=kOutput, calls=%fused_computation.18 | convolution fusion | flops 12615680 | bytes 213248 | tf_op jit(solution)/shard_map/dot_general | solution.py:135
  33.9 0.7 %fusion.11 = (bf16[64,16384]{1,0:T(8,128)(2,1)S(1)}, bf16[64,16384]{1,0:T(8,128)(2,1)S(1)}) fusion(s32[16384]{0:T(1024)S(1)} %get-tuple-element.18, bf16[16384]{0:T(1024)(128)(2,1)S(1)} %get-tuple-element.15, bf16[16384]{0:T(1024)(128)(2,1)S(1)} %get-tuple-element.16), kind=kLoop, calls=%fused_computation.13 | loop fusion | flops 3145728 | bytes 4325376 | tf_op jit(solution)/shard_map/jit(_where)/select_n | solution.py:65
  34.5 1.7 %fusion = f32[128,128]{1,0:T(8,128)S(1)} fusion(bf16[64,16384]{1,0:T(8,128)(2,1)S(1)} %get-tuple-element.14, bf16[64,16384]{1,0:T(8,128)(2,1)S(1)} %get-tuple-element.13, s32[16384]{0:T(1024)S(1)} %get-tuple-element.17), kind=kOutput, calls=%fused_computation.1 | convolution fusion | flops 547356672 | bytes 4325376 | tf_op jit(solution)/shard_map/dot_general | solution.py:66
  36.3 14.7 %all_to_all.9 = f32[16,1,1024]{2,1,0:T(1,128)S(1)} all-to-all(f32[16,1,1024]{2,1,0:T(1,128)S(1)} %all_to_all.6), channel_id=1, replica_groups=mesh['section'=8,'wafer'=4,'sub'=4] {'wafer','sub'}, dimensions={0} | all-to-all | bytes 131072 | tf_op jit(solution)/shard_map/all_to_all | solution.py:144
  51.2 1.2 %collective-permute-done.5 = f32[1024]{0:T(1024)S(1)} collective-permute-done((f32[1024]{0:T(1024)S(1)}, f32[1024]{0:T(1024)S(1)}, u32[]{:S(2)}, u32[]{:S(2)}) %collective-permute-start.5) | collective-permute-done | bytes 4128 | tf_op jit(solution)/shard_map/ppermute | solution.py:39
  52.3 0.3 collective-permute-start.6
  52.6 3.3 %collective-permute-done.6 = f32[1024]{0:T(1024)S(1)} collective-permute-done((f32[1024]{0:T(1024)S(1)}, f32[1024]{0:T(1024)S(1)}, u32[]{:S(2)}, u32[]{:S(2)}) %collective-permute-start.6) | collective-permute-done | bytes 4128 | tf_op jit(solution)/shard_map/ppermute | solution.py:39
  55.9 2.8 %collective-permute-start.7 = (f32[1024]{0:T(1024)S(1)}, f32[1024]{0:T(1024)S(1)}, u32[]{:S(2)}, u32[]{:S(2)}) collective-permute-start(f32[1024]{0:T(1024)S(1)} %add.72), channel_id=1, source_target_pairs={{0,96},{16,112},{32,64},{48,80},{64,32},{80,48},{96,0},{112,16},{1... | collective-permute-start | bytes 12296 | tf_op jit(solution)/shard_map/ppermute | solution.py:39
  58.7 2.1 %collective-permute-done.7 = f32[1024]{0:T(1024)S(1)} collective-permute-done((f32[1024]{0:T(1024)S(1)}, f32[1024]{0:T(1024)S(1)}, u32[]{:S(2)}, u32[]{:S(2)}) %collective-permute-start.7) | collective-permute-done | bytes 4128 | tf_op jit(solution)/shard_map/ppermute | solution.py:39
  60.7 0.6 maximum_divide_fusion
  (33 shorter events, 0.8 us)
Async XLA Ops:
  0.0 0.8 %copy-start = (f32[1,64,256]{2,1,0:T(8,128)S(1)}, f32[1,64,256]{2,1,0:T(8,128)}, u32[]{:S(2)}) copy-start(f32[1,64,256]{2,1,0:T(8,128)} %param.7) | copy-start | bytes 196612
  2.2 4.0 %collective-permute-start = (f32[64,128]{1,0:T(8,128)S(1)}, f32[64,128]{1,0:T(8,128)S(1)}, u32[]{:S(2)}, u32[]{:S(2)}) collective-permute-start(f32[64,128]{1,0:T(8,128)S(1)} %pad_maximum_fusion.1), channel_id=1, source_target_pairs={{0,16},{16,0},{32,48},{48,32},{64,80},{80,64},{96,112},{112,96},{1... | collective-permute-start | bytes 98312 | tf_op jit(solution)/shard_map/ppermute | solution.py:48
  6.3 3.9 %collective-permute-start.1 = (f32[64,128]{1,0:T(8,128)S(1)}, f32[64,128]{1,0:T(8,128)S(1)}, u32[]{:S(2)}, u32[]{:S(2)}) collective-permute-start(f32[64,128]{1,0:T(8,128)S(1)} %fusion.36), channel_id=1, source_target_pairs={{0,32},{16,48},{32,0},{48,16},{64,96},{80,112},{96,64},{112,80},{1... | collective-permute-start | bytes 98312 | tf_op jit(solution)/shard_map/ppermute | solution.py:48
  10.2 5.1 %collective-permute-start.2 = (f32[64,128]{1,0:T(8,128)S(1)}, f32[64,128]{1,0:T(8,128)S(1)}, u32[]{:S(2)}, u32[]{:S(2)}) collective-permute-start(f32[64,128]{1,0:T(8,128)S(1)} %add.62), channel_id=1, source_target_pairs={{0,96},{16,112},{32,64},{48,80},{64,32},{80,48},{96,0},{112,16},{1... | collective-permute-start | bytes 98312 | tf_op jit(solution)/shard_map/ppermute | solution.py:48
  15.4 3.9 %collective-permute-start.3 = (f32[64,128]{1,0:T(8,128)S(1)}, f32[64,128]{1,0:T(8,128)S(1)}, u32[]{:S(2)}, u32[]{:S(2)}) collective-permute-start(f32[64,128]{1,0:T(8,128)S(1)} %add.63), channel_id=1, source_target_pairs={{0,1},{1,0},{2,3},{3,2},{4,5},{5,4},{6,7},{7,6},{8,9},{9,8},{10,11... | collective-permute-start | bytes 98312 | tf_op jit(solution)/shard_map/ppermute | solution.py:48
  17.4 15.4 %copy-start.1 = (f32[1,64,256]{2,1,0:T(8,128)S(1)}, f32[1,64,256]{2,1,0:T(8,128)}, u32[]{:S(2)}) copy-start(f32[1,64,256]{2,1,0:T(8,128)} %param.6) | copy-start | bytes 196612
  17.4 15.4 %copy-start.2 = (f32[64]{0:T(128)S(1)}, f32[64]{0:T(128)}, u32[]{:S(2)}) copy-start(f32[64]{0:T(128)} %param.8) | copy-start | bytes 772
  19.3 6.0 %collective-permute-start.4 = (f32[64,128]{1,0:T(8,128)S(1)}, f32[64,128]{1,0:T(8,128)S(1)}, u32[]{:S(2)}, u32[]{:S(2)}) collective-permute-start(f32[64,128]{1,0:T(8,128)S(1)} %add.64), channel_id=1, source_target_pairs={{0,3},{1,2},{2,1},{3,0},{4,7},{5,6},{6,5},{7,4},{8,11},{9,10},{10,... | collective-permute-start | bytes 98312 | tf_op jit(solution)/shard_map/ppermute | solution.py:50
  51.1 1.2 %collective-permute-start.5 = (f32[1024]{0:T(1024)S(1)}, f32[1024]{0:T(1024)S(1)}, u32[]{:S(2)}, u32[]{:S(2)}) collective-permute-start(f32[1024]{0:T(1024)S(1)} %reduce_sum.19), channel_id=1, source_target_pairs={{0,16},{16,0},{32,48},{48,32},{64,80},{80,64},{96,112},{112,96},{1... | collective-permute-start | bytes 12296 | tf_op jit(solution)/shard_map/ppermute | solution.py:39
  52.3 3.6 %collective-permute-start.6 = (f32[1024]{0:T(1024)S(1)}, f32[1024]{0:T(1024)S(1)}, u32[]{:S(2)}, u32[]{:S(2)}) collective-permute-start(f32[1024]{0:T(1024)S(1)} %add.71), channel_id=1, source_target_pairs={{0,32},{16,48},{32,0},{48,16},{64,96},{80,112},{96,64},{112,80},{1... | collective-permute-start | bytes 12296 | tf_op jit(solution)/shard_map/ppermute | solution.py:39
  55.9 4.8 %collective-permute-start.7 = (f32[1024]{0:T(1024)S(1)}, f32[1024]{0:T(1024)S(1)}, u32[]{:S(2)}, u32[]{:S(2)}) collective-permute-start(f32[1024]{0:T(1024)S(1)} %add.72), channel_id=1, source_target_pairs={{0,96},{16,112},{32,64},{48,80},{64,32},{80,48},{96,0},{112,16},{1... | collective-permute-start | bytes 12296 | tf_op jit(solution)/shard_map/ppermute | solution.py:39
